TPU v7x, 32 devices: a whole 2x2x4 slice. The times are simulated.
32 devices in a mesh: group: 2 (over x), chan: 16 (over z, y, core).
Axes of the slice: x: 2, y: 2, z: 4, core: 2. Of those that a mesh axis runs over, the one named last changes fastest.
Arguments:
- parent_state: float32 [32, 16, 16384], P('group', None, 'chan'), parts along dimension 0, may hold values from -6 to 6
- parent_conv: bfloat16 [32, 3, 16384], P('group', None, 'chan'), parts along dimension 0, may hold values from -6 to 6
- fork_map: int32 [32], P('group'), parts along dimension 0, may hold values from 0 to 15
- judge_lengths: int32 [32], P('group'), parts along dimension 0, may hold values from 1 to 16, 128 in all
- mixer_input: bfloat16 [32, 20, 16384], P('group', None, 'chan'), parts along dimension 0, may hold values from -6 to 6
- gate_input: bfloat16 [32, 20, 16384], P('group', None, 'chan'), parts along dimension 0, may hold values from -6 to 6
- conv_weight: bfloat16 [4, 16384], P(None, 'chan'), may hold values from -3 to 3
- conv_bias: float32 [16384], P('chan'), may hold values from -0.5 to 0.5
- rate_down: bfloat16 [16384, 512], P('chan'), may hold values from -0.046875 to 0.046875
- selection_weight: bfloat16 [16384, 32], P('chan'), may hold values from -0.046875 to 0.046875
- rate_up: bfloat16 [512, 16384], P(None, 'chan'), may hold values from -0.25 to 0.25
- rate_bias: float32 [16384], P('chan'), may hold values from -7 to -2.3
- decay_log: float32 [16, 16384], P(None, 'chan'), may hold values from 0 to 2.77
- skip_gain: float32 [16384], P('chan'), may hold values from 0.5 to 1.5
Outputs:
- mixer_output: bfloat16 [32, 20, 16384], P(('group', 'chan')), parts along dimension 0
- final_state: float32 [32, 16, 16384], P(('group', 'chan')), parts along dimension 0
There are 2 independent parts, one for each index of `group`. A program takes and returns all parts, laid end to end along the dimension named above; an argument that names none is the same for every part. Nothing has to cross between parts.
Inputs may be any that keep to these rules, and one draw needn't show every extreme that they name: `fork_map`: index of the parent node a thought continues. `judge_lengths`: the lengths of one part sum to 128 and the longest is exactly 16.
All inputs are finite; a program needn't handle non-finite values.
Results may differ from a plain program's by a relative error of at most 0.0095.
Values may be sent and summed in bfloat16 or wider, within the bound.
No kernel may reach another device: no remote copies, remote signals or barrier semaphores. Data moves between devices by JAX's collectives and lax.ppermute only.
A program may use at most 128 MiB of HBM per device.

v0:
```python
import jax
import jax.numpy as jnp
from jax import lax
from jax.sharding import PartitionSpec as P

GEN = 4


def convolve(parent_conv, fork_map, mixer_input, conv_weight, conv_bias):
    positions = mixer_input.shape[1]
    start_conv = jnp.take(parent_conv, fork_map, axis=0)
    padded = jnp.concatenate([start_conv, mixer_input], axis=1).astype(jnp.float32)
    tap_weights = conv_weight.astype(jnp.float32)
    summed = conv_bias[None, None, :] + tap_weights[0][None, None, :] * padded[:, 0:positions, :]
    for offset in range(1, conv_weight.shape[0]):
        summed = (
            summed + tap_weights[offset][None, None, :] * padded[:, offset : offset + positions, :]
        )
    return jax.nn.silu(summed).astype(jnp.bfloat16)


def combine(before, after_pair):
    return (before[0] * after_pair[0], after_pair[0] * before[1] + after_pair[1])


def run_scan(
    driven, gate_input, step_rate, selection, live_mask, start_state, decay_log, skip_gain
):
    thought_count, positions, width_all = driven.shape
    state_size = start_state.shape[1]
    block_len = 4
    blocks = positions // block_len
    decay_rate = -jnp.exp(decay_log)

    def split_blocks(values):
        shaped = values.reshape((thought_count, blocks, block_len) + values.shape[2:])
        return jnp.moveaxis(shaped, 0, 2)

    def one_block(carried, pieces):
        drive_rows, gate_rows, rate_rows, select_rows, alive_rows = pieces
        inflow = drive_rows.astype(jnp.float32)
        factor = jnp.exp(rate_rows[:, :, None, :] * decay_rate[None, None, :, :])
        push_term = (rate_rows * inflow)[:, :, None, :] * select_rows[:, :, :state_size, None]
        decay_run, push_run = lax.associative_scan(combine, (factor, push_term), axis=0)
        states_all = decay_run * carried[None] + push_run
        readout = jnp.sum(select_rows[:, :, state_size:, None] * states_all, axis=2)
        result = (readout + skip_gain * inflow) * jax.nn.silu(gate_rows.astype(jnp.float32))
        result = jnp.where(alive_rows[:, :, None], result, 0.0).astype(jnp.bfloat16)
        return (states_all[-1], result)

    pieces = (
        split_blocks(driven),
        split_blocks(gate_input),
        split_blocks(step_rate),
        split_blocks(selection),
        split_blocks(live_mask),
    )
    final_state, outputs = lax.scan(one_block, start_state, pieces)
    outputs = jnp.moveaxis(outputs, 2, 0).reshape(thought_count, positions, width_all)
    return (outputs, final_state)


def body(
    parent_state,
    parent_conv,
    fork_map,
    judge_lengths,
    mixer_input,
    gate_input,
    conv_weight,
    conv_bias,
    rate_down,
    selection_weight,
    rate_up,
    rate_bias,
    decay_log,
    skip_gain,
):
    thought_count, positions, width_local = mixer_input.shape
    driven = convolve(parent_conv, fork_map, mixer_input, conv_weight, conv_bias)
    token_rows = driven.reshape(thought_count * positions, width_local)
    low_part = jnp.dot(token_rows, rate_down, preferred_element_type=jnp.float32)
    select_part = jnp.dot(token_rows, selection_weight, preferred_element_type=jnp.float32)
    low_sum, selection = lax.psum((low_part, select_part), "chan")
    rate_low = low_sum.astype(jnp.bfloat16)
    step_rate = jax.nn.softplus(
        jnp.dot(rate_low, rate_up, preferred_element_type=jnp.float32) + rate_bias[None, :]
    )
    position = lax.broadcasted_iota(jnp.int32, (thought_count, positions), 1)
    live_mask = position < (GEN + judge_lengths)[:, None]
    step_rate = step_rate.reshape(thought_count, positions, width_local) * live_mask[
        :, :, None
    ].astype(jnp.float32)
    selection = selection.reshape(thought_count, positions, -1)
    start_state = jnp.take(parent_state, fork_map, axis=0)
    per_device = thought_count // lax.axis_size("chan")
    first_thought = lax.axis_index("chan") * per_device
    driven_mine, gate_mine = (
        lax.all_to_all(driven, "chan", split_axis=0, concat_axis=2, tiled=True),
        lax.all_to_all(gate_input, "chan", split_axis=0, concat_axis=2, tiled=True),
    )
    rate_mine, state_mine = (
        lax.all_to_all(
            step_rate.astype(jnp.bfloat16), "chan", split_axis=0, concat_axis=2, tiled=True
        ).astype(step_rate.dtype),
        lax.all_to_all(
            start_state.astype(jnp.bfloat16), "chan", split_axis=0, concat_axis=2, tiled=True
        ).astype(start_state.dtype),
    )
    decay_all, skip_all = (
        lax.all_gather(decay_log, "chan", axis=1, tiled=True),
        lax.all_gather(skip_gain, "chan", axis=0, tiled=True),
    )
    select_mine = lax.dynamic_slice_in_dim(selection, first_thought, per_device, 0)
    alive_mine = lax.dynamic_slice_in_dim(live_mask, first_thought, per_device, 0)
    mixer_output, final_state = run_scan(
        driven_mine, gate_mine, rate_mine, select_mine, alive_mine, state_mine, decay_all, skip_all
    )
    return (mixer_output, final_state)


def solution(mesh):
    placed = (
        P("group", None, "chan"),
        P("group", None, "chan"),
        P("group"),
        P("group"),
        P("group", None, "chan"),
        P("group", None, "chan"),
        P(None, "chan"),
        P("chan"),
        P("chan", None),
        P("chan", None),
        P(None, "chan"),
        P("chan"),
        P(None, "chan"),
        P("chan"),
    )
    return jax.shard_map(
        body,
        mesh=mesh,
        in_specs=placed,
        out_specs=(P(("group", "chan"), None, None), P(("group", "chan"), None, None)),
        check_vma=False,
    )
```

profile of v0, /device:TPU:1, one launch (start us, length us, event | category | flops | bytes accessed | tf_op | source)
XLA Modules:
  0.0 461.3 jit_solution(12604734536397217808)
XLA Ops:
  11.5 7.3 %all-to-all-start = ((bf16[16,16,1024]{2,1,0:T(8,128)(2,1)}), bf16[16,16,1024]{2,1,0:T(8,128)(2,1)S(1)}, u32[]{:S(2)}, u32[]{:S(2)}) async-start(bf16[16,16,1024]{2,1,0:T(8,128)(2,1)} %select_convert_fusion), calls=%async_computation | async-start | bytes 1048576 | tf_op jit(solution)/shard_map/all_to_all | solution.py:106
  26.2 66.7 %all-reduce.10 = (bf16[320,512]{1,0:T(8,128)(2,1)S(1)}, f32[16,20,32]{1,0,2:T(8,128)S(1)}) all-reduce(f32[320,512]{1,0:T(8,128)S(1)} %fusion.15, f32[16,20,32]{1,0,2:T(8,128)S(1)} %reshape.169), channel_id=1, replica_groups=mesh['group'=2,'chan'=16] {'chan'}, use_global_device_ids=true, to_apply=%region_0.1 | all-reduce | flops 174080 | bytes 1064960 | tf_op jit(solution)/shard_map/psum | solution.py:84
  96.7 28.4 %all_to_all.48 = bf16[16,20,1024]{2,1,0:T(8,128)(2,1)S(1)} all-to-all(bf16[16,20,1024]{2,1,0:T(8,128)(2,1)S(1)} %multiply_convert_fusion), channel_id=1, replica_groups=mesh['group'=2,'chan'=16] {'chan'}, dimensions={0} | all-to-all | bytes 1310720 | tf_op jit(solution)/shard_map/all_to_all | solution.py:103
  125.2 3.5 all-to-all-start.2
  131.9 16.1 %all-to-all-done.2 = bf16[16,20,1024]{2,1,0:T(8,128)(2,1)S(1)} async-done(((bf16[16,20,1024]{2,1,0:T(8,128)(2,1)}), bf16[16,20,1024]{2,1,0:T(8,128)(2,1)S(1)}, u32[]{:S(2)}, u32[]{:S(2)}) %all-to-all-start.2) | async-done | bytes 655392 | tf_op jit(solution)/shard_map/all_to_all | solution.py:99
  148.0 6.3 %all-to-all-start.3 = ((bf16[16,20,1024]{2,1,0:T(8,128)(2,1)}), bf16[16,20,1024]{2,1,0:T(8,128)(2,1)}, u32[]{:S(2)}, u32[]{:S(2)}) async-start(bf16[16,20,1024]{2,1,0:T(8,128)(2,1)} %copy.42), calls=%async_computation.3 | async-start | bytes 1572864 | tf_op jit(solution)/shard_map/all_to_all | solution.py:100
  154.5 33.2 %all_gather.7 = f32[16384]{0:T(1024)S(1)} all-gather(f32[1024]{0:T(1024)S(1)} %copy-done.16), channel_id=1, replica_groups=mesh['group'=2,'chan'=16] {'chan'}, dimensions={0}, use_global_device_ids=true | all-gather | bytes 69632 | tf_op jit(solution)/shard_map/all_gather | solution.py:112
  198.1 249.7 %while.12 = (s32[]{:T(128)}, f32[1,16,16384]{2,1,0:T(8,128)}, bf16[5,4,1,16384]{3,2,1,0:T(2,128)(2,1)}, f32[5,4,1,16384]{3,1,2,0:T(4,128)}, f32[16,16384]{1,0:T(...) while((s32[]{:T(128)}, f32[1,16,16384]{2,1,0:T(8,128)}, ...), condition=%wide.region_4.5_spmd, body=%wide.region_2.4_spmd.sunk | while | flops 14942210 | bytes 138480496 | solution.py:58
  204.5 6.1 %pad.85 = f32[4,1,16,16384]{3,2,1,0:T(8,128)} pad(f32[2,1,16,16384]{3,2,1,0:T(8,128)} %pad_maximum_fusion.4, f32[]{:T(128)} %constant.40.clone.7..sunk), padding=0_1_1x0_0_0x0_0_0x0_0_0 | pad | bytes 6291460 | tf_op jit(solution)/shard_map/while/body/eval_jaxpr/pad | solution.py:44
  210.6 2.8 pad_add_fusion.4
  213.3 6.2 %pad.86 = f32[4,1,16,16384]{3,2,1,0:T(8,128)} pad(f32[2,1,16,16384]{3,2,1,0:T(8,128)} %pad_add_fusion.4, f32[]{:T(128)} %constant.40.clone.7..sunk), padding=1_0_1x0_0_0x0_0_0x0_0_0 | pad | bytes 6291460 | tf_op jit(solution)/shard_map/while/body/eval_jaxpr/pad | solution.py:44
  219.6 2.7 pad_maximum_fusion.5
  222.2 6.2 %pad.87 = f32[4,1,16,16384]{3,2,1,0:T(8,128)} pad(f32[2,1,16,16384]{3,2,1,0:T(8,128)} %pad_maximum_fusion.5, f32[]{:T(128)} %constant.40.clone.7..sunk), padding=0_1_1x0_0_0x0_0_0x0_0_0 | pad | bytes 6291460 | tf_op jit(solution)/shard_map/while/body/eval_jaxpr/pad | solution.py:44
  229.8 6.1 %pad.88 = f32[4,1,16,16384]{3,2,1,0:T(8,128)} pad(f32[2,1,16,16384]{3,2,1,0:T(8,128)} %pad_add_fusion.5, f32[]{:T(128)} %constant.40.clone.7..sunk), padding=1_0_1x0_0_0x0_0_0x0_0_0 | pad | bytes 6291460 | tf_op jit(solution)/shard_map/while/body/eval_jaxpr/pad | solution.py:44
  235.9 8.0 %multiply_reduce_fusion.2 = (f32[4,16384]{1,0:T(4,128)S(1)}, f32[4,1,16,16384]{3,2,1,0:T(8,128)S(1)}) fusion(f32[4,16]{1,0:T(4,128)S(1)} %get-tuple-element.222, f32[4,1,16,16384]{3,2,1,0:T(8,128)} %pad.85, f32[4,1,16,16384]{3,2,1,0:T(8,128)} %pad.86, f32[16,16384]{1,0:T(8,128)S(1)} %bitcast.69, f32[4,1,16,16384]{3,2,1,0:T(8,128)} %pad.87, ...), kind=kLoop, calls=%fused_computation.2.clone.1 | loop fusion | flops 6225920 | bytes 22282496 | tf_op jit(solution)/shard_map/while/body/eval_jaxpr/reduce_sum | solution.py:46
  245.6 2.5 convert_dynamic-update-slice_fusion.2
  254.4 6.1 %pad.85 = f32[4,1,16,16384]{3,2,1,0:T(8,128)} pad(f32[2,1,16,16384]{3,2,1,0:T(8,128)} %pad_maximum_fusion.4, f32[]{:T(128)} %constant.40.clone.7..sunk), padding=0_1_1x0_0_0x0_0_0x0_0_0 | pad | bytes 6291460 | tf_op jit(solution)/shard_map/while/body/eval_jaxpr/pad | solution.py:44
  260.5 2.8 pad_add_fusion.4
  263.3 6.2 %pad.86 = f32[4,1,16,16384]{3,2,1,0:T(8,128)} pad(f32[2,1,16,16384]{3,2,1,0:T(8,128)} %pad_add_fusion.4, f32[]{:T(128)} %constant.40.clone.7..sunk), padding=1_0_1x0_0_0x0_0_0x0_0_0 | pad | bytes 6291460 | tf_op jit(solution)/shard_map/while/body/eval_jaxpr/pad | solution.py:44
  269.5 2.7 pad_maximum_fusion.5
  272.2 6.2 %pad.87 = f32[4,1,16,16384]{3,2,1,0:T(8,128)} pad(f32[2,1,16,16384]{3,2,1,0:T(8,128)} %pad_maximum_fusion.5, f32[]{:T(128)} %constant.40.clone.7..sunk), padding=0_1_1x0_0_0x0_0_0x0_0_0 | pad | bytes 6291460 | tf_op jit(solution)/shard_map/while/body/eval_jaxpr/pad | solution.py:44
  279.8 6.1 %pad.88 = f32[4,1,16,16384]{3,2,1,0:T(8,128)} pad(f32[2,1,16,16384]{3,2,1,0:T(8,128)} %pad_add_fusion.5, f32[]{:T(128)} %constant.40.clone.7..sunk), padding=1_0_1x0_0_0x0_0_0x0_0_0 | pad | bytes 6291460 | tf_op jit(solution)/shard_map/while/body/eval_jaxpr/pad | solution.py:44
  285.9 8.0 %multiply_reduce_fusion.2 = (f32[4,16384]{1,0:T(4,128)S(1)}, f32[4,1,16,16384]{3,2,1,0:T(8,128)S(1)}) fusion(f32[4,16]{1,0:T(4,128)S(1)} %get-tuple-element.222, f32[4,1,16,16384]{3,2,1,0:T(8,128)} %pad.85, f32[4,1,16,16384]{3,2,1,0:T(8,128)} %pad.86, f32[16,16384]{1,0:T(8,128)S(1)} %bitcast.69, f32[4,1,16,16384]{3,2,1,0:T(8,128)} %pad.87, ...), kind=kLoop, calls=%fused_computation.2.clone.1 | loop fusion | flops 6225920 | bytes 22282496 | tf_op jit(solution)/shard_map/while/body/eval_jaxpr/reduce_sum | solution.py:46
  295.6 2.5 convert_dynamic-update-slice_fusion.2
  304.4 6.1 %pad.85 = f32[4,1,16,16384]{3,2,1,0:T(8,128)} pad(f32[2,1,16,16384]{3,2,1,0:T(8,128)} %pad_maximum_fusion.4, f32[]{:T(128)} %constant.40.clone.7..sunk), padding=0_1_1x0_0_0x0_0_0x0_0_0 | pad | bytes 6291460 | tf_op jit(solution)/shard_map/while/body/eval_jaxpr/pad | solution.py:44
  310.5 2.8 pad_add_fusion.4
  313.2 6.2 %pad.86 = f32[4,1,16,16384]{3,2,1,0:T(8,128)} pad(f32[2,1,16,16384]{3,2,1,0:T(8,128)} %pad_add_fusion.4, f32[]{:T(128)} %constant.40.clone.7..sunk), padding=1_0_1x0_0_0x0_0_0x0_0_0 | pad | bytes 6291460 | tf_op jit(solution)/shard_map/while/body/eval_jaxpr/pad | solution.py:44
  319.4 2.7 pad_maximum_fusion.5
  322.1 6.2 %pad.87 = f32[4,1,16,16384]{3,2,1,0:T(8,128)} pad(f32[2,1,16,16384]{3,2,1,0:T(8,128)} %pad_maximum_fusion.5, f32[]{:T(128)} %constant.40.clone.7..sunk), padding=0_1_1x0_0_0x0_0_0x0_0_0 | pad | bytes 6291460 | tf_op jit(solution)/shard_map/while/body/eval_jaxpr/pad | solution.py:44
  329.7 6.1 %pad.88 = f32[4,1,16,16384]{3,2,1,0:T(8,128)} pad(f32[2,1,16,16384]{3,2,1,0:T(8,128)} %pad_add_fusion.5, f32[]{:T(128)} %constant.40.clone.7..sunk), padding=1_0_1x0_0_0x0_0_0x0_0_0 | pad | bytes 6291460 | tf_op jit(solution)/shard_map/while/body/eval_jaxpr/pad | solution.py:44
  335.8 8.0 %multiply_reduce_fusion.2 = (f32[4,16384]{1,0:T(4,128)S(1)}, f32[4,1,16,16384]{3,2,1,0:T(8,128)S(1)}) fusion(f32[4,16]{1,0:T(4,128)S(1)} %get-tuple-element.222, f32[4,1,16,16384]{3,2,1,0:T(8,128)} %pad.85, f32[4,1,16,16384]{3,2,1,0:T(8,128)} %pad.86, f32[16,16384]{1,0:T(8,128)S(1)} %bitcast.69, f32[4,1,16,16384]{3,2,1,0:T(8,128)} %pad.87, ...), kind=kLoop, calls=%fused_computation.2.clone.1 | loop fusion | flops 6225920 | bytes 22282496 | tf_op jit(solution)/shard_map/while/body/eval_jaxpr/reduce_sum | solution.py:46
  345.5 2.5 convert_dynamic-update-slice_fusion.2
  354.3 6.1 %pad.85 = f32[4,1,16,16384]{3,2,1,0:T(8,128)} pad(f32[2,1,16,16384]{3,2,1,0:T(8,128)} %pad_maximum_fusion.4, f32[]{:T(128)} %constant.40.clone.7..sunk), padding=0_1_1x0_0_0x0_0_0x0_0_0 | pad | bytes 6291460 | tf_op jit(solution)/shard_map/while/body/eval_jaxpr/pad | solution.py:44
  360.4 2.8 pad_add_fusion.4
  363.2 6.2 %pad.86 = f32[4,1,16,16384]{3,2,1,0:T(8,128)} pad(f32[2,1,16,16384]{3,2,1,0:T(8,128)} %pad_add_fusion.4, f32[]{:T(128)} %constant.40.clone.7..sunk), padding=1_0_1x0_0_0x0_0_0x0_0_0 | pad | bytes 6291460 | tf_op jit(solution)/shard_map/while/body/eval_jaxpr/pad | solution.py:44
  369.4 2.7 pad_maximum_fusion.5
  372.1 6.2 %pad.87 = f32[4,1,16,16384]{3,2,1,0:T(8,128)} pad(f32[2,1,16,16384]{3,2,1,0:T(8,128)} %pad_maximum_fusion.5, f32[]{:T(128)} %constant.40.clone.7..sunk), padding=0_1_1x0_0_0x0_0_0x0_0_0 | pad | bytes 6291460 | tf_op jit(solution)/shard_map/while/body/eval_jaxpr/pad | solution.py:44
  379.7 6.1 %pad.88 = f32[4,1,16,16384]{3,2,1,0:T(8,128)} pad(f32[2,1,16,16384]{3,2,1,0:T(8,128)} %pad_add_fusion.5, f32[]{:T(128)} %constant.40.clone.7..sunk), padding=1_0_1x0_0_0x0_0_0x0_0_0 | pad | bytes 6291460 | tf_op jit(solution)/shard_map/while/body/eval_jaxpr/pad | solution.py:44
  385.8 8.0 %multiply_reduce_fusion.2 = (f32[4,16384]{1,0:T(4,128)S(1)}, f32[4,1,16,16384]{3,2,1,0:T(8,128)S(1)}) fusion(f32[4,16]{1,0:T(4,128)S(1)} %get-tuple-element.222, f32[4,1,16,16384]{3,2,1,0:T(8,128)} %pad.85, f32[4,1,16,16384]{3,2,1,0:T(8,128)} %pad.86, f32[16,16384]{1,0:T(8,128)S(1)} %bitcast.69, f32[4,1,16,16384]{3,2,1,0:T(8,128)} %pad.87, ...), kind=kLoop, calls=%fused_computation.2.clone.1 | loop fusion | flops 6225920 | bytes 22282496 | tf_op jit(solution)/shard_map/while/body/eval_jaxpr/reduce_sum | solution.py:46
  395.5 2.5 convert_dynamic-update-slice_fusion.2
  404.3 6.1 %pad.85 = f32[4,1,16,16384]{3,2,1,0:T(8,128)} pad(f32[2,1,16,16384]{3,2,1,0:T(8,128)} %pad_maximum_fusion.4, f32[]{:T(128)} %constant.40.clone.7..sunk), padding=0_1_1x0_0_0x0_0_0x0_0_0 | pad | bytes 6291460 | tf_op jit(solution)/shard_map/while/body/eval_jaxpr/pad | solution.py:44
  410.4 2.8 pad_add_fusion.4
  413.1 6.2 %pad.86 = f32[4,1,16,16384]{3,2,1,0:T(8,128)} pad(f32[2,1,16,16384]{3,2,1,0:T(8,128)} %pad_add_fusion.4, f32[]{:T(128)} %constant.40.clone.7..sunk), padding=1_0_1x0_0_0x0_0_0x0_0_0 | pad | bytes 6291460 | tf_op jit(solution)/shard_map/while/body/eval_jaxpr/pad | solution.py:44
  419.3 2.7 pad_maximum_fusion.5
  422.0 6.2 %pad.87 = f32[4,1,16,16384]{3,2,1,0:T(8,128)} pad(f32[2,1,16,16384]{3,2,1,0:T(8,128)} %pad_maximum_fusion.5, f32[]{:T(128)} %constant.40.clone.7..sunk), padding=0_1_1x0_0_0x0_0_0x0_0_0 | pad | bytes 6291460 | tf_op jit(solution)/shard_map/while/body/eval_jaxpr/pad | solution.py:44
  429.6 6.1 %pad.88 = f32[4,1,16,16384]{3,2,1,0:T(8,128)} pad(f32[2,1,16,16384]{3,2,1,0:T(8,128)} %pad_add_fusion.5, f32[]{:T(128)} %constant.40.clone.7..sunk), padding=1_0_1x0_0_0x0_0_0x0_0_0 | pad | bytes 6291460 | tf_op jit(solution)/shard_map/while/body/eval_jaxpr/pad | solution.py:44
  435.7 8.0 %multiply_reduce_fusion.2 = (f32[4,16384]{1,0:T(4,128)S(1)}, f32[4,1,16,16384]{3,2,1,0:T(8,128)S(1)}) fusion(f32[4,16]{1,0:T(4,128)S(1)} %get-tuple-element.222, f32[4,1,16,16384]{3,2,1,0:T(8,128)} %pad.85, f32[4,1,16,16384]{3,2,1,0:T(8,128)} %pad.86, f32[16,16384]{1,0:T(8,128)S(1)} %bitcast.69, f32[4,1,16,16384]{3,2,1,0:T(8,128)} %pad.87, ...), kind=kLoop, calls=%fused_computation.2.clone.1 | loop fusion | flops 6225920 | bytes 22282496 | tf_op jit(solution)/shard_map/while/body/eval_jaxpr/reduce_sum | solution.py:46
  447.9 5.5 %reduce.2 = bf16[5,4,16384]{2,1,0:T(4,128)(2,1)S(1)} reduce(bf16[5,4,1,16384]{3,2,1,0:T(2,128)(2,1)} %get-tuple-element.55, bf16[]{:T(256)} %constant.83), dimensions={2}, to_apply=%get-tuple-element.55.reduce_sub_computation | reduce | bytes 1310722 | tf_op jit(solution)/shard_map/while | solution.py:58
  (198 shorter events, 79.6 us)
Async XLA Ops:
  7.2 85.8 %copy-start = (bf16[512,1024]{1,0:T(8,128)(2,1)S(1)}, bf16[512,1024]{1,0:T(8,128)(2,1)}, u32[]{:S(2)}) copy-start(bf16[512,1024]{1,0:T(8,128)(2,1)} %param.26) | copy-start | bytes 3145732
  8.6 10.2 %copy-start.12 = (bf16[16,20,1024]{2,0,1:T(8,128)(2,1)S(1)}, bf16[16,20,1024]{2,0,1:T(8,128)(2,1)}, u32[]{:S(2)}) copy-start(bf16[16,20,1024]{2,0,1:T(8,128)(2,1)} %param.20) | copy-start | bytes 1966084
  10.5 8.7 %copy-start.9 = (bf16[16,3,1024]{2,0,1:T(8,128)(2,1)S(1)}, bf16[16,3,1024]{2,0,1:T(8,128)(2,1)}, u32[]{:S(2)}) copy-start(bf16[16,3,1024]{2,0,1:T(8,128)(2,1)} %param.17) | copy-start | bytes 294916
  11.5 85.3 %all-to-all-start = ((bf16[16,16,1024]{2,1,0:T(8,128)(2,1)}), bf16[16,16,1024]{2,1,0:T(8,128)(2,1)S(1)}, u32[]{:S(2)}, u32[]{:S(2)}) async-start(bf16[16,16,1024]{2,1,0:T(8,128)(2,1)} %select_convert_fusion), calls=%async_computation | async-start | bytes 1048576 | tf_op jit(solution)/shard_map/all_to_all | solution.py:106
  22.6 3.0 copy-start.13
  25.7 67.3 %copy-start.17 = (f32[1024]{0:T(1024)S(1)}, f32[1024]{0:T(1024)}, u32[]{:S(2)}) copy-start(f32[1024]{0:T(1024)} %param.27) | copy-start | bytes 12292
  96.7 28.4 %copy-start.10 = (bf16[16,16,1024]{2,1,0:T(8,128)(2,1)}, bf16[16,16,1024]{2,1,0:T(8,128)(2,1)S(1)}, u32[]{:S(2)}) copy-start(bf16[16,16,1024]{2,1,0:T(8,128)(2,1)S(1)} %all-to-all-done) | copy-start | bytes 1572868
  125.2 22.8 %all-to-all-start.2 = ((bf16[16,20,1024]{2,1,0:T(8,128)(2,1)}), bf16[16,20,1024]{2,1,0:T(8,128)(2,1)S(1)}, u32[]{:S(2)}, u32[]{:S(2)}) async-start(bf16[16,20,1024]{2,1,0:T(8,128)(2,1)} %multiply_convert_fusion.1), calls=%async_computation.2 | async-start | bytes 1572864 | tf_op jit(solution)/shard_map/all_to_all | solution.py:99
  128.7 25.9 %copy-start.16 = (f32[1024]{0:T(1024)S(1)}, f32[1024]{0:T(1024)}, u32[]{:S(2)}) copy-start(f32[1024]{0:T(1024)} %param.29) | copy-start | bytes 12292
  128.7 68.1 %all-gather.2.cloned.1.call-start = ((), (), s32[]{:S(2)}) async-start(), calls=%async_computation.4 | async-start | bytes 1114112 | tf_op jit(solution)/shard_map/all_gather | solution.py:111
  129.4 58.3 %copy-start.11 = (bf16[16,16,1024]{2,1,0:T(8,128)(2,1)S(1)}, bf16[16,16,1024]{2,1,0:T(8,128)(2,1)}, u32[]{:S(2)}) copy-start(bf16[16,16,1024]{2,1,0:T(8,128)(2,1)} %copy-done.10) | copy-start | bytes 1572868
  148.0 44.9 %all-to-all-start.3 = ((bf16[16,20,1024]{2,1,0:T(8,128)(2,1)}), bf16[16,20,1024]{2,1,0:T(8,128)(2,1)}, u32[]{:S(2)}, u32[]{:S(2)}) async-start(bf16[16,20,1024]{2,1,0:T(8,128)(2,1)} %copy.42), calls=%async_computation.3 | async-start | bytes 1572864 | tf_op jit(solution)/shard_map/all_to_all | solution.py:100
  198.2 2.4 copy-start.5
  198.2 2.4 copy-start.7
  201.3 1.7 copy-start.2
  213.3 6.2 %copy-start.3 = (f32[1,1,16,16384]{3,2,1,0:T(8,128)S(1)}, f32[1,1,16,16384]{3,2,1,0:T(8,128)}, u32[]{:S(2)}) copy-start(f32[1,1,16,16384]{3,2,1,0:T(8,128)} %get-tuple-element.237) | copy-start | bytes 3145732 | tf_op jit(solution)/shard_map/while
  229.8 6.1 %copy-start.4 = (f32[1,16,16384]{2,1,0:T(8,128)S(1)}, f32[1,16,16384]{2,1,0:T(8,128)}, u32[]{:S(2)}) copy-start(f32[1,16,16384]{2,1,0:T(8,128)} %get-tuple-element.253) | copy-start | bytes 3145732 | tf_op jit(solution)/shard_map/while
  243.9 1.7 copy-start.8
  244.0 4.2 copy-start.6
  248.1 2.4 copy-start.5
  248.1 2.4 copy-start.7
  251.2 1.7 copy-start.2
  263.3 6.2 %copy-start.3 = (f32[1,1,16,16384]{3,2,1,0:T(8,128)S(1)}, f32[1,1,16,16384]{3,2,1,0:T(8,128)}, u32[]{:S(2)}) copy-start(f32[1,1,16,16384]{3,2,1,0:T(8,128)} %get-tuple-element.237) | copy-start | bytes 3145732 | tf_op jit(solution)/shard_map/while
  279.8 6.1 %copy-start.4 = (f32[1,16,16384]{2,1,0:T(8,128)S(1)}, f32[1,16,16384]{2,1,0:T(8,128)}, u32[]{:S(2)}) copy-start(f32[1,16,16384]{2,1,0:T(8,128)} %get-tuple-element.253) | copy-start | bytes 3145732 | tf_op jit(solution)/shard_map/while
  293.9 1.7 copy-start.8
  293.9 4.2 copy-start.6
  298.1 2.4 copy-start.5
  298.1 2.4 copy-start.7
  301.2 1.7 copy-start.2
  313.2 6.2 %copy-start.3 = (f32[1,1,16,16384]{3,2,1,0:T(8,128)S(1)}, f32[1,1,16,16384]{3,2,1,0:T(8,128)}, u32[]{:S(2)}) copy-start(f32[1,1,16,16384]{3,2,1,0:T(8,128)} %get-tuple-element.237) | copy-start | bytes 3145732 | tf_op jit(solution)/shard_map/while
  329.7 6.1 %copy-start.4 = (f32[1,16,16384]{2,1,0:T(8,128)S(1)}, f32[1,16,16384]{2,1,0:T(8,128)}, u32[]{:S(2)}) copy-start(f32[1,16,16384]{2,1,0:T(8,128)} %get-tuple-element.253) | copy-start | bytes 3145732 | tf_op jit(solution)/shard_map/while
  343.8 1.7 copy-start.8
  343.8 4.2 copy-start.6
  348.0 2.4 copy-start.5
  348.0 2.4 copy-start.7
  351.1 1.7 copy-start.2
  363.2 6.2 %copy-start.3 = (f32[1,1,16,16384]{3,2,1,0:T(8,128)S(1)}, f32[1,1,16,16384]{3,2,1,0:T(8,128)}, u32[]{:S(2)}) copy-start(f32[1,1,16,16384]{3,2,1,0:T(8,128)} %get-tuple-element.237) | copy-start | bytes 3145732 | tf_op jit(solution)/shard_map/while
  379.7 6.1 %copy-start.4 = (f32[1,16,16384]{2,1,0:T(8,128)S(1)}, f32[1,16,16384]{2,1,0:T(8,128)}, u32[]{:S(2)}) copy-start(f32[1,16,16384]{2,1,0:T(8,128)} %get-tuple-element.253) | copy-start | bytes 3145732 | tf_op jit(solution)/shard_map/while
  393.8 1.7 copy-start.8
  393.8 4.2 copy-start.6
  398.0 2.4 copy-start.5
  398.0 2.4 copy-start.7
  401.1 1.7 copy-start.2
  413.1 6.2 %copy-start.3 = (f32[1,1,16,16384]{3,2,1,0:T(8,128)S(1)}, f32[1,1,16,16384]{3,2,1,0:T(8,128)}, u32[]{:S(2)}) copy-start(f32[1,1,16,16384]{3,2,1,0:T(8,128)} %get-tuple-element.237) | copy-start | bytes 3145732 | tf_op jit(solution)/shard_map/while
  429.6 6.1 %copy-start.4 = (f32[1,16,16384]{2,1,0:T(8,128)S(1)}, f32[1,16,16384]{2,1,0:T(8,128)}, u32[]{:S(2)}) copy-start(f32[1,16,16384]{2,1,0:T(8,128)} %get-tuple-element.253) | copy-start | bytes 3145732 | tf_op jit(solution)/shard_map/while
  443.7 1.7 copy-start.8
  443.7 4.2 copy-start.6
  447.9 6.5 %copy-start.1 = (bf16[512,1024]{1,0:T(8,128)(2,1)S(1)}, bf16[512,1024]{1,0:T(8,128)(2,1)}, u32[]{:S(2)}) copy-start(bf16[512,1024]{1,0:T(8,128)(2,1)} %param.26) | copy-start | bytes 3145732
  (3 other events, 3.5 us)
Sparse Core Ops, SparseCore 0:
  131.7 44.2 all-gather.1
where the time goes:
time: 464 us; the launch traced here: 461 us
  local copies, waits for them, and re-layouts  150 us (32%)
  other arithmetic  130 us (28%)
  blocking collectives  128 us (28%)
  starting transfers between devices  17.2 us (4%)
  waiting for transfers between devices  16.8 us (4%)
  between operations  14.3 us (3%)
    pad x20, local copies, waits for them, and re-layouts, one_block(): lax.associative_scan(combine, (factor, push_term), axis=0)  123 us
    psum x1, blocking collectives, body(): low_sum, selection = lax.psum((low_part, select_part), 'chan')  66.7 us
    reduce_sum x5, other arithmetic, one_block(): readout = jnp.sum(select_rows[:, :, state_size:, None] * states_all, axis=2)  40 us
    all_gather x1, blocking collectives, body(): lax.all_gather(skip_gain, 'chan', axis=0, tiled=True)  33.2 us
    all_to_all x1, blocking collectives, body(): lax.all_to_all(step_rate.astype(jnp.bfloat16), 'chan', split_axis=0, conc...  28.4 us
    add x10, other arithmetic, one_block(): lax.associative_scan(combine, (factor, push_term), axis=0)  21.1 us
    concatenate x10, other arithmetic, one_block(): lax.associative_scan(combine, (factor, push_term), axis=0)  20.8 us
    all_to_all x1, waiting for transfers between devices, body(): lax.all_to_all(driven, 'chan', split_axis=0, concat_axis=2, tiled=True)  16.1 us
  transfers between devices with their start and end apart: 4, of which 1 were waited for; matrix products, arithmetic and copies ran while one was open for 5% of the time, Pallas kernels for 0%

commit v1 on v0

v1 whole, which is shorter than its diff:
```python
import functools

import jax
import jax.numpy as jnp
from jax import lax
from jax.experimental import pallas as pl
from jax.experimental.pallas import tpu as pltpu
from jax.sharding import PartitionSpec as P

GEN = 4


def convolve(parent_conv, fork_map, mixer_input, conv_weight, conv_bias):
    positions = mixer_input.shape[1]
    start_conv = jnp.take(parent_conv, fork_map, axis=0)
    padded = jnp.concatenate([start_conv, mixer_input], axis=1).astype(jnp.float32)
    tap_weights = conv_weight.astype(jnp.float32)
    summed = conv_bias[None, None, :] + tap_weights[0][None, None, :] * padded[:, 0:positions, :]
    for offset in range(1, conv_weight.shape[0]):
        summed = (
            summed + tap_weights[offset][None, None, :] * padded[:, offset : offset + positions, :]
        )
    return jax.nn.silu(summed).astype(jnp.bfloat16)


def scan_kernel(
    lens_ref, fmap_ref, rate_ref, drive_ref, gate_ref, b_ref, c_ref, h0_ref, a_ref, skip_ref,
    out_ref, hT_ref, u_scr, y_scr, *, width
):
    t = pl.program_id(0)
    positions = rate_ref.shape[1]
    state_size, width_local = h0_ref.shape[1], h0_ref.shape[2]
    live = jnp.clip(lens_ref[t] + GEN, 0, positions)
    inflow = drive_ref[0].astype(jnp.float32)
    u_scr[...] = rate_ref[0] * inflow
    b_all = b_ref[0]
    c_all = c_ref[0]
    lane = lax.broadcasted_iota(jnp.int32, b_all.shape, 1)
    for chunk in range(width_local // width):
        cols = pl.ds(chunk * width, width)
        decay = a_ref[:, cols]

        def step(p, h):
            pick = lane == p
            b_col = jnp.sum(jnp.where(pick, b_all, 0.0), axis=1, keepdims=True)
            c_col = jnp.sum(jnp.where(pick, c_all, 0.0), axis=1, keepdims=True)
            rate_row = rate_ref[0, pl.ds(p, 1), cols]
            push_row = u_scr[pl.ds(p, 1), cols]
            h = jnp.exp(rate_row * decay) * h + push_row * b_col
            y_scr[pl.ds(p, 1), cols] = jnp.sum(c_col * h, axis=0, keepdims=True)
            return h

        h = lax.fori_loop(0, live, step, h0_ref[0, :, cols])
        hT_ref[0, :, cols] = h
    gate = gate_ref[0].astype(jnp.float32)
    result = (y_scr[...] + skip_ref[...] * inflow) * jax.nn.silu(gate)
    row = lax.broadcasted_iota(jnp.int32, result.shape, 0)
    out_ref[0] = jnp.where(row < live, result, 0.0).astype(out_ref.dtype)


def run_scan(judge_lengths, fork_map, step_rate, driven, gate_input, b_t, c_t, parent_state,
             decay_rate, skip_gain):
    thought_count, positions, width_local = driven.shape
    state_size = parent_state.shape[1]
    width = min(512, width_local)
    kernel = functools.partial(scan_kernel, width=width)
    row_block = lambda t, lens, fmap: (t, 0, 0)
    grid_spec = pltpu.PrefetchScalarGridSpec(
        num_scalar_prefetch=2,
        grid=(thought_count,),
        in_specs=[
            pl.BlockSpec((1, positions, width_local), row_block),
            pl.BlockSpec((1, positions, width_local), row_block),
            pl.BlockSpec((1, positions, width_local), row_block),
            pl.BlockSpec((1, state_size, positions), row_block),
            pl.BlockSpec((1, state_size, positions), row_block),
            pl.BlockSpec((1, state_size, width_local), lambda t, lens, fmap: (fmap[t], 0, 0)),
            pl.BlockSpec((state_size, width_local), lambda t, lens, fmap: (0, 0)),
            pl.BlockSpec((1, width_local), lambda t, lens, fmap: (0, 0)),
        ],
        out_specs=[
            pl.BlockSpec((1, positions, width_local), row_block),
            pl.BlockSpec((1, state_size, width_local), row_block),
        ],
        scratch_shapes=[
            pltpu.VMEM((positions, width_local), jnp.float32),
            pltpu.VMEM((positions, width_local), jnp.float32),
        ],
    )
    return pl.pallas_call(
        kernel,
        grid_spec=grid_spec,
        out_shape=(
            jax.ShapeDtypeStruct((thought_count, positions, width_local), jnp.bfloat16),
            jax.ShapeDtypeStruct((thought_count, state_size, width_local), jnp.float32),
        ),
        compiler_params=pltpu.CompilerParams(dimension_semantics=("arbitrary",)),
    )(judge_lengths, fork_map, step_rate, driven, gate_input, b_t, c_t, parent_state,
      decay_rate, skip_gain.reshape(1, width_local))


def body(
    parent_state,
    parent_conv,
    fork_map,
    judge_lengths,
    mixer_input,
    gate_input,
    conv_weight,
    conv_bias,
    rate_down,
    selection_weight,
    rate_up,
    rate_bias,
    decay_log,
    skip_gain,
):
    thought_count, positions, width_local = mixer_input.shape
    state_size = parent_state.shape[1]
    rank = rate_down.shape[1]
    driven = convolve(parent_conv, fork_map, mixer_input, conv_weight, conv_bias)
    token_rows = driven.reshape(thought_count * positions, width_local)
    low_part = jnp.dot(token_rows, rate_down, preferred_element_type=jnp.float32)
    select_part = jnp.dot(token_rows, selection_weight, preferred_element_type=jnp.float32)
    summed = lax.psum(jnp.concatenate([low_part, select_part], axis=1), "chan")
    rate_low = summed[:, :rank].astype(jnp.bfloat16)
    selection = summed[:, rank:].reshape(thought_count, positions, 2 * state_size)
    step_rate = jax.nn.softplus(
        jnp.dot(rate_low, rate_up, preferred_element_type=jnp.float32) + rate_bias[None, :]
    ).reshape(thought_count, positions, width_local)
    b_t = jnp.swapaxes(selection[:, :, :state_size], 1, 2)
    c_t = jnp.swapaxes(selection[:, :, state_size:], 1, 2)
    decay_rate = -jnp.exp(decay_log)
    out_local, state_local = run_scan(
        judge_lengths, fork_map, step_rate, driven, gate_input, b_t, c_t, parent_state,
        decay_rate, skip_gain,
    )
    mixer_output = lax.all_to_all(out_local, "chan", split_axis=0, concat_axis=2, tiled=True)
    final_state = lax.all_to_all(state_local, "chan", split_axis=0, concat_axis=2, tiled=True)
    return (mixer_output, final_state)


def solution(mesh):
    placed = (
        P("group", None, "chan"),
        P("group", None, "chan"),
        P("group"),
        P("group"),
        P("group", None, "chan"),
        P("group", None, "chan"),
        P(None, "chan"),
        P("chan"),
        P("chan", None),
        P("chan", None),
        P(None, "chan"),
        P("chan"),
        P(None, "chan"),
        P("chan"),
    )
    return jax.shard_map(
        body,
        mesh=mesh,
        in_specs=placed,
        out_specs=(P(("group", "chan"), None, None), P(("group", "chan"), None, None)),
        check_vma=False,
    )
```

time: 464 us -> 219 us (0.47)
  local copies, waits for them, and re-layouts: 150 us -> 12 us
  other arithmetic: 130 us -> 4.4 us
  blocking collectives: 128 us -> 25.8 us
  waiting for transfers between devices: 16.8 us -> 114 us
  Pallas kernels: 0 us -> 40.6 us
  starting transfers between devices: 17.2 us -> 3.6 us
    pad x20 -> x0, local copies, waits for them, and re-layouts: 123 us -> none  [one_block(): lax.associative_scan(combine, (factor, push_term), axis=0)]
    psum x0 -> x1, waiting for transfers between devices: none -> 92 us  [body(): summed = lax.psum(jnp.concatenate([low_part, select_part], axis=1), 'chan')]
    psum x1 -> x0, blocking collectives: 66.7 us -> none  [body(): low_sum, selection = lax.psum((low_part, select_part), 'chan')]
    pallas_call x0 -> x1, Pallas kernels: none -> 40.6 us  [run_scan(): pl.pallas_call(kernel, grid_spec=grid_spec, out_shape=(jax.ShapeDtypeStru...]
    reduce_sum x5 -> x0, other arithmetic: 40 us -> none  [one_block(): readout = jnp.sum(select_rows[:, :, state_size:, None] * states_all, axis=2)]
    all_gather x1 -> x0, blocking collectives: 33.2 us -> none  [body(): lax.all_gather(skip_gain, 'chan', axis=0, tiled=True)]
    add x11 -> x0, other arithmetic: 21.1 us -> none  [the longest x10 21.1 us: one_block(): lax.associative_scan(combine, (factor, push_term), axis=0)]
    concatenate x10 -> x1, other arithmetic: 20.8 us -> 0.95 us  [body(): summed = lax.psum(jnp.concatenate([low_part, select_part], axis=1), 'chan')]
  transfers between devices with their start and end apart: 4 -> 2, of which waited for: 1 -> 2; matrix products, arithmetic and copies ran while one was open for 5% -> 1% of each run, Pallas kernels for 0% -> 0%
where the time goes in v1:
time: 219 us; the launch traced here: 217 us
  waiting for transfers between devices  114 us (52%)
  Pallas kernels  40.6 us (19%)
  blocking collectives  25.8 us (12%)
  between operations  14.2 us (6%)
  local copies, waits for them, and re-layouts  12 us (5%)
  other arithmetic  4.4 us (2%)
  starting transfers between devices  3.6 us (2%)
  matrix products  3.02 us (1%)
    psum x1, waiting for transfers between devices, body(): summed = lax.psum(jnp.concatenate([low_part, select_part], axis=1), 'chan')  92 us
    pallas_call x1, Pallas kernels, run_scan(): pl.pallas_call(kernel, grid_spec=grid_spec, out_shape=(jax.ShapeDtypeStru...  40.6 us
    all_to_all x1, blocking collectives, body(): lax.all_to_all(out_local, 'chan', split_axis=0, concat_axis=2, tiled=True)  25.8 us
    all_to_all x1, waiting for transfers between devices, body(): lax.all_to_all(state_local, 'chan', split_axis=0, concat_axis=2, tiled=True)  21.5 us
    unnamed x22, local copies, waits for them, and re-layouts  5.03 us
  transfers between devices with their start and end apart: 2, of which 2 were waited for; matrix products, arithmetic and copies ran while one was open for 1% of the time, Pallas kernels for 0%

profile of v1, /device:TPU:1, one launch (start us, length us, event | category | flops | bytes accessed | tf_op | source)
XLA Modules:
  0.0 217.1 jit_solution(17721640954601768058)
XLA Ops:
  7.2 0.0 copy-start
  7.2 0.0 copy-start.1
  7.2 0.0 all-reduce.2.cloned.1.call-start
  7.2 0.7 compare_and_fusion
  8.0 0.7 compare_select_fusion.1
  8.6 0.9 fusion.5
  9.5 1.5 copy.20
  11.0 0.0 copy-done.1
  11.0 0.8 gather_fusion
  11.8 0.0 copy-start.7
  11.8 0.1 copy_select_fusion
  12.0 0.3 maximum_convert_fusion
  12.2 0.3 copy-done.7
  12.5 1.0 multiply_convert_fusion.drive_ref
  13.5 0.0 copy-start.2
  13.5 0.0 copy-start.3
  13.6 0.1 reshape.27
  13.7 1.5 fusion.7
  15.2 0.0 copy-done.3
  15.2 0.5 fusion.6
  15.7 0.0 copy-done.2
  15.7 0.0 copy-start.4
  15.8 0.0 copy-start.5
  15.8 0.9 pad_maximum_fusion
  16.7 0.0 all-reduce.2.cloned.1.call-update
  16.7 0.4 copy-done.4
  17.1 0.0 copy-start.8
  17.1 1.3 copy.25.gate_ref
  18.3 0.0 copy-done.5
  18.3 0.6 exponential_negate_fusion.a_ref
  19.0 92.0 %all-reduce.2.cloned.1.call-done = f32[320,544]{1,0:T(8,128)} async-done(((f32[320,544]{1,0:T(8,128)}), f32[320,544]{1,0:T(8,128)}) %all-reduce.2.cloned.1.call-update) | async-done | bytes 696336 | tf_op jit(solution)/shard_map/psum | solution.py:125
  111.0 0.0 copy-start.6
  111.0 1.0 slice.60
  112.0 0.1 fusion.4
  112.2 0.8 copy.32
  113.0 0.8 copy.31
  113.8 0.0 copy-done
  113.8 0.0 copy-done.8
  113.8 0.0 copy-done.6
  113.8 1.0 compare_select_fusion
  114.8 1.3 reshape.28.rate_ref
  116.1 40.6 %shard_map.149 = (bf16[16,20,1024]{2,1,0:T(8,128)(2,1)}, f32[16,16,1024]{2,1,0:T(8,128)}) custom-call(s32[16]{0:T(128)} %lens_ref.1, s32[16]{0:T(128)} %fmap_ref.1, f32[16,20,1024]{2,1,0:T(8,128)} %reshape.28.rate_ref, bf16[16,20,1024]{2,1,0:T(8,128)(2,1)} %copy-done.2, bf16[16,20,1024]{2,1,0:T(8,128)(2,1)} %copy.25.gate_ref, f32[16,16,20]{2,1,0:T(8,128)} %bitcast.26, ...), custom_call_target="tpu_custom_call" | custom-call | tf_op jit(solution)/shard_map/pallas_call | solution.py:90
  156.7 25.8 %all_to_all.36 = bf16[16,20,1024]{2,1,0:T(8,128)(2,1)S(1)} all-to-all(bf16[16,20,1024]{2,1,0:T(8,128)(2,1)} %get-tuple-element.4), channel_id=1, replica_groups=mesh['group'=2,'chan'=16] {'chan'}, dimensions={0} | all-to-all | bytes 1310720 | tf_op jit(solution)/shard_map/all_to_all | solution.py:138
  182.6 3.6 %all-to-all-start.1 = ((f32[16,16,1024]{2,1,0:T(8,128)}), f32[16,16,1024]{2,1,0:T(8,128)S(1)}, u32[]{:S(2)}, u32[]{:S(2)}) async-start(f32[16,16,1024]{2,1,0:T(8,128)} %get-tuple-element.5), calls=%async_computation.1 | async-start | bytes 2097152 | tf_op jit(solution)/shard_map/all_to_all | solution.py:139
  186.1 0.4 copy.26
  186.5 1.3 all_to_all.29
  187.8 21.5 %all-to-all-done.1 = f32[16,16,1024]{2,1,0:T(8,128)S(1)} async-done(((f32[16,16,1024]{2,1,0:T(8,128)}), f32[16,16,1024]{2,1,0:T(8,128)S(1)}, u32[]{:S(2)}, u32[]{:S(2)}) %all-to-all-start.1) | async-done | bytes 1048608 | tf_op jit(solution)/shard_map/all_to_all | solution.py:139
  209.3 1.0 copy.33
  (2 shorter events, 0.0 us)
Async XLA Ops:
  7.2 106.6 %copy-start = (bf16[512,1024]{1,0:T(8,128)(2,1)S(1)}, bf16[512,1024]{1,0:T(8,128)(2,1)}, u32[]{:S(2)}) copy-start(bf16[512,1024]{1,0:T(8,128)(2,1)} %param.24) | copy-start | bytes 3145732
  7.2 3.8 %copy-start.1 = (bf16[16,3,1024]{2,0,1:T(8,128)(2,1)S(1)}, bf16[16,3,1024]{2,0,1:T(8,128)(2,1)}, u32[]{:S(2)}) copy-start(bf16[16,3,1024]{2,0,1:T(8,128)(2,1)} %param.15) | copy-start | bytes 294916
  7.2 103.8 %all-reduce.2.cloned.1.call-start = ((), (), s32[]{:S(2)}) async-start(), calls=%async_computation.2 | async-start | bytes 1638400 | tf_op jit(solution)/shard_map/psum | solution.py:125
  11.8 0.7 copy-start.7
  13.5 2.2 %copy-start.2 = (bf16[16,20,1024]{2,1,0:T(8,128)(2,1)}, bf16[16,20,1024]{2,1,0:T(8,128)(2,1)S(1)}, u32[]{:S(2)}) copy-start(bf16[16,20,1024]{2,1,0:T(8,128)(2,1)S(1)} %multiply_convert_fusion.drive_ref) | copy-start | bytes 1966084
  13.5 1.7 copy-start.3
  15.7 1.4 copy-start.4
  15.8 2.6 %copy-start.5 = (f32[16,1024]{1,0:T(8,128)S(1)}, f32[16,1024]{1,0:T(8,128)}, u32[]{:S(2)}) copy-start(f32[16,1024]{1,0:T(8,128)} %param.26) | copy-start | bytes 196612
  17.1 96.7 %copy-start.8 = (f32[1024]{0:T(1024)S(1)}, f32[1024]{0:T(1024)}, u32[]{:S(2)}) copy-start(f32[1024]{0:T(1024)} %param.25) | copy-start | bytes 12292
  111.0 2.8 %copy-start.6 = (f32[320,544]{1,0:T(8,128)S(1)}, f32[320,544]{1,0:T(8,128)}, u32[]{:S(2)}) copy-start(f32[320,544]{1,0:T(8,128)} %all-reduce.2.cloned.1.call-done) | copy-start | bytes 2088964
  182.6 26.7 %all-to-all-start.1 = ((f32[16,16,1024]{2,1,0:T(8,128)}), f32[16,16,1024]{2,1,0:T(8,128)S(1)}, u32[]{:S(2)}, u32[]{:S(2)}) async-start(f32[16,16,1024]{2,1,0:T(8,128)} %get-tuple-element.5), calls=%async_computation.1 | async-start | bytes 2097152 | tf_op jit(solution)/shard_map/all_to_all | solution.py:139
Sparse Core Ops, SparseCore 0:
  16.9 94.1 all-reduce.1

commit v2 on v1

--- a/solution.py
+++ b/solution.py
@@ -122,7 +122,12 @@
     token_rows = driven.reshape(thought_count * positions, width_local)
     low_part = jnp.dot(token_rows, rate_down, preferred_element_type=jnp.float32)
     select_part = jnp.dot(token_rows, selection_weight, preferred_element_type=jnp.float32)
-    summed = lax.psum(jnp.concatenate([low_part, select_part], axis=1), "chan")
+    partial = jnp.concatenate([low_part, select_part], axis=1)
+    devices = lax.axis_size("chan")
+    pieces = lax.all_to_all(
+        partial.reshape(devices, -1, partial.shape[1]), "chan", 0, 0, tiled=True
+    )
+    summed = lax.all_gather(jnp.sum(pieces, axis=0), "chan", axis=0, tiled=True)
     rate_low = summed[:, :rank].astype(jnp.bfloat16)
     selection = summed[:, rank:].reshape(thought_count, positions, 2 * state_size)
     step_rate = jax.nn.softplus(

time: 219 us -> 163 us (0.74)
  waiting for transfers between devices: 114 us -> 41.5 us
  blocking collectives: 25.8 us -> 49.2 us
  between operations: 14.2 us -> 0.82 us
  starting transfers between devices: 3.6 us -> 11 us
    psum x1 -> x0, waiting for transfers between devices: 92 us -> none  [body(): summed = lax.psum(jnp.concatenate([low_part, select_part], axis=1), 'chan')]
    all_gather x0 -> x1, blocking collectives: none -> 25 us  [body(): summed = lax.all_gather(jnp.sum(pieces, axis=0), 'chan', axis=0, tiled=True)]
    all_to_all x0 -> x1, waiting for transfers between devices: none -> 20.1 us  [body(): lax.all_to_all(partial.reshape(devices, -1, partial.shape[1]), 'chan', 0,...]
    all_to_all x0 -> x1, starting transfers between devices: none -> 7.48 us  [body(): lax.all_to_all(partial.reshape(devices, -1, partial.shape[1]), 'chan', 0,...]
    unnamed x22 -> x21, local copies, waits for them, and re-layouts: 5.03 us -> 4.75 us
where the time goes in v2:
time: 163 us; the launch traced here: 162 us
  blocking collectives  49.2 us (30%)
  waiting for transfers between devices  41.5 us (25%)
  Pallas kernels  40.6 us (25%)
  local copies, waits for them, and re-layouts  11.7 us (7%)
  starting transfers between devices  11 us (7%)
  other arithmetic  3.59 us (2%)
  matrix products  3.02 us (2%)
    pallas_call x1, Pallas kernels, run_scan(): pl.pallas_call(kernel, grid_spec=grid_spec, out_shape=(jax.ShapeDtypeStru...  40.6 us
    all_gather x1, blocking collectives, body(): summed = lax.all_gather(jnp.sum(pieces, axis=0), 'chan', axis=0, tiled=True)  25 us
    all_to_all x1, blocking collectives, body(): lax.all_to_all(out_local, 'chan', split_axis=0, concat_axis=2, tiled=True)  24.2 us
    all_to_all x1, waiting for transfers between devices, body(): lax.all_to_all(state_local, 'chan', split_axis=0, concat_axis=2, tiled=True)  21.4 us
    all_to_all x1, waiting for transfers between devices, body(): lax.all_to_all(partial.reshape(devices, -1, partial.shape[1]), 'chan', 0,...  20.1 us
    all_to_all x1, starting transfers between devices, body(): lax.all_to_all(partial.reshape(devices, -1, partial.shape[1]), 'chan', 0,...  7.48 us
    unnamed x21, local copies, waits for them, and re-layouts  4.75 us
    all_to_all x1, starting transfers between devices, body(): lax.all_to_all(state_local, 'chan', split_axis=0, concat_axis=2, tiled=True)  3.55 us
  transfers between devices with their start and end apart: 2, of which 2 were waited for; matrix products, arithmetic and copies ran while one was open for 1% of the time, Pallas kernels for 0%

profile of v2, /device:TPU:1, one launch (start us, length us, event | category | flops | bytes accessed | tf_op | source)
XLA Modules:
  0.0 161.5 jit_solution(7821107504575650878)
XLA Ops:
  0.6 0.0 copy-start
  0.6 0.0 copy-start.1
  0.7 0.8 compare_and_fusion
  1.4 0.7 compare_select_fusion.1
  2.1 0.9 fusion.5
  3.0 1.5 copy.29
  4.4 0.0 copy-done.1
  4.4 0.8 gather_fusion
  5.3 0.0 copy-start.6
  5.3 0.1 copy_select_fusion
  5.4 0.3 maximum_convert_fusion
  5.7 0.3 copy-done.6
  6.0 1.0 multiply_convert_fusion.drive_ref
  7.0 0.0 copy-start.2
  7.0 0.0 copy-start.3
  7.0 0.1 reshape.30
  7.1 1.5 fusion.7
  8.7 0.0 copy-done.3
  8.7 0.5 fusion.6
  9.2 0.0 copy-done.2
  9.2 0.1 pad_maximum_fusion
  9.3 0.0 copy-start.4
  9.3 1.0 reshape.31
  10.3 0.0 copy-start.5
  10.3 7.5 %all-to-all-start = ((f32[16,20,544]{2,1,0:T(8,128)}), f32[16,20,544]{2,1,0:T(8,128)S(1)}, u32[]{:S(2)}, u32[]{:S(2)}) async-start(f32[16,20,544]{2,1,0:T(8,128)} %reshape.31), calls=%async_computation | async-start | bytes 1966080 | tf_op jit(solution)/shard_map/all_to_all | solution.py:127
  17.8 0.0 copy-done.4
  17.8 1.3 copy.34.gate_ref
  19.0 0.0 copy-done.5
  19.0 0.6 exponential_negate_fusion.a_ref
  19.7 20.1 %all-to-all-done = f32[16,20,544]{2,1,0:T(8,128)S(1)} async-done(((f32[16,20,544]{2,1,0:T(8,128)}), f32[16,20,544]{2,1,0:T(8,128)S(1)}, u32[]{:S(2)}, u32[]{:S(2)}) %all-to-all-start) | async-done | bytes 696352 | tf_op jit(solution)/shard_map/all_to_all | solution.py:127
  39.8 0.1 reduce_sum.9
  39.8 25.0 %all-gather = f32[16,20,544]{2,1,0:T(8,128)S(1)} all-gather(f32[1,20,544]{2,1,0:T(8,128)S(1)} %bitcast.28), channel_id=1, replica_groups=mesh['group'=2,'chan'=16] {'chan'}, dimensions={0}, use_global_device_ids=true | all-gather | bytes 739840 | tf_op jit(solution)/shard_map/all_gather | solution.py:130
  64.8 0.0 copy-start.7
  64.8 0.1 reshape.45
  64.9 0.1 fusion.4
  65.0 0.8 copy.41
  65.9 0.8 copy.40
  66.7 0.0 copy-done
  66.7 0.0 copy-done.7
  66.7 1.0 compare_select_fusion
  67.7 1.3 reshape.32.rate_ref
  69.0 40.6 %shard_map.149 = (bf16[16,20,1024]{2,1,0:T(8,128)(2,1)}, f32[16,16,1024]{2,1,0:T(8,128)}) custom-call(s32[16]{0:T(128)} %lens_ref.1, s32[16]{0:T(128)} %fmap_ref.1, f32[16,20,1024]{2,1,0:T(8,128)} %reshape.32.rate_ref, bf16[16,20,1024]{2,1,0:T(8,128)(2,1)} %copy-done.2, bf16[16,20,1024]{2,1,0:T(8,128)(2,1)} %copy.34.gate_ref, f32[16,16,20]{2,1,0:T(8,128)} %bitcast.27, ...), custom_call_target="tpu_custom_call" | custom-call | tf_op jit(solution)/shard_map/pallas_call | solution.py:90
  109.6 24.2 %all_to_all.41 = bf16[16,20,1024]{2,1,0:T(8,128)(2,1)S(1)} all-to-all(bf16[16,20,1024]{2,1,0:T(8,128)(2,1)} %get-tuple-element.4), channel_id=1, replica_groups=mesh['group'=2,'chan'=16] {'chan'}, dimensions={0} | all-to-all | bytes 1310720 | tf_op jit(solution)/shard_map/all_to_all | solution.py:143
  133.9 3.6 %all-to-all-start.2 = ((f32[16,16,1024]{2,1,0:T(8,128)}), f32[16,16,1024]{2,1,0:T(8,128)S(1)}, u32[]{:S(2)}, u32[]{:S(2)}) async-start(f32[16,16,1024]{2,1,0:T(8,128)} %get-tuple-element.5), calls=%async_computation.2 | async-start | bytes 2097152 | tf_op jit(solution)/shard_map/all_to_all | solution.py:144
  137.4 0.4 copy.35
  137.8 1.3 all_to_all.33
  139.1 21.4 %all-to-all-done.2 = f32[16,16,1024]{2,1,0:T(8,128)S(1)} async-done(((f32[16,16,1024]{2,1,0:T(8,128)}), f32[16,16,1024]{2,1,0:T(8,128)S(1)}, u32[]{:S(2)}, u32[]{:S(2)}) %all-to-all-start.2) | async-done | bytes 1048608 | tf_op jit(solution)/shard_map/all_to_all | solution.py:144
  160.5 1.0 copy.42
  (3 shorter events, 0.0 us)
Async XLA Ops:
  0.6 66.0 %copy-start = (bf16[512,1024]{1,0:T(8,128)(2,1)S(1)}, bf16[512,1024]{1,0:T(8,128)(2,1)}, u32[]{:S(2)}) copy-start(bf16[512,1024]{1,0:T(8,128)(2,1)} %param.24) | copy-start | bytes 3145732
  0.6 3.8 %copy-start.1 = (bf16[16,3,1024]{2,0,1:T(8,128)(2,1)S(1)}, bf16[16,3,1024]{2,0,1:T(8,128)(2,1)}, u32[]{:S(2)}) copy-start(bf16[16,3,1024]{2,0,1:T(8,128)(2,1)} %param.15) | copy-start | bytes 294916
  5.3 0.7 copy-start.6
  7.0 2.2 %copy-start.2 = (bf16[16,20,1024]{2,1,0:T(8,128)(2,1)}, bf16[16,20,1024]{2,1,0:T(8,128)(2,1)S(1)}, u32[]{:S(2)}) copy-start(bf16[16,20,1024]{2,1,0:T(8,128)(2,1)S(1)} %multiply_convert_fusion.drive_ref) | copy-start | bytes 1966084
  7.0 1.7 %copy-start.3 = (bf16[1024,512]{1,0:T(8,128)(2,1)S(1)}, bf16[1024,512]{1,0:T(8,128)(2,1)}, u32[]{:S(2)}) copy-start(bf16[1024,512]{1,0:T(8,128)(2,1)} %param.22) | copy-start | bytes 3145732
  9.3 8.5 %copy-start.4 = (bf16[16,20,1024]{2,0,1:T(8,128)(2,1)S(1)}, bf16[16,20,1024]{2,0,1:T(8,128)(2,1)}, u32[]{:S(2)}) copy-start(bf16[16,20,1024]{2,0,1:T(8,128)(2,1)} %param.19) | copy-start | bytes 1966084
  10.3 8.7 %copy-start.5 = (f32[16,1024]{1,0:T(8,128)S(1)}, f32[16,1024]{1,0:T(8,128)}, u32[]{:S(2)}) copy-start(f32[16,1024]{1,0:T(8,128)} %param.26) | copy-start | bytes 196612
  10.3 29.5 %all-to-all-start = ((f32[16,20,544]{2,1,0:T(8,128)}), f32[16,20,544]{2,1,0:T(8,128)S(1)}, u32[]{:S(2)}, u32[]{:S(2)}) async-start(f32[16,20,544]{2,1,0:T(8,128)} %reshape.31), calls=%async_computation | async-start | bytes 1966080 | tf_op jit(solution)/shard_map/all_to_all | solution.py:127
  64.8 1.9 %copy-start.7 = (f32[1024]{0:T(1024)S(1)}, f32[1024]{0:T(1024)}, u32[]{:S(2)}) copy-start(f32[1024]{0:T(1024)} %param.25) | copy-start | bytes 12292
  133.9 26.6 %all-to-all-start.2 = ((f32[16,16,1024]{2,1,0:T(8,128)}), f32[16,16,1024]{2,1,0:T(8,128)S(1)}, u32[]{:S(2)}, u32[]{:S(2)}) async-start(f32[16,16,1024]{2,1,0:T(8,128)} %get-tuple-element.5), calls=%async_computation.2 | async-start | bytes 2097152 | tf_op jit(solution)/shard_map/all_to_all | solution.py:144

commit v3 on v2

--- a/solution.py
+++ b/solution.py
@@ -25,7 +25,7 @@
 
 def scan_kernel(
     lens_ref, fmap_ref, rate_ref, drive_ref, gate_ref, b_ref, c_ref, h0_ref, a_ref, skip_ref,
-    out_ref, hT_ref, u_scr, y_scr, *, width
+    packed_ref, u_scr, y_scr, *, width
 ):
     t = pl.program_id(0)
     positions = rate_ref.shape[1]
@@ -51,11 +51,11 @@
             return h
 
         h = lax.fori_loop(0, live, step, h0_ref[0, :, cols])
-        hT_ref[0, :, cols] = h
+        packed_ref[0, :state_size, cols] = h.astype(packed_ref.dtype)
     gate = gate_ref[0].astype(jnp.float32)
     result = (y_scr[...] + skip_ref[...] * inflow) * jax.nn.silu(gate)
     row = lax.broadcasted_iota(jnp.int32, result.shape, 0)
-    out_ref[0] = jnp.where(row < live, result, 0.0).astype(out_ref.dtype)
+    packed_ref[0, state_size:, :] = jnp.where(row < live, result, 0.0).astype(packed_ref.dtype)
 
 
 def run_scan(judge_lengths, fork_map, step_rate, driven, gate_input, b_t, c_t, parent_state,
@@ -78,10 +78,7 @@
             pl.BlockSpec((state_size, width_local), lambda t, lens, fmap: (0, 0)),
             pl.BlockSpec((1, width_local), lambda t, lens, fmap: (0, 0)),
         ],
-        out_specs=[
-            pl.BlockSpec((1, positions, width_local), row_block),
-            pl.BlockSpec((1, state_size, width_local), row_block),
-        ],
+        out_specs=pl.BlockSpec((1, state_size + positions, width_local), row_block),
         scratch_shapes=[
             pltpu.VMEM((positions, width_local), jnp.float32),
             pltpu.VMEM((positions, width_local), jnp.float32),
@@ -90,9 +87,8 @@
     return pl.pallas_call(
         kernel,
         grid_spec=grid_spec,
-        out_shape=(
-            jax.ShapeDtypeStruct((thought_count, positions, width_local), jnp.bfloat16),
-            jax.ShapeDtypeStruct((thought_count, state_size, width_local), jnp.float32),
+        out_shape=jax.ShapeDtypeStruct(
+            (thought_count, state_size + positions, width_local), jnp.bfloat16
         ),
         compiler_params=pltpu.CompilerParams(dimension_semantics=("arbitrary",)),
     )(judge_lengths, fork_map, step_rate, driven, gate_input, b_t, c_t, parent_state,
@@ -127,21 +123,31 @@
     pieces = lax.all_to_all(
         partial.reshape(devices, -1, partial.shape[1]), "chan", 0, 0, tiled=True
     )
-    summed = lax.all_gather(jnp.sum(pieces, axis=0), "chan", axis=0, tiled=True)
-    rate_low = summed[:, :rank].astype(jnp.bfloat16)
-    selection = summed[:, rank:].reshape(thought_count, positions, 2 * state_size)
+    reduced = jnp.sum(pieces, axis=0)
+    low_mine = reduced[:, :rank].astype(jnp.bfloat16)
+    select_high = reduced[:, rank:].astype(jnp.bfloat16)
+    select_low = (reduced[:, rank:] - select_high.astype(jnp.float32)).astype(jnp.bfloat16)
+    gathered = lax.all_gather(
+        jnp.concatenate([low_mine, select_high, select_low], axis=1), "chan", axis=0, tiled=True
+    )
+    rate_low = gathered[:, :rank]
+    selection = (
+        gathered[:, rank : rank + 2 * state_size].astype(jnp.float32)
+        + gathered[:, rank + 2 * state_size :].astype(jnp.float32)
+    ).reshape(thought_count, positions, 2 * state_size)
     step_rate = jax.nn.softplus(
         jnp.dot(rate_low, rate_up, preferred_element_type=jnp.float32) + rate_bias[None, :]
     ).reshape(thought_count, positions, width_local)
     b_t = jnp.swapaxes(selection[:, :, :state_size], 1, 2)
     c_t = jnp.swapaxes(selection[:, :, state_size:], 1, 2)
     decay_rate = -jnp.exp(decay_log)
-    out_local, state_local = run_scan(
+    packed_local = run_scan(
         judge_lengths, fork_map, step_rate, driven, gate_input, b_t, c_t, parent_state,
         decay_rate, skip_gain,
     )
-    mixer_output = lax.all_to_all(out_local, "chan", split_axis=0, concat_axis=2, tiled=True)
-    final_state = lax.all_to_all(state_local, "chan", split_axis=0, concat_axis=2, tiled=True)
+    packed = lax.all_to_all(packed_local, "chan", split_axis=0, concat_axis=2, tiled=True)
+    final_state = packed[:, :state_size].astype(jnp.float32)
+    mixer_output = packed[:, state_size:]
     return (mixer_output, final_state)
 
 

time: 163 us -> 147 us (0.902)
  waiting for transfers between devices: 41.5 us -> 20.1 us
  blocking collectives: 49.2 us -> 59.1 us
  starting transfers between devices: 11 us -> 7.48 us
    all_to_all x1 -> x0, waiting for transfers between devices: 21.4 us -> none  [body(): lax.all_to_all(state_local, 'chan', split_axis=0, concat_axis=2, tiled=True)]
    all_to_all x1, blocking collectives: 24.2 us -> 35.6 us  [body(): lax.all_to_all(packed_local, 'chan', split_axis=0, concat_axis=2, tiled=T...]
    all_to_all x1 -> x0, starting transfers between devices: 3.55 us -> none  [body(): lax.all_to_all(state_local, 'chan', split_axis=0, concat_axis=2, tiled=True)]
  transfers between devices with their start and end apart: 2 -> 1, of which waited for: 2 -> 1; matrix products, arithmetic and copies ran while one was open for 1% -> 1% of each run, Pallas kernels for 0% -> 0%
where the time goes in v3:
time: 147 us
  blocking collectives  59.1 us (40%)
  Pallas kernels  40.6 us (28%)
  waiting for transfers between devices  20.1 us (14%)
  local copies, waits for them, and re-layouts  10.8 us (7%)
  starting transfers between devices  7.48 us (5%)
  other arithmetic  4.72 us (3%)
  matrix products  3.03 us (2%)
    pallas_call x1, Pallas kernels, run_scan(): pl.pallas_call(kernel, grid_spec=grid_spec, out_shape=jax.ShapeDtypeStruc...  40.6 us
    all_to_all x1, blocking collectives, body(): lax.all_to_all(packed_local, 'chan', split_axis=0, concat_axis=2, tiled=T...  35.6 us
    all_gather x1, blocking collectives, body(): lax.all_gather(jnp.concatenate([low_mine, select_high, select_low], axis=...  23.5 us
    all_to_all x1, waiting for transfers between devices, body(): lax.all_to_all(partial.reshape(devices, -1, partial.shape[1]), 'chan', 0,...  20.1 us
    all_to_all x1, starting transfers between devices, body(): lax.all_to_all(partial.reshape(devices, -1, partial.shape[1]), 'chan', 0,...  7.48 us
    unnamed x21, local copies, waits for them, and re-layouts  3.38 us
  transfers between devices with their start and end apart: 1, of which 1 were waited for; matrix products, arithmetic and copies ran while one was open for 1% of the time, Pallas kernels for 0%

profile of v3, /device:TPU:1, one launch (start us, length us, event | category | flops | bytes accessed | tf_op | source)
XLA Modules:
  0.0 146.7 jit_solution(8079616188427137161)
XLA Ops:
  0.6 0.0 copy-start
  0.6 0.0 copy-start.1
  0.7 0.8 compare_and_fusion
  1.4 0.7 compare_select_fusion.1
  2.1 0.9 fusion.7
  3.0 1.5 copy.36
  4.4 0.0 copy-done.1
  4.4 0.8 gather_fusion
  5.3 0.0 copy-start.6
  5.3 0.1 copy_select_fusion
  5.4 0.3 maximum_convert_fusion
  5.7 0.3 copy-done.6
  6.0 1.0 multiply_convert_fusion.drive_ref
  7.0 0.0 copy-start.2
  7.0 0.0 copy-start.3
  7.0 0.1 reshape.30
  7.1 1.5 %fusion.9 = f32[320,32]{1,0:T(8,128)S(1)} fusion(bf16[320,1024]{1,0:T(8,128)(2,1)S(1)} %reshape.30, bf16[1024,32]{0,1:T(8,128)(2,1)} %param.23), kind=kOutput, calls=%fused_computation.32 | convolution fusion | flops 20971520 | bytes 761856 | tf_op jit(solution)/shard_map/dot_general | solution.py:120
  8.7 0.0 copy-done.3
  8.7 0.5 fusion.8
  9.2 0.0 copy-done.2
  9.2 0.1 pad_maximum_fusion
  9.3 0.0 copy-start.4
  9.3 1.0 reshape.31
  10.3 7.5 %all-to-all-start = ((f32[16,20,544]{2,1,0:T(8,128)}), f32[16,20,544]{2,1,0:T(8,128)S(1)}, u32[]{:S(2)}, u32[]{:S(2)}) async-start(f32[16,20,544]{2,1,0:T(8,128)} %reshape.31), calls=%async_computation | async-start | bytes 1966080 | tf_op jit(solution)/shard_map/all_to_all | solution.py:123
  17.8 0.0 copy-done.4
  17.8 1.3 copy.42.gate_ref
  19.1 0.0 copy-done.5
  19.1 0.6 exponential_negate_fusion.a_ref
  19.7 20.1 %all-to-all-done = f32[16,20,544]{2,1,0:T(8,128)S(1)} async-done(((f32[16,20,544]{2,1,0:T(8,128)}), f32[16,20,544]{2,1,0:T(8,128)S(1)}, u32[]{:S(2)}, u32[]{:S(2)}) %all-to-all-start) | async-done | bytes 696352 | tf_op jit(solution)/shard_map/all_to_all | solution.py:123
  39.8 0.1 reduce_sum.9
  39.8 0.0 copy-start.7
  39.9 0.1 maximum_bitcast_fusion
  39.9 23.5 %all-gather = bf16[16,20,576]{2,1,0:T(8,128)(2,1)S(1)} all-gather(bf16[1,20,576]{2,1,0:T(8,128)(2,1)S(1)} %maximum_bitcast_fusion), channel_id=1, replica_groups=mesh['group'=2,'chan'=16] {'chan'}, dimensions={0}, use_global_device_ids=true | all-gather | bytes 391680 | tf_op jit(solution)/shard_map/all_gather | solution.py:130
  63.4 0.2 reshape.45
  63.6 0.1 fusion.5
  63.7 0.1 copy.45
  63.8 0.1 copy.46
  63.9 0.2 reshape.33
  64.1 0.0 copy-done
  64.1 1.0 compare_select_fusion
  65.2 1.3 reshape.32.rate_ref
  66.5 0.8 copy_bitcast_fusion
  67.2 40.6 %shard_map.149 = bf16[16,36,1024]{2,1,0:T(8,128)(2,1)} custom-call(s32[16]{0:T(128)} %lens_ref.1, s32[16]{0:T(128)} %fmap_ref.1, f32[16,20,1024]{2,1,0:T(8,128)} %reshape.32.rate_ref, bf16[16,20,1024]{2,1,0:T(8,128)(2,1)} %copy-done.2, bf16[16,20,1024]{2,1,0:T(8,128)(2,1)} %copy.42.gate_ref, f32[16,16,20]{2,1,0:T(8,128)} %get-tuple-element.13.b_ref, ...), custom_call_target="tpu_custom_call" | custom-call | tf_op jit(solution)/shard_map/pallas_call | solution.py:87
  107.8 35.6 %all_to_all.23 = bf16[16,36,1024]{2,1,0:T(8,128)(2,1)S(1)} all-to-all(bf16[16,36,1024]{2,1,0:T(8,128)(2,1)} %shard_map.149), channel_id=1, replica_groups=mesh['group'=2,'chan'=16] {'chan'}, dimensions={0} | all-to-all | bytes 2359296 | tf_op jit(solution)/shard_map/all_to_all | solution.py:148
  143.4 0.7 copy.43
  144.1 0.6 all_to_all.20
  144.7 0.9 slice.87
  145.6 1.0 slice_convert_fusion
  (7 shorter events, 0.1 us)
Async XLA Ops:
  0.6 63.5 %copy-start = (bf16[512,1024]{1,0:T(8,128)(2,1)S(1)}, bf16[512,1024]{1,0:T(8,128)(2,1)}, u32[]{:S(2)}) copy-start(bf16[512,1024]{1,0:T(8,128)(2,1)} %param.24) | copy-start | bytes 3145732
  0.6 3.8 %copy-start.1 = (bf16[16,3,1024]{2,0,1:T(8,128)(2,1)S(1)}, bf16[16,3,1024]{2,0,1:T(8,128)(2,1)}, u32[]{:S(2)}) copy-start(bf16[16,3,1024]{2,0,1:T(8,128)(2,1)} %param.15) | copy-start | bytes 294916
  5.3 0.7 copy-start.6
  7.0 2.2 %copy-start.2 = (bf16[16,20,1024]{2,1,0:T(8,128)(2,1)}, bf16[16,20,1024]{2,1,0:T(8,128)(2,1)S(1)}, u32[]{:S(2)}) copy-start(bf16[16,20,1024]{2,1,0:T(8,128)(2,1)S(1)} %multiply_convert_fusion.drive_ref) | copy-start | bytes 1966084
  7.0 1.7 %copy-start.3 = (bf16[1024,512]{1,0:T(8,128)(2,1)S(1)}, bf16[1024,512]{1,0:T(8,128)(2,1)}, u32[]{:S(2)}) copy-start(bf16[1024,512]{1,0:T(8,128)(2,1)} %param.22) | copy-start | bytes 3145732
  9.3 8.5 %copy-start.4 = (bf16[16,20,1024]{2,0,1:T(8,128)(2,1)S(1)}, bf16[16,20,1024]{2,0,1:T(8,128)(2,1)}, u32[]{:S(2)}) copy-start(bf16[16,20,1024]{2,0,1:T(8,128)(2,1)} %param.19) | copy-start | bytes 1966084
  10.3 8.8 %copy-start.5 = (f32[16,1024]{1,0:T(8,128)S(1)}, f32[16,1024]{1,0:T(8,128)}, u32[]{:S(2)}) copy-start(f32[16,1024]{1,0:T(8,128)} %param.26) | copy-start | bytes 196612
  10.3 29.5 %all-to-all-start = ((f32[16,20,544]{2,1,0:T(8,128)}), f32[16,20,544]{2,1,0:T(8,128)S(1)}, u32[]{:S(2)}, u32[]{:S(2)}) async-start(f32[16,20,544]{2,1,0:T(8,128)} %reshape.31), calls=%async_computation | async-start | bytes 1966080 | tf_op jit(solution)/shard_map/all_to_all | solution.py:123
  39.8 24.3 %copy-start.7 = (f32[1024]{0:T(1024)S(1)}, f32[1024]{0:T(1024)}, u32[]{:S(2)}) copy-start(f32[1024]{0:T(1024)} %param.25) | copy-start | bytes 12292

commit v4 on v3

--- a/solution.py
+++ b/solution.py
@@ -1,5 +1,3 @@
-import functools
-
 import jax
 import jax.numpy as jnp
 from jax import lax
@@ -25,45 +23,35 @@
 
 def scan_kernel(
     lens_ref, fmap_ref, rate_ref, drive_ref, gate_ref, b_ref, c_ref, h0_ref, a_ref, skip_ref,
-    packed_ref, u_scr, y_scr, *, width
+    packed_ref, r_scr, u_scr, y_scr
 ):
     t = pl.program_id(0)
     positions = rate_ref.shape[1]
-    state_size, width_local = h0_ref.shape[1], h0_ref.shape[2]
+    state_size = h0_ref.shape[1]
     live = jnp.clip(lens_ref[t] + GEN, 0, positions)
     inflow = drive_ref[0].astype(jnp.float32)
-    u_scr[...] = rate_ref[0] * inflow
+    alive = lax.broadcasted_iota(jnp.int32, inflow.shape, 0) < live
+    rate = jnp.where(alive, rate_ref[0], 0.0)
+    r_scr[...] = rate
+    u_scr[...] = rate * inflow
     b_all = b_ref[0]
     c_all = c_ref[0]
-    lane = lax.broadcasted_iota(jnp.int32, b_all.shape, 1)
-    for chunk in range(width_local // width):
-        cols = pl.ds(chunk * width, width)
-        decay = a_ref[:, cols]
-
-        def step(p, h):
-            pick = lane == p
-            b_col = jnp.sum(jnp.where(pick, b_all, 0.0), axis=1, keepdims=True)
-            c_col = jnp.sum(jnp.where(pick, c_all, 0.0), axis=1, keepdims=True)
-            rate_row = rate_ref[0, pl.ds(p, 1), cols]
-            push_row = u_scr[pl.ds(p, 1), cols]
-            h = jnp.exp(rate_row * decay) * h + push_row * b_col
-            y_scr[pl.ds(p, 1), cols] = jnp.sum(c_col * h, axis=0, keepdims=True)
-            return h
-
-        h = lax.fori_loop(0, live, step, h0_ref[0, :, cols])
-        packed_ref[0, :state_size, cols] = h.astype(packed_ref.dtype)
+    decay = a_ref[...]
+    h = h0_ref[0]
+    for p in range(positions):
+        h = jnp.exp(r_scr[p : p + 1, :] * decay) * h + u_scr[p : p + 1, :] * b_all[:, p : p + 1]
+        y_scr[p : p + 1, :] = jnp.sum(c_all[:, p : p + 1] * h, axis=0, keepdims=True)
+    packed_ref[0, :state_size, :] = h.astype(packed_ref.dtype)
     gate = gate_ref[0].astype(jnp.float32)
     result = (y_scr[...] + skip_ref[...] * inflow) * jax.nn.silu(gate)
-    row = lax.broadcasted_iota(jnp.int32, result.shape, 0)
-    packed_ref[0, state_size:, :] = jnp.where(row < live, result, 0.0).astype(packed_ref.dtype)
+    packed_ref[0, state_size:, :] = jnp.where(alive, result, 0.0).astype(packed_ref.dtype)
 
 
 def run_scan(judge_lengths, fork_map, step_rate, driven, gate_input, b_t, c_t, parent_state,
              decay_rate, skip_gain):
     thought_count, positions, width_local = driven.shape
     state_size = parent_state.shape[1]
-    width = min(512, width_local)
-    kernel = functools.partial(scan_kernel, width=width)
+    kernel = scan_kernel
     row_block = lambda t, lens, fmap: (t, 0, 0)
     grid_spec = pltpu.PrefetchScalarGridSpec(
         num_scalar_prefetch=2,
@@ -79,10 +67,7 @@
             pl.BlockSpec((1, width_local), lambda t, lens, fmap: (0, 0)),
         ],
         out_specs=pl.BlockSpec((1, state_size + positions, width_local), row_block),
-        scratch_shapes=[
-            pltpu.VMEM((positions, width_local), jnp.float32),
-            pltpu.VMEM((positions, width_local), jnp.float32),
-        ],
+        scratch_shapes=[pltpu.VMEM((positions, width_local), jnp.float32)] * 3,
     )
     return pl.pallas_call(
         kernel,

time: 147 us -> 123 us (0.84)
  Pallas kernels: 40.6 us -> 15.5 us
    pallas_call x1, Pallas kernels: 40.6 us -> 15.5 us  [run_scan(): pl.pallas_call(kernel, grid_spec=grid_spec, out_shape=jax.ShapeDtypeStruc...]
  transfers between devices with their start and end apart: 1 -> 1, of which waited for: 1 -> 1; matrix products, arithmetic and copies ran while one was open for 1% -> 2% of each run, Pallas kernels for 0% -> 0%
where the time goes in v4:
time: 123 us; the launch traced here: 122 us
  blocking collectives  59.1 us (48%)
  waiting for transfers between devices  20.1 us (16%)
  Pallas kernels  15.5 us (13%)
  local copies, waits for them, and re-layouts  10.8 us (9%)
  starting transfers between devices  7.48 us (6%)
  other arithmetic  4.72 us (4%)
  matrix products  3.03 us (2%)
    all_to_all x1, blocking collectives, body(): lax.all_to_all(packed_local, 'chan', split_axis=0, concat_axis=2, tiled=T...  35.6 us
    all_gather x1, blocking collectives, body(): lax.all_gather(jnp.concatenate([low_mine, select_high, select_low], axis=...  23.5 us
    all_to_all x1, waiting for transfers between devices, body(): lax.all_to_all(partial.reshape(devices, -1, partial.shape[1]), 'chan', 0,...  20.1 us
    pallas_call x1, Pallas kernels, run_scan(): pl.pallas_call(kernel, grid_spec=grid_spec, out_shape=jax.ShapeDtypeStruc...  15.5 us
    all_to_all x1, starting transfers between devices, body(): lax.all_to_all(partial.reshape(devices, -1, partial.shape[1]), 'chan', 0,...  7.48 us
    unnamed x21, local copies, waits for them, and re-layouts  3.38 us
  transfers between devices with their start and end apart: 1, of which 1 were waited for; matrix products, arithmetic and copies ran while one was open for 2% of the time, Pallas kernels for 0%

profile of v4, /device:TPU:1, one launch (start us, length us, event | category | flops | bytes accessed | tf_op | source)
XLA Modules:
  0.0 121.5 jit_solution(9371823463902624242)
XLA Ops:
  0.6 0.0 copy-start
  0.6 0.0 copy-start.1
  0.7 0.8 compare_and_fusion
  1.4 0.7 compare_select_fusion.1
  2.1 0.9 fusion.7
  3.0 1.5 %copy.36 = bf16[16,20,1024]{2,1,0:T(8,128)(2,1)S(1)} copy(bf16[16,20,1024]{2,0,1:T(8,128)(2,1)} %param.18) | data formatting | bytes 1310720 | tf_op args[4]
  4.4 0.0 copy-done.1
  4.4 0.8 gather_fusion
  5.3 0.0 copy-start.6
  5.3 0.1 copy_select_fusion
  5.4 0.3 maximum_convert_fusion
  5.7 0.3 copy-done.6
  6.0 1.0 multiply_convert_fusion.drive_ref
  7.0 0.0 copy-start.2
  7.0 0.0 copy-start.3
  7.0 0.1 reshape.30
  7.1 1.5 %fusion.9 = f32[320,32]{1,0:T(8,128)S(1)} fusion(bf16[320,1024]{1,0:T(8,128)(2,1)S(1)} %reshape.30, bf16[1024,32]{0,1:T(8,128)(2,1)} %param.23), kind=kOutput, calls=%fused_computation.32 | convolution fusion | flops 20971520 | bytes 761856 | tf_op jit(solution)/shard_map/dot_general | solution.py:105
  8.7 0.0 copy-done.3
  8.7 0.5 fusion.8
  9.2 0.0 copy-done.2
  9.2 0.1 pad_maximum_fusion
  9.3 0.0 copy-start.4
  9.3 1.0 reshape.31
  10.3 7.5 %all-to-all-start = ((f32[16,20,544]{2,1,0:T(8,128)}), f32[16,20,544]{2,1,0:T(8,128)S(1)}, u32[]{:S(2)}, u32[]{:S(2)}) async-start(f32[16,20,544]{2,1,0:T(8,128)} %reshape.31), calls=%async_computation | async-start | bytes 1966080 | tf_op jit(solution)/shard_map/all_to_all | solution.py:108
  17.8 0.0 copy-done.4
  17.8 1.3 %copy.42.gate_ref = bf16[16,20,1024]{2,1,0:T(8,128)(2,1)} copy(bf16[16,20,1024]{2,0,1:T(8,128)(2,1)S(1)} %copy-done.4) | data formatting | bytes 1310720 | tf_op args[5]
  19.1 0.0 copy-done.5
  19.1 0.6 exponential_negate_fusion.a_ref
  19.7 20.1 %all-to-all-done = f32[16,20,544]{2,1,0:T(8,128)S(1)} async-done(((f32[16,20,544]{2,1,0:T(8,128)}), f32[16,20,544]{2,1,0:T(8,128)S(1)}, u32[]{:S(2)}, u32[]{:S(2)}) %all-to-all-start) | async-done | bytes 696352 | tf_op jit(solution)/shard_map/all_to_all | solution.py:108
  39.8 0.1 reduce_sum.9
  39.8 0.0 copy-start.7
  39.9 0.1 maximum_bitcast_fusion
  39.9 23.5 %all-gather = bf16[16,20,576]{2,1,0:T(8,128)(2,1)S(1)} all-gather(bf16[1,20,576]{2,1,0:T(8,128)(2,1)S(1)} %maximum_bitcast_fusion), channel_id=1, replica_groups=mesh['group'=2,'chan'=16] {'chan'}, dimensions={0}, use_global_device_ids=true | all-gather | bytes 391680 | tf_op jit(solution)/shard_map/all_gather | solution.py:115
  63.4 0.2 reshape.45
  63.6 0.1 fusion.5
  63.7 0.1 copy.45
  63.8 0.1 copy.46
  63.9 0.2 reshape.33
  64.1 0.0 copy-done
  64.1 1.0 compare_select_fusion
  65.2 1.3 %reshape.32.rate_ref = f32[16,20,1024]{2,1,0:T(8,128)} reshape(f32[320,1024]{1,0:T(8,128)S(1)} %compare_select_fusion) | data formatting | bytes 2621440 | tf_op jit(solution)/shard_map/reshape | solution.py:125
  66.5 0.8 copy_bitcast_fusion
  67.2 15.5 %shard_map.149 = bf16[16,36,1024]{2,1,0:T(8,128)(2,1)} custom-call(s32[16]{0:T(128)} %lens_ref.1, s32[16]{0:T(128)} %fmap_ref.1, f32[16,20,1024]{2,1,0:T(8,128)} %reshape.32.rate_ref, bf16[16,20,1024]{2,1,0:T(8,128)(2,1)} %copy-done.2, bf16[16,20,1024]{2,1,0:T(8,128)(2,1)} %copy.42.gate_ref, f32[16,16,20]{2,1,0:T(8,128)} %get-tuple-element.13.b_ref, ...), custom_call_target="tpu_custom_call" | custom-call | tf_op jit(solution)/shard_map/pallas_call | solution.py:72
  82.7 35.6 %all_to_all.23 = bf16[16,36,1024]{2,1,0:T(8,128)(2,1)S(1)} all-to-all(bf16[16,36,1024]{2,1,0:T(8,128)(2,1)} %shard_map.149), channel_id=1, replica_groups=mesh['group'=2,'chan'=16] {'chan'}, dimensions={0} | all-to-all | bytes 2359296 | tf_op jit(solution)/shard_map/all_to_all | solution.py:133
  118.2 0.7 copy.43
  118.9 0.6 all_to_all.20
  119.5 0.9 slice.87
  120.5 1.0 slice_convert_fusion
  (7 shorter events, 0.1 us)
Async XLA Ops:
  0.6 63.5 %copy-start = (bf16[512,1024]{1,0:T(8,128)(2,1)S(1)}, bf16[512,1024]{1,0:T(8,128)(2,1)}, u32[]{:S(2)}) copy-start(bf16[512,1024]{1,0:T(8,128)(2,1)} %param.24) | copy-start | bytes 3145732
  0.6 3.8 %copy-start.1 = (bf16[16,3,1024]{2,0,1:T(8,128)(2,1)S(1)}, bf16[16,3,1024]{2,0,1:T(8,128)(2,1)}, u32[]{:S(2)}) copy-start(bf16[16,3,1024]{2,0,1:T(8,128)(2,1)} %param.15) | copy-start | bytes 294916
  5.3 0.7 copy-start.6
  7.0 2.2 %copy-start.2 = (bf16[16,20,1024]{2,1,0:T(8,128)(2,1)}, bf16[16,20,1024]{2,1,0:T(8,128)(2,1)S(1)}, u32[]{:S(2)}) copy-start(bf16[16,20,1024]{2,1,0:T(8,128)(2,1)S(1)} %multiply_convert_fusion.drive_ref) | copy-start | bytes 1966084
  7.0 1.7 %copy-start.3 = (bf16[1024,512]{1,0:T(8,128)(2,1)S(1)}, bf16[1024,512]{1,0:T(8,128)(2,1)}, u32[]{:S(2)}) copy-start(bf16[1024,512]{1,0:T(8,128)(2,1)} %param.22) | copy-start | bytes 3145732
  9.3 8.5 %copy-start.4 = (bf16[16,20,1024]{2,0,1:T(8,128)(2,1)S(1)}, bf16[16,20,1024]{2,0,1:T(8,128)(2,1)}, u32[]{:S(2)}) copy-start(bf16[16,20,1024]{2,0,1:T(8,128)(2,1)} %param.19) | copy-start | bytes 1966084
  10.3 8.8 %copy-start.5 = (f32[16,1024]{1,0:T(8,128)S(1)}, f32[16,1024]{1,0:T(8,128)}, u32[]{:S(2)}) copy-start(f32[16,1024]{1,0:T(8,128)} %param.26) | copy-start | bytes 196612
  10.3 29.5 %all-to-all-start = ((f32[16,20,544]{2,1,0:T(8,128)}), f32[16,20,544]{2,1,0:T(8,128)S(1)}, u32[]{:S(2)}, u32[]{:S(2)}) async-start(f32[16,20,544]{2,1,0:T(8,128)} %reshape.31), calls=%async_computation | async-start | bytes 1966080 | tf_op jit(solution)/shard_map/all_to_all | solution.py:108
  39.8 24.3 %copy-start.7 = (f32[1024]{0:T(1024)S(1)}, f32[1024]{0:T(1024)}, u32[]{:S(2)}) copy-start(f32[1024]{0:T(1024)} %param.25) | copy-start | bytes 12292

commit v5 on v4

--- a/solution.py
+++ b/solution.py
@@ -103,18 +103,22 @@
     token_rows = driven.reshape(thought_count * positions, width_local)
     low_part = jnp.dot(token_rows, rate_down, preferred_element_type=jnp.float32)
     select_part = jnp.dot(token_rows, selection_weight, preferred_element_type=jnp.float32)
-    partial = jnp.concatenate([low_part, select_part], axis=1)
+    select_high = select_part.astype(jnp.bfloat16)
+    select_low = (select_part - select_high.astype(jnp.float32)).astype(jnp.bfloat16)
+    partial = jnp.concatenate([low_part.astype(jnp.bfloat16), select_high, select_low], axis=1)
     devices = lax.axis_size("chan")
     pieces = lax.all_to_all(
         partial.reshape(devices, -1, partial.shape[1]), "chan", 0, 0, tiled=True
-    )
+    ).astype(jnp.float32)
     reduced = jnp.sum(pieces, axis=0)
     low_mine = reduced[:, :rank].astype(jnp.bfloat16)
-    select_high = reduced[:, rank:].astype(jnp.bfloat16)
-    select_low = (reduced[:, rank:] - select_high.astype(jnp.float32)).astype(jnp.bfloat16)
-    gathered = lax.all_gather(
-        jnp.concatenate([low_mine, select_high, select_low], axis=1), "chan", axis=0, tiled=True
-    )
+    select_sum = reduced[:, rank : rank + 2 * state_size] + reduced[:, rank + 2 * state_size :]
+    select_high = select_sum.astype(jnp.bfloat16)
+    select_low = (select_sum - select_high.astype(jnp.float32)).astype(jnp.bfloat16)
+    mine = jnp.concatenate([low_mine, select_high, select_low], axis=1)
+    gathered = lax.all_to_all(
+        jnp.broadcast_to(mine[None], (devices,) + mine.shape), "chan", 0, 0, tiled=True
+    ).reshape(-1, mine.shape[1])
     rate_low = gathered[:, :rank]
     selection = (
         gathered[:, rank : rank + 2 * state_size].astype(jnp.float32)

time: 123 us -> 109 us (0.89)
  waiting for transfers between devices: 20.1 us -> 11.6 us
  starting transfers between devices: 7.48 us -> 4.39 us
  blocking collectives: 59.1 us -> 57 us
    all_gather x1 -> x0, blocking collectives: 23.5 us -> none  [body(): lax.all_gather(jnp.concatenate([low_mine, select_high, select_low], axis=...]
    all_to_all x0 -> x1, blocking collectives: none -> 20.8 us  [body(): lax.all_to_all(partial.reshape(devices, -1, partial.shape[1]), 'chan', 0,...]
    all_to_all x1, waiting for transfers between devices: 20.1 us -> 11.6 us  [body(): lax.all_to_all(jnp.broadcast_to(mine[None], (devices,) + mine.shape), 'ch...]
    all_to_all x1, starting transfers between devices: 7.48 us -> 4.39 us  [body(): lax.all_to_all(jnp.broadcast_to(mine[None], (devices,) + mine.shape), 'ch...]
    dot_general x1, matrix products: 0.5 us -> 1.74 us  [body(): jnp.dot(token_rows, rate_down, preferred_element_type=jnp.float32)]
    unnamed x21 -> x20, local copies, waits for them, and re-layouts: 3.38 us -> 3.21 us
where the time goes in v5:
time: 109 us; the launch traced here: 108 us
  blocking collectives  57 us (52%)
  Pallas kernels  15.5 us (14%)
  waiting for transfers between devices  11.6 us (11%)
  local copies, waits for them, and re-layouts  11 us (10%)
  other arithmetic  4.86 us (4%)
  starting transfers between devices  4.39 us (4%)
  matrix products  3.08 us (3%)
    all_to_all x1, blocking collectives, body(): lax.all_to_all(packed_local, 'chan', split_axis=0, concat_axis=2, tiled=T...  36.3 us
    all_to_all x1, blocking collectives, body(): lax.all_to_all(partial.reshape(devices, -1, partial.shape[1]), 'chan', 0,...  20.8 us
    pallas_call x1, Pallas kernels, run_scan(): pl.pallas_call(kernel, grid_spec=grid_spec, out_shape=jax.ShapeDtypeStruc...  15.5 us
    all_to_all x1, waiting for transfers between devices, body(): lax.all_to_all(jnp.broadcast_to(mine[None], (devices,) + mine.shape), 'ch...  11.6 us
    all_to_all x1, starting transfers between devices, body(): lax.all_to_all(jnp.broadcast_to(mine[None], (devices,) + mine.shape), 'ch...  4.39 us
    unnamed x20, local copies, waits for them, and re-layouts  3.21 us
  transfers between devices with their start and end apart: 1, of which 1 were waited for; matrix products, arithmetic and copies ran while one was open for 2% of the time, Pallas kernels for 0%

profile of v5, /device:TPU:1, one launch (start us, length us, event | category | flops | bytes accessed | tf_op | source)
XLA Modules:
  0.0 108.2 jit_solution(16743041621511341779)
XLA Ops:
  0.6 0.0 copy-start
  0.6 0.0 copy-start.1
  0.7 0.8 compare_and_fusion
  1.4 0.7 compare_select_fusion.1
  2.1 0.9 fusion.9
  3.0 1.5 %copy.30 = bf16[16,20,1024]{2,1,0:T(8,128)(2,1)S(1)} copy(bf16[16,20,1024]{2,0,1:T(8,128)(2,1)} %param.18) | data formatting | bytes 1310720 | tf_op args[4]
  4.4 0.0 copy-done.1
  4.4 0.8 gather_fusion
  5.3 0.0 copy-start.6
  5.3 0.1 copy_select_fusion
  5.4 0.3 maximum_convert_fusion
  5.7 0.3 copy-done.6
  6.0 1.0 multiply_convert_fusion.drive_ref
  7.0 0.0 copy-start.2
  7.0 0.1 reshape.34
  7.1 0.3 subtract_convert_fusion
  7.5 1.7 %convolution_convert_fusion = bf16[320,512]{1,0:T(8,128)(2,1)S(1)} fusion(bf16[320,1024]{1,0:T(8,128)(2,1)S(1)} %reshape.34, bf16[1024,512]{1,0:T(8,128)(2,1)} %param.22), kind=kOutput, calls=%fused_computation.12 | convolution fusion | flops 335708160 | bytes 2031616 | tf_op jit(solution)/shard_map/dot_general | solution.py:104
  9.2 0.1 copy.32
  9.4 0.1 copy.31
  9.5 0.1 pad_maximum_fusion
  9.6 0.1 reshape.35
  9.7 0.0 copy-start.3
  9.7 20.8 %all_to_all.28 = bf16[16,20,576]{2,1,0:T(8,128)(2,1)S(1)} all-to-all(bf16[16,20,576]{2,1,0:T(8,128)(2,1)S(1)} %reshape.35), channel_id=1, replica_groups=mesh['group'=2,'chan'=16] {'chan'}, dimensions={0} | all-to-all | bytes 737280 | tf_op jit(solution)/shard_map/all_to_all | solution.py:110
  30.5 0.1 convert_reduce_fusion
  30.5 0.0 copy-start.5
  30.6 0.1 subtract_convert_fusion.1
  30.6 0.1 pad_maximum_fusion.1
  30.7 0.8 broadcast_in_dim.23
  31.5 4.4 %all-to-all-start.1 = ((bf16[16,20,576]{2,1,0:T(8,128)(2,1)}), bf16[16,20,576]{2,1,0:T(8,128)(2,1)S(1)}, u32[]{:S(2)}, u32[]{:S(2)}) async-start(bf16[16,20,576]{2,1,0:T(8,128)(2,1)} %broadcast_in_dim.23), calls=%async_computation.1 | async-start | bytes 983040 | tf_op jit(solution)/shard_map/all_to_all | solution.py:119
  35.9 1.3 %copy.37.gate_ref = bf16[16,20,1024]{2,1,0:T(8,128)(2,1)} copy(bf16[16,20,1024]{2,0,1:T(8,128)(2,1)S(1)} %copy-done.3) | data formatting | bytes 1310720 | tf_op args[5]
  37.2 0.0 copy-done.5
  37.2 0.6 exponential_negate_fusion.a_ref
  37.8 11.6 %all-to-all-done.1 = bf16[16,20,576]{2,1,0:T(8,128)(2,1)S(1)} async-done(((bf16[16,20,576]{2,1,0:T(8,128)(2,1)}), bf16[16,20,576]{2,1,0:T(8,128)(2,1)S(1)}, u32[]{:S(2)}, u32[]{:S(2)}) %all-to-all-start.1) | async-done | bytes 368672 | tf_op jit(solution)/shard_map/all_to_all | solution.py:119
  49.4 0.2 reshape.36
  49.6 0.1 fusion.7
  49.7 0.1 copy.39
  49.8 0.1 copy.40
  49.9 0.2 reshape.38
  50.1 0.0 copy-done
  50.1 1.0 compare_select_fusion
  51.1 1.3 %reshape.37.rate_ref = f32[16,20,1024]{2,1,0:T(8,128)} reshape(f32[320,1024]{1,0:T(8,128)S(1)} %compare_select_fusion) | data formatting | bytes 2621440 | tf_op jit(solution)/shard_map/reshape | solution.py:129
  52.4 0.8 copy_bitcast_fusion
  53.2 15.5 %shard_map.149 = bf16[16,36,1024]{2,1,0:T(8,128)(2,1)} custom-call(s32[16]{0:T(128)} %lens_ref.1, s32[16]{0:T(128)} %fmap_ref.1, f32[16,20,1024]{2,1,0:T(8,128)} %reshape.37.rate_ref, bf16[16,20,1024]{2,1,0:T(8,128)(2,1)} %copy-done.2, bf16[16,20,1024]{2,1,0:T(8,128)(2,1)} %copy.37.gate_ref, f32[16,16,20]{2,1,0:T(8,128)} %get-tuple-element.15.b_ref, ...), custom_call_target="tpu_custom_call" | custom-call | tf_op jit(solution)/shard_map/pallas_call | solution.py:72
  68.7 36.3 %all_to_all.29 = bf16[16,36,1024]{2,1,0:T(8,128)(2,1)S(1)} all-to-all(bf16[16,36,1024]{2,1,0:T(8,128)(2,1)} %shard_map.149), channel_id=1, replica_groups=mesh['group'=2,'chan'=16] {'chan'}, dimensions={0} | all-to-all | bytes 2359296 | tf_op jit(solution)/shard_map/all_to_all | solution.py:137
  105.0 0.7 copy.38
  105.6 0.6 all_to_all.24
  106.3 0.9 slice.91
  107.2 1.0 slice_convert_fusion
  (10 shorter events, 0.1 us)
Async XLA Ops:
  0.6 49.4 %copy-start = (bf16[512,1024]{1,0:T(8,128)(2,1)S(1)}, bf16[512,1024]{1,0:T(8,128)(2,1)}, u32[]{:S(2)}) copy-start(bf16[512,1024]{1,0:T(8,128)(2,1)} %param.24) | copy-start | bytes 3145732
  0.6 3.8 %copy-start.1 = (bf16[16,3,1024]{2,0,1:T(8,128)(2,1)S(1)}, bf16[16,3,1024]{2,0,1:T(8,128)(2,1)}, u32[]{:S(2)}) copy-start(bf16[16,3,1024]{2,0,1:T(8,128)(2,1)} %param.15) | copy-start | bytes 294916
  5.3 0.7 copy-start.6
  6.0 1.2 %copy-start.4 = (bf16[1024,32]{0,1:T(8,128)(2,1)S(1)}, bf16[1024,32]{0,1:T(8,128)(2,1)}, u32[]{:S(2)}) copy-start(bf16[1024,32]{0,1:T(8,128)(2,1)} %param.23) | copy-start | bytes 196612
  7.0 2.2 %copy-start.2 = (bf16[16,20,1024]{2,1,0:T(8,128)(2,1)}, bf16[16,20,1024]{2,1,0:T(8,128)(2,1)S(1)}, u32[]{:S(2)}) copy-start(bf16[16,20,1024]{2,1,0:T(8,128)(2,1)S(1)} %multiply_convert_fusion.drive_ref) | copy-start | bytes 1966084
  9.7 26.2 %copy-start.3 = (bf16[16,20,1024]{2,0,1:T(8,128)(2,1)S(1)}, bf16[16,20,1024]{2,0,1:T(8,128)(2,1)}, u32[]{:S(2)}) copy-start(bf16[16,20,1024]{2,0,1:T(8,128)(2,1)} %param.19) | copy-start | bytes 1966084
  30.5 6.6 %copy-start.5 = (f32[16,1024]{1,0:T(8,128)S(1)}, f32[16,1024]{1,0:T(8,128)}, u32[]{:S(2)}) copy-start(f32[16,1024]{1,0:T(8,128)} %param.26) | copy-start | bytes 196612
  31.5 17.9 %all-to-all-start.1 = ((bf16[16,20,576]{2,1,0:T(8,128)(2,1)}), bf16[16,20,576]{2,1,0:T(8,128)(2,1)S(1)}, u32[]{:S(2)}, u32[]{:S(2)}) async-start(bf16[16,20,576]{2,1,0:T(8,128)(2,1)} %broadcast_in_dim.23), calls=%async_computation.1 | async-start | bytes 983040 | tf_op jit(solution)/shard_map/all_to_all | solution.py:119
  37.2 12.9 %copy-start.7 = (f32[1024]{0:T(1024)S(1)}, f32[1024]{0:T(1024)}, u32[]{:S(2)}) copy-start(f32[1024]{0:T(1024)} %param.25) | copy-start | bytes 12292

commit v6 on v5

--- a/solution.py
+++ b/solution.py
@@ -22,62 +22,77 @@
 
 
 def scan_kernel(
-    lens_ref, fmap_ref, rate_ref, drive_ref, gate_ref, b_ref, c_ref, h0_ref, a_ref, skip_ref,
-    packed_ref, r_scr, u_scr, y_scr
+    lens_ref, fmap_ref, gathered_ref, up_ref, bias_ref, drive_ref, gate_ref, b_ref, h0_ref,
+    a_ref, skip_ref, packed_ref, r_scr, u_scr, y_scr
 ):
     t = pl.program_id(0)
-    positions = rate_ref.shape[1]
+    positions = drive_ref.shape[1]
     state_size = h0_ref.shape[1]
+    rank = up_ref.shape[0]
     live = jnp.clip(lens_ref[t] + GEN, 0, positions)
+    row_all = gathered_ref[0]
+    pre = (
+        jnp.dot(row_all[:, :rank], up_ref[...], preferred_element_type=jnp.float32)
+        + bias_ref[...]
+    )
+    rate = jnp.maximum(pre, 0.0) + jnp.log1p(jnp.exp(-jnp.abs(pre)))
+    readout_rows = (
+        row_all[:, rank + state_size : rank + 2 * state_size].astype(jnp.float32)
+        + row_all[:, rank + 3 * state_size :].astype(jnp.float32)
+    )
     inflow = drive_ref[0].astype(jnp.float32)
     alive = lax.broadcasted_iota(jnp.int32, inflow.shape, 0) < live
-    rate = jnp.where(alive, rate_ref[0], 0.0)
+    rate = jnp.where(alive, rate, 0.0)
     r_scr[...] = rate
     u_scr[...] = rate * inflow
     b_all = b_ref[0]
-    c_all = c_ref[0]
     decay = a_ref[...]
     h = h0_ref[0]
     for p in range(positions):
         h = jnp.exp(r_scr[p : p + 1, :] * decay) * h + u_scr[p : p + 1, :] * b_all[:, p : p + 1]
-        y_scr[p : p + 1, :] = jnp.sum(c_all[:, p : p + 1] * h, axis=0, keepdims=True)
+        y_scr[p : p + 1, :] = jnp.dot(
+            readout_rows[p : p + 1, :], h,
+            precision=lax.Precision.HIGHEST, preferred_element_type=jnp.float32,
+        )
     packed_ref[0, :state_size, :] = h.astype(packed_ref.dtype)
     gate = gate_ref[0].astype(jnp.float32)
     result = (y_scr[...] + skip_ref[...] * inflow) * jax.nn.silu(gate)
     packed_ref[0, state_size:, :] = jnp.where(alive, result, 0.0).astype(packed_ref.dtype)
 
 
-def run_scan(judge_lengths, fork_map, step_rate, driven, gate_input, b_t, c_t, parent_state,
-             decay_rate, skip_gain):
+def run_scan(judge_lengths, fork_map, gathered, rate_up, rate_bias, driven, gate_input, b_t,
+             parent_state, decay_rate, skip_gain):
     thought_count, positions, width_local = driven.shape
     state_size = parent_state.shape[1]
-    kernel = scan_kernel
+    rank, columns = rate_up.shape[0], gathered.shape[2]
     row_block = lambda t, lens, fmap: (t, 0, 0)
+    whole = lambda t, lens, fmap: (0, 0)
     grid_spec = pltpu.PrefetchScalarGridSpec(
         num_scalar_prefetch=2,
         grid=(thought_count,),
         in_specs=[
-            pl.BlockSpec((1, positions, width_local), row_block),
+            pl.BlockSpec((1, positions, columns), row_block),
+            pl.BlockSpec((rank, width_local), whole),
+            pl.BlockSpec((1, width_local), whole),
             pl.BlockSpec((1, positions, width_local), row_block),
             pl.BlockSpec((1, positions, width_local), row_block),
             pl.BlockSpec((1, state_size, positions), row_block),
-            pl.BlockSpec((1, state_size, positions), row_block),
             pl.BlockSpec((1, state_size, width_local), lambda t, lens, fmap: (fmap[t], 0, 0)),
-            pl.BlockSpec((state_size, width_local), lambda t, lens, fmap: (0, 0)),
-            pl.BlockSpec((1, width_local), lambda t, lens, fmap: (0, 0)),
+            pl.BlockSpec((state_size, width_local), whole),
+            pl.BlockSpec((1, width_local), whole),
         ],
         out_specs=pl.BlockSpec((1, state_size + positions, width_local), row_block),
         scratch_shapes=[pltpu.VMEM((positions, width_local), jnp.float32)] * 3,
     )
     return pl.pallas_call(
-        kernel,
+        scan_kernel,
         grid_spec=grid_spec,
         out_shape=jax.ShapeDtypeStruct(
             (thought_count, state_size + positions, width_local), jnp.bfloat16
         ),
         compiler_params=pltpu.CompilerParams(dimension_semantics=("arbitrary",)),
-    )(judge_lengths, fork_map, step_rate, driven, gate_input, b_t, c_t, parent_state,
-      decay_rate, skip_gain.reshape(1, width_local))
+    )(judge_lengths, fork_map, gathered, rate_up, rate_bias.reshape(1, width_local), driven,
+      gate_input, b_t, parent_state, decay_rate, skip_gain.reshape(1, width_local))
 
 
 def body(
@@ -118,21 +133,16 @@
     mine = jnp.concatenate([low_mine, select_high, select_low], axis=1)
     gathered = lax.all_to_all(
         jnp.broadcast_to(mine[None], (devices,) + mine.shape), "chan", 0, 0, tiled=True
-    ).reshape(-1, mine.shape[1])
-    rate_low = gathered[:, :rank]
-    selection = (
-        gathered[:, rank : rank + 2 * state_size].astype(jnp.float32)
-        + gathered[:, rank + 2 * state_size :].astype(jnp.float32)
-    ).reshape(thought_count, positions, 2 * state_size)
-    step_rate = jax.nn.softplus(
-        jnp.dot(rate_low, rate_up, preferred_element_type=jnp.float32) + rate_bias[None, :]
-    ).reshape(thought_count, positions, width_local)
-    b_t = jnp.swapaxes(selection[:, :, :state_size], 1, 2)
-    c_t = jnp.swapaxes(selection[:, :, state_size:], 1, 2)
+    )
+    b_t = jnp.swapaxes(
+        gathered[:, :, rank : rank + state_size].astype(jnp.float32)
+        + gathered[:, :, rank + 2 * state_size : rank + 3 * state_size].astype(jnp.float32),
+        1, 2,
+    )
     decay_rate = -jnp.exp(decay_log)
     packed_local = run_scan(
-        judge_lengths, fork_map, step_rate, driven, gate_input, b_t, c_t, parent_state,
-        decay_rate, skip_gain,
+        judge_lengths, fork_map, gathered, rate_up, rate_bias, driven, gate_input, b_t,
+        parent_state, decay_rate, skip_gain,
     )
     packed = lax.all_to_all(packed_local, "chan", split_axis=0, concat_axis=2, tiled=True)
     final_state = packed[:, :state_size].astype(jnp.float32)

time: 109 us -> 123 us (1.13)
  Pallas kernels: 15.5 us -> 33.4 us
  matrix products: 3.08 us -> 0.82 us
  local copies, waits for them, and re-layouts: 11 us -> 8.76 us
    pallas_call x1, Pallas kernels: 15.5 us -> 33.4 us  [run_scan(): pl.pallas_call(scan_kernel, grid_spec=grid_spec, out_shape=jax.ShapeDtype...]
    reshape x3 -> x0, local copies, waits for them, and re-layouts: 1.62 us -> none  [the longest x1 1.3 us: body(): step_rate = jax.nn.softplus(jnp.dot(rate_low, rate_up, preferred_element_...]
    dot_general x1, matrix products: 1.74 us -> 0.5 us  [body(): jnp.dot(token_rows, rate_down, preferred_element_type=jnp.float32)]
where the time goes in v6:
time: 123 us; the launch traced here: 122 us
  blocking collectives  57 us (46%)
  Pallas kernels  33.4 us (27%)
  waiting for transfers between devices  11.6 us (9%)
  local copies, waits for them, and re-layouts  8.76 us (7%)
  other arithmetic  5.51 us (4%)
  starting transfers between devices  4.39 us (4%)
    all_to_all x1, blocking collectives, body(): lax.all_to_all(packed_local, 'chan', split_axis=0, concat_axis=2, tiled=T...  36.3 us
    pallas_call x1, Pallas kernels, run_scan(): pl.pallas_call(scan_kernel, grid_spec=grid_spec, out_shape=jax.ShapeDtype...  33.4 us
    all_to_all x1, blocking collectives, body(): lax.all_to_all(partial.reshape(devices, -1, partial.shape[1]), 'chan', 0,...  20.8 us
    all_to_all x1, waiting for transfers between devices, body(): lax.all_to_all(jnp.broadcast_to(mine[None], (devices,) + mine.shape), 'ch...  11.6 us
    all_to_all x1, starting transfers between devices, body(): lax.all_to_all(jnp.broadcast_to(mine[None], (devices,) + mine.shape), 'ch...  4.39 us
    unnamed x20, local copies, waits for them, and re-layouts  3.43 us
  transfers between devices with their start and end apart: 1, of which 1 were waited for; matrix products, arithmetic and copies ran while one was open for 2% of the time, Pallas kernels for 0%

profile of v6, /device:TPU:1, one launch (start us, length us, event | category | flops | bytes accessed | tf_op | source)
XLA Modules:
  0.0 122.3 jit_solution(17332641757774960788)
XLA Ops:
  0.6 0.0 copy-start
  0.6 0.0 copy-start.1
  0.7 0.8 compare_and_fusion
  1.4 0.7 compare_select_fusion
  2.1 0.9 fusion.7
  3.0 1.5 %copy.37 = bf16[16,20,1024]{2,1,0:T(8,128)(2,1)S(1)} copy(bf16[16,20,1024]{2,0,1:T(8,128)(2,1)} %param.18) | data formatting | bytes 1310720 | tf_op args[4]
  4.4 0.0 copy-done.1
  4.4 0.8 gather_fusion
  5.3 0.0 copy-start.7
  5.3 0.1 copy_select_fusion
  5.4 0.3 maximum_convert_fusion
  5.7 0.3 copy-done.7
  6.0 1.0 multiply_convert_fusion.drive_ref
  7.0 0.0 copy-start.2
  7.0 0.1 reshape.27
  7.1 0.0 copy-done.5
  7.1 0.3 subtract_convert_fusion
  7.5 0.0 copy-done
  7.5 0.5 convolution_convert_fusion
  8.0 0.0 copy-done.2
  8.0 0.1 copy.39
  8.1 0.1 copy.38
  8.3 0.1 pad_maximum_fusion
  8.4 0.1 reshape.28
  8.5 0.0 copy-start.4
  8.5 20.8 %all_to_all.28 = bf16[16,20,576]{2,1,0:T(8,128)(2,1)S(1)} all-to-all(bf16[16,20,576]{2,1,0:T(8,128)(2,1)S(1)} %reshape.28), channel_id=1, replica_groups=mesh['group'=2,'chan'=16] {'chan'}, dimensions={0} | all-to-all | bytes 737280 | tf_op jit(solution)/shard_map/all_to_all | solution.py:125
  29.2 0.1 convert_reduce_fusion
  29.3 0.0 copy-start.6
  29.3 0.1 subtract_convert_fusion.1
  29.4 0.1 pad_maximum_fusion.1
  29.5 0.8 broadcast_in_dim.22
  30.3 4.4 %all-to-all-start.1 = ((bf16[16,20,576]{2,1,0:T(8,128)(2,1)}), bf16[16,20,576]{2,1,0:T(8,128)(2,1)S(1)}, u32[]{:S(2)}, u32[]{:S(2)}) async-start(bf16[16,20,576]{2,1,0:T(8,128)(2,1)} %broadcast_in_dim.22), calls=%async_computation.1 | async-start | bytes 983040 | tf_op jit(solution)/shard_map/all_to_all | solution.py:134
  34.7 0.0 copy-done.4
  34.7 1.3 %copy.42.gate_ref = bf16[16,20,1024]{2,1,0:T(8,128)(2,1)} copy(bf16[16,20,1024]{2,0,1:T(8,128)(2,1)S(1)} %copy-done.4) | data formatting | bytes 1310720 | tf_op args[5]
  36.0 0.0 copy-done.6
  36.0 0.6 exponential_negate_fusion.a_ref
  36.6 11.6 %all-to-all-done.1.gathered_ref = bf16[16,20,576]{2,1,0:T(8,128)(2,1)S(1)} async-done(((bf16[16,20,576]{2,1,0:T(8,128)(2,1)}), bf16[16,20,576]{2,1,0:T(8,128)(2,1)S(1)}, u32[]{:S(2)}, u32[]{:S(2)}) %all-to-all-start.1) | async-done | bytes 368672 | tf_op jit(solution)/shard_map/all_to_all | solution.py:134
  48.2 0.1 fusion.6
  48.3 0.2 copy.44
  48.5 0.2 copy.45
  48.7 0.7 add_bitcast_fusion.b_ref
  49.3 0.0 copy-done.3
  49.3 33.4 %shard_map.149 = bf16[16,36,1024]{2,1,0:T(8,128)(2,1)} custom-call(s32[16]{0:T(128)} %lens_ref.1, s32[16]{0:T(128)} %fmap_ref.1, bf16[16,20,576]{2,1,0:T(8,128)(2,1)} %copy-done.3, bf16[512,1024]{1,0:T(8,128)(2,1)} %up_ref.1, f32[1,1024]{1,0:T(1,128)} %bitcast.22, bf16[16,20,1024]{2,1,0:T(8,128)(2,1)} %copy-done.2, bf16[16,20,1024]{2,1,0:T(8,128)(2,1)} %copy.42.gate_ref, ...), custom_call_target="tpu_custom_call" | custom-call | tf_op jit(solution)/shard_map/pallas_call | solution.py:87
  82.8 36.3 %all_to_all.29 = bf16[16,36,1024]{2,1,0:T(8,128)(2,1)S(1)} all-to-all(bf16[16,36,1024]{2,1,0:T(8,128)(2,1)} %shard_map.149), channel_id=1, replica_groups=mesh['group'=2,'chan'=16] {'chan'}, dimensions={0} | all-to-all | bytes 2359296 | tf_op jit(solution)/shard_map/all_to_all | solution.py:147
  119.0 0.7 copy.43
  119.7 0.6 all_to_all.24
  120.3 0.9 slice.76
  121.2 1.0 slice_convert_fusion
  (4 shorter events, 0.0 us)
Async XLA Ops:
  0.6 6.8 %copy-start = (bf16[1024,512]{1,0:T(8,128)(2,1)S(1)}, bf16[1024,512]{1,0:T(8,128)(2,1)}, u32[]{:S(2)}) copy-start(bf16[1024,512]{1,0:T(8,128)(2,1)} %param.22) | copy-start | bytes 3145732
  0.6 3.8 %copy-start.1 = (bf16[16,3,1024]{2,0,1:T(8,128)(2,1)S(1)}, bf16[16,3,1024]{2,0,1:T(8,128)(2,1)}, u32[]{:S(2)}) copy-start(bf16[16,3,1024]{2,0,1:T(8,128)(2,1)} %param.15) | copy-start | bytes 294916
  5.3 0.7 copy-start.7
  6.0 1.2 copy-start.5
  7.0 1.0 copy-start.2
  8.5 26.3 %copy-start.4 = (bf16[16,20,1024]{2,0,1:T(8,128)(2,1)S(1)}, bf16[16,20,1024]{2,0,1:T(8,128)(2,1)}, u32[]{:S(2)}) copy-start(bf16[16,20,1024]{2,0,1:T(8,128)(2,1)} %param.19) | copy-start | bytes 1966084
  29.3 6.7 %copy-start.6 = (f32[16,1024]{1,0:T(8,128)S(1)}, f32[16,1024]{1,0:T(8,128)}, u32[]{:S(2)}) copy-start(f32[16,1024]{1,0:T(8,128)} %param.26) | copy-start | bytes 196612
  30.3 17.9 %all-to-all-start.1 = ((bf16[16,20,576]{2,1,0:T(8,128)(2,1)}), bf16[16,20,576]{2,1,0:T(8,128)(2,1)S(1)}, u32[]{:S(2)}, u32[]{:S(2)}) async-start(bf16[16,20,576]{2,1,0:T(8,128)(2,1)} %broadcast_in_dim.22), calls=%async_computation.1 | async-start | bytes 983040 | tf_op jit(solution)/shard_map/all_to_all | solution.py:134
  48.2 1.1 copy-start.3

commit v7 on v5

--- a/solution.py
+++ b/solution.py
@@ -10,7 +10,7 @@
 
 def convolve(parent_conv, fork_map, mixer_input, conv_weight, conv_bias):
     positions = mixer_input.shape[1]
-    start_conv = jnp.take(parent_conv, fork_map, axis=0)
+    start_conv = jnp.take(parent_conv, fork_map, axis=0, mode="clip")
     padded = jnp.concatenate([start_conv, mixer_input], axis=1).astype(jnp.float32)
     tap_weights = conv_weight.astype(jnp.float32)
     summed = conv_bias[None, None, :] + tap_weights[0][None, None, :] * padded[:, 0:positions, :]
@@ -22,62 +22,79 @@
 
 
 def scan_kernel(
-    lens_ref, fmap_ref, rate_ref, drive_ref, gate_ref, b_ref, c_ref, h0_ref, a_ref, skip_ref,
-    packed_ref, r_scr, u_scr, y_scr
+    lens_ref, fmap_ref, rate_ref, drive_ref, gate_ref, b_ref, c_ref, *rest
 ):
-    t = pl.program_id(0)
+    pair = len(rest) - 6
+    h0_refs, (a_ref, skip_ref, packed_ref, r_scr, u_scr, y_scr) = rest[:pair], rest[pair:]
     positions = rate_ref.shape[1]
-    state_size = h0_ref.shape[1]
-    live = jnp.clip(lens_ref[t] + GEN, 0, positions)
-    inflow = drive_ref[0].astype(jnp.float32)
-    alive = lax.broadcasted_iota(jnp.int32, inflow.shape, 0) < live
-    rate = jnp.where(alive, rate_ref[0], 0.0)
-    r_scr[...] = rate
-    u_scr[...] = rate * inflow
-    b_all = b_ref[0]
-    c_all = c_ref[0]
+    state_size = h0_refs[0].shape[1]
     decay = a_ref[...]
-    h = h0_ref[0]
+    states, lives = [], []
+    for k in range(pair):
+        live = jnp.clip(lens_ref[pl.program_id(0) * pair + k] + GEN, 0, positions)
+        inflow = drive_ref[k].astype(jnp.float32)
+        alive = lax.broadcasted_iota(jnp.int32, inflow.shape, 0) < live
+        rate = jnp.where(alive, rate_ref[k], 0.0)
+        r_scr[k] = rate
+        u_scr[k] = rate * inflow
+        states.append(h0_refs[k][0])
+        lives.append(alive)
     for p in range(positions):
-        h = jnp.exp(r_scr[p : p + 1, :] * decay) * h + u_scr[p : p + 1, :] * b_all[:, p : p + 1]
-        y_scr[p : p + 1, :] = jnp.sum(c_all[:, p : p + 1] * h, axis=0, keepdims=True)
-    packed_ref[0, :state_size, :] = h.astype(packed_ref.dtype)
-    gate = gate_ref[0].astype(jnp.float32)
-    result = (y_scr[...] + skip_ref[...] * inflow) * jax.nn.silu(gate)
-    packed_ref[0, state_size:, :] = jnp.where(alive, result, 0.0).astype(packed_ref.dtype)
+        for k in range(pair):
+            b_col = b_ref[k][:, p : p + 1]
+            c_col = c_ref[k][:, p : p + 1]
+            h = states[k]
+            h = jnp.exp(r_scr[k, p : p + 1, :] * decay) * h + u_scr[k, p : p + 1, :] * b_col
+            y_scr[k, p : p + 1, :] = jnp.sum(c_col * h, axis=0, keepdims=True)
+            states[k] = h
+    for k in range(pair):
+        packed_ref[k, :state_size, :] = states[k].astype(packed_ref.dtype)
+        inflow = drive_ref[k].astype(jnp.float32)
+        gate = gate_ref[k].astype(jnp.float32)
+        result = (y_scr[k] + skip_ref[...] * inflow) * jax.nn.silu(gate)
+        packed_ref[k, state_size:, :] = jnp.where(lives[k], result, 0.0).astype(packed_ref.dtype)
 
 
 def run_scan(judge_lengths, fork_map, step_rate, driven, gate_input, b_t, c_t, parent_state,
              decay_rate, skip_gain):
     thought_count, positions, width_local = driven.shape
     state_size = parent_state.shape[1]
-    kernel = scan_kernel
+    pair = 2 if thought_count % 2 == 0 else 1
     row_block = lambda t, lens, fmap: (t, 0, 0)
+    whole = lambda t, lens, fmap: (0, 0)
+
+    def state_block(k):
+        return pl.BlockSpec(
+            (1, state_size, width_local), lambda t, lens, fmap: (fmap[t * pair + k], 0, 0)
+        )
+
     grid_spec = pltpu.PrefetchScalarGridSpec(
         num_scalar_prefetch=2,
-        grid=(thought_count,),
+        grid=(thought_count // pair,),
         in_specs=[
-            pl.BlockSpec((1, positions, width_local), row_block),
-            pl.BlockSpec((1, positions, width_local), row_block),
-            pl.BlockSpec((1, positions, width_local), row_block),
-            pl.BlockSpec((1, state_size, positions), row_block),
-            pl.BlockSpec((1, state_size, positions), row_block),
-            pl.BlockSpec((1, state_size, width_local), lambda t, lens, fmap: (fmap[t], 0, 0)),
-            pl.BlockSpec((state_size, width_local), lambda t, lens, fmap: (0, 0)),
-            pl.BlockSpec((1, width_local), lambda t, lens, fmap: (0, 0)),
+            pl.BlockSpec((pair, positions, width_local), row_block),
+            pl.BlockSpec((pair, positions, width_local), row_block),
+            pl.BlockSpec((pair, positions, width_local), row_block),
+            pl.BlockSpec((pair, state_size, positions), row_block),
+            pl.BlockSpec((pair, state_size, positions), row_block),
+        ]
+        + [state_block(k) for k in range(pair)]
+        + [
+            pl.BlockSpec((state_size, width_local), whole),
+            pl.BlockSpec((1, width_local), whole),
         ],
-        out_specs=pl.BlockSpec((1, state_size + positions, width_local), row_block),
-        scratch_shapes=[pltpu.VMEM((positions, width_local), jnp.float32)] * 3,
+        out_specs=pl.BlockSpec((pair, state_size + positions, width_local), row_block),
+        scratch_shapes=[pltpu.VMEM((pair, positions, width_local), jnp.float32)] * 3,
     )
     return pl.pallas_call(
-        kernel,
+        scan_kernel,
         grid_spec=grid_spec,
         out_shape=jax.ShapeDtypeStruct(
             (thought_count, state_size + positions, width_local), jnp.bfloat16
         ),
         compiler_params=pltpu.CompilerParams(dimension_semantics=("arbitrary",)),
-    )(judge_lengths, fork_map, step_rate, driven, gate_input, b_t, c_t, parent_state,
-      decay_rate, skip_gain.reshape(1, width_local))
+    )(judge_lengths, fork_map, step_rate, driven, gate_input, b_t, c_t,
+      *([parent_state] * pair), decay_rate, skip_gain.reshape(1, width_local))
 
 
 def body(

time: 109 us -> 106 us (0.972)
  Pallas kernels: 15.5 us -> 13.2 us
    pallas_call x1, Pallas kernels: 15.5 us -> 13.2 us  [run_scan(): pl.pallas_call(scan_kernel, grid_spec=grid_spec, out_shape=jax.ShapeDtype...]
where the time goes in v7:
time: 106 us; the launch traced here: 105 us
  blocking collectives  57 us (54%)
  Pallas kernels  13.2 us (12%)
  waiting for transfers between devices  11.6 us (11%)
  local copies, waits for them, and re-layouts  11 us (10%)
  starting transfers between devices  4.39 us (4%)
  other arithmetic  4.08 us (4%)
  matrix products  3.08 us (3%)
    all_to_all x1, blocking collectives, body(): lax.all_to_all(packed_local, 'chan', split_axis=0, concat_axis=2, tiled=T...  36.3 us
    all_to_all x1, blocking collectives, body(): lax.all_to_all(partial.reshape(devices, -1, partial.shape[1]), 'chan', 0,...  20.8 us
    pallas_call x1, Pallas kernels, run_scan(): pl.pallas_call(scan_kernel, grid_spec=grid_spec, out_shape=jax.ShapeDtype...  13.2 us
    all_to_all x1, waiting for transfers between devices, body(): lax.all_to_all(jnp.broadcast_to(mine[None], (devices,) + mine.shape), 'ch...  11.6 us
    all_to_all x1, starting transfers between devices, body(): lax.all_to_all(jnp.broadcast_to(mine[None], (devices,) + mine.shape), 'ch...  4.39 us
    unnamed x20, local copies, waits for them, and re-layouts  2.25 us
  transfers between devices with their start and end apart: 1, of which 1 were waited for; matrix products, arithmetic and copies ran while one was open for 2% of the time, Pallas kernels for 0%

profile of v7, /device:TPU:1, one launch (start us, length us, event | category | flops | bytes accessed | tf_op | source)
XLA Modules:
  0.0 105.1 jit_solution(6702604062544544621)
XLA Ops:
  0.6 0.0 copy-start
  0.6 0.0 copy-start.2
  0.7 0.8 pad_clamp_fusion
  1.4 0.9 fusion.9
  2.3 1.7 %gather_fusion = bf16[16,3,1024]{2,0,1:T(8,128)(2,1)S(1)} fusion(bf16[16,3,1024]{2,0,1:T(8,128)(2,1)} %param.15, s32[1024]{0:T(1024)S(1)} %pad_clamp_fusion), kind=kCustom, calls=%fused_computation | custom fusion | bytes 196672 | tf_op jit(solution)/shard_map/jit(_take)/gather | solution.py:13
  4.0 0.1 copy.29
  4.1 0.0 copy-done.2
  4.2 0.4 copy.30
  4.5 0.0 copy-start.6
  4.5 0.3 maximum_convert_fusion
  4.8 0.4 copy-done.6
  5.2 1.0 multiply_convert_fusion.drive_ref
  6.2 0.0 copy-start.1
  6.2 0.1 reshape.29
  6.4 0.3 subtract_convert_fusion
  6.7 1.7 %convolution_convert_fusion = bf16[320,512]{1,0:T(8,128)(2,1)S(1)} fusion(bf16[320,1024]{1,0:T(8,128)(2,1)S(1)} %reshape.29, bf16[1024,512]{1,0:T(8,128)(2,1)} %param.22), kind=kOutput, calls=%fused_computation.12 | convolution fusion | flops 335708160 | bytes 2031616 | tf_op jit(solution)/shard_map/dot_general | solution.py:121
  8.5 0.1 copy.32
  8.6 0.1 copy.31
  8.7 0.1 pad_maximum_fusion
  8.8 0.1 reshape.30
  8.9 0.0 copy-start.3
  8.9 20.8 %all_to_all.28 = bf16[16,20,576]{2,1,0:T(8,128)(2,1)S(1)} all-to-all(bf16[16,20,576]{2,1,0:T(8,128)(2,1)S(1)} %reshape.30), channel_id=1, replica_groups=mesh['group'=2,'chan'=16] {'chan'}, dimensions={0} | all-to-all | bytes 737280 | tf_op jit(solution)/shard_map/all_to_all | solution.py:127
  29.7 0.1 convert_reduce_fusion
  29.8 0.0 copy-start.5
  29.8 0.1 subtract_convert_fusion.1
  29.9 0.1 pad_maximum_fusion.1
  30.0 0.8 broadcast_in_dim.7
  30.8 4.4 %all-to-all-start.1 = ((bf16[16,20,576]{2,1,0:T(8,128)(2,1)}), bf16[16,20,576]{2,1,0:T(8,128)(2,1)S(1)}, u32[]{:S(2)}, u32[]{:S(2)}) async-start(bf16[16,20,576]{2,1,0:T(8,128)(2,1)} %broadcast_in_dim.7), calls=%async_computation.1 | async-start | bytes 983040 | tf_op jit(solution)/shard_map/all_to_all | solution.py:136
  35.2 1.3 %copy.37.gate_ref = bf16[16,20,1024]{2,1,0:T(8,128)(2,1)} copy(bf16[16,20,1024]{2,0,1:T(8,128)(2,1)S(1)} %copy-done.3) | data formatting | bytes 1310720 | tf_op args[5]
  36.4 0.0 copy-done.5
  36.4 0.6 exponential_negate_fusion.rest_2_
  37.1 11.6 %all-to-all-done.1 = bf16[16,20,576]{2,1,0:T(8,128)(2,1)S(1)} async-done(((bf16[16,20,576]{2,1,0:T(8,128)(2,1)}), bf16[16,20,576]{2,1,0:T(8,128)(2,1)S(1)}, u32[]{:S(2)}, u32[]{:S(2)}) %all-to-all-start.1) | async-done | bytes 368672 | tf_op jit(solution)/shard_map/all_to_all | solution.py:136
  48.7 0.2 reshape.31
  48.8 0.1 fusion.7
  48.9 0.1 copy.39
  49.0 0.1 copy.40
  49.1 0.2 reshape.33
  49.3 0.0 copy-done
  49.3 0.0 copy-done.7
  49.3 1.0 compare_select_fusion
  50.4 1.3 %reshape.32.rate_ref = f32[16,20,1024]{2,1,0:T(8,128)} reshape(f32[320,1024]{1,0:T(8,128)S(1)} %compare_select_fusion) | data formatting | bytes 2621440 | tf_op jit(solution)/shard_map/reshape | solution.py:146
  51.7 0.8 copy_bitcast_fusion
  52.5 13.2 %shard_map.149 = bf16[16,36,1024]{2,1,0:T(8,128)(2,1)} custom-call(s32[16]{0:T(128)} %lens_ref.1, s32[16]{0:T(128)} %fmap_ref.1, f32[16,20,1024]{2,1,0:T(8,128)} %reshape.32.rate_ref, bf16[16,20,1024]{2,1,0:T(8,128)(2,1)} %copy-done.1, bf16[16,20,1024]{2,1,0:T(8,128)(2,1)} %copy.37.gate_ref, f32[16,16,20]{2,1,0:T(8,128)} %get-tuple-element.15.b_ref, ...), custom_call_target="tpu_custom_call" | custom-call | tf_op jit(solution)/shard_map/pallas_call | solution.py:89
  65.6 36.3 %all_to_all.29 = bf16[16,36,1024]{2,1,0:T(8,128)(2,1)S(1)} all-to-all(bf16[16,36,1024]{2,1,0:T(8,128)(2,1)} %shard_map.149), channel_id=1, replica_groups=mesh['group'=2,'chan'=16] {'chan'}, dimensions={0} | all-to-all | bytes 2359296 | tf_op jit(solution)/shard_map/all_to_all | solution.py:154
  101.9 0.7 copy.38
  102.5 0.6 all_to_all.24
  103.2 0.9 slice.91
  104.1 1.0 slice_convert_fusion
  (8 shorter events, 0.0 us)
Async XLA Ops:
  0.6 48.7 %copy-start = (bf16[512,1024]{1,0:T(8,128)(2,1)S(1)}, bf16[512,1024]{1,0:T(8,128)(2,1)}, u32[]{:S(2)}) copy-start(bf16[512,1024]{1,0:T(8,128)(2,1)} %param.24) | copy-start | bytes 3145732
  0.6 3.5 %copy-start.2 = (bf16[16,20,1024]{2,0,1:T(8,128)(2,1)S(1)}, bf16[16,20,1024]{2,0,1:T(8,128)(2,1)}, u32[]{:S(2)}) copy-start(bf16[16,20,1024]{2,0,1:T(8,128)(2,1)} %param.18) | copy-start | bytes 1966084
  4.5 0.7 copy-start.6
  5.2 1.2 %copy-start.4 = (bf16[1024,32]{0,1:T(8,128)(2,1)S(1)}, bf16[1024,32]{0,1:T(8,128)(2,1)}, u32[]{:S(2)}) copy-start(bf16[1024,32]{0,1:T(8,128)(2,1)} %param.23) | copy-start | bytes 196612
  6.2 2.2 %copy-start.1 = (bf16[16,20,1024]{2,1,0:T(8,128)(2,1)}, bf16[16,20,1024]{2,1,0:T(8,128)(2,1)S(1)}, u32[]{:S(2)}) copy-start(bf16[16,20,1024]{2,1,0:T(8,128)(2,1)S(1)} %multiply_convert_fusion.drive_ref) | copy-start | bytes 1966084
  8.9 26.2 %copy-start.3 = (bf16[16,20,1024]{2,0,1:T(8,128)(2,1)S(1)}, bf16[16,20,1024]{2,0,1:T(8,128)(2,1)}, u32[]{:S(2)}) copy-start(bf16[16,20,1024]{2,0,1:T(8,128)(2,1)} %param.19) | copy-start | bytes 1966084
  29.8 6.6 %copy-start.5 = (f32[16,1024]{1,0:T(8,128)S(1)}, f32[16,1024]{1,0:T(8,128)}, u32[]{:S(2)}) copy-start(f32[16,1024]{1,0:T(8,128)} %param.26) | copy-start | bytes 196612
  30.8 17.9 %all-to-all-start.1 = ((bf16[16,20,576]{2,1,0:T(8,128)(2,1)}), bf16[16,20,576]{2,1,0:T(8,128)(2,1)S(1)}, u32[]{:S(2)}, u32[]{:S(2)}) async-start(bf16[16,20,576]{2,1,0:T(8,128)(2,1)} %broadcast_in_dim.7), calls=%async_computation.1 | async-start | bytes 983040 | tf_op jit(solution)/shard_map/all_to_all | solution.py:136
  36.4 12.9 %copy-start.7 = (f32[1024]{0:T(1024)S(1)}, f32[1024]{0:T(1024)}, u32[]{:S(2)}) copy-start(f32[1024]{0:T(1024)} %param.25) | copy-start | bytes 12292

commit v8 on v7

--- a/solution.py
+++ b/solution.py
@@ -59,7 +59,7 @@
              decay_rate, skip_gain):
     thought_count, positions, width_local = driven.shape
     state_size = parent_state.shape[1]
-    pair = 2 if thought_count % 2 == 0 else 1
+    pair = 4 if thought_count % 4 == 0 else 1
     row_block = lambda t, lens, fmap: (t, 0, 0)
     whole = lambda t, lens, fmap: (0, 0)
 

time: 106 us -> 106 us (level)
  no operation moved by 1% of the time
where the time goes in v8:
time: 106 us; the launch traced here: 105 us
  blocking collectives  57 us (54%)
  Pallas kernels  13.2 us (12%)
  waiting for transfers between devices  11.6 us (11%)
  local copies, waits for them, and re-layouts  11 us (10%)
  starting transfers between devices  4.39 us (4%)
  other arithmetic  4.08 us (4%)
  matrix products  3.08 us (3%)
    all_to_all x1, blocking collectives, body(): lax.all_to_all(packed_local, 'chan', split_axis=0, concat_axis=2, tiled=T...  36.3 us
    all_to_all x1, blocking collectives, body(): lax.all_to_all(partial.reshape(devices, -1, partial.shape[1]), 'chan', 0,...  20.8 us
    pallas_call x1, Pallas kernels, run_scan(): pl.pallas_call(scan_kernel, grid_spec=grid_spec, out_shape=jax.ShapeDtype...  13.2 us
    all_to_all x1, waiting for transfers between devices, body(): lax.all_to_all(jnp.broadcast_to(mine[None], (devices,) + mine.shape), 'ch...  11.6 us
    all_to_all x1, starting transfers between devices, body(): lax.all_to_all(jnp.broadcast_to(mine[None], (devices,) + mine.shape), 'ch...  4.39 us
    unnamed x20, local copies, waits for them, and re-layouts  2.25 us
  transfers between devices with their start and end apart: 1, of which 1 were waited for; matrix products, arithmetic and copies ran while one was open for 2% of the time, Pallas kernels for 0%

profile of v8, /device:TPU:1, one launch (start us, length us, event | category | flops | bytes accessed | tf_op | source)
XLA Modules:
  0.0 105.2 jit_solution(14215807823648071291)
XLA Ops:
  0.6 0.0 copy-start
  0.6 0.0 copy-start.2
  0.7 0.8 pad_clamp_fusion
  1.4 0.9 fusion.9
  2.3 1.7 %gather_fusion = bf16[16,3,1024]{2,0,1:T(8,128)(2,1)S(1)} fusion(bf16[16,3,1024]{2,0,1:T(8,128)(2,1)} %param.15, s32[1024]{0:T(1024)S(1)} %pad_clamp_fusion), kind=kCustom, calls=%fused_computation | custom fusion | bytes 196672 | tf_op jit(solution)/shard_map/jit(_take)/gather | solution.py:13
  4.0 0.1 copy.29
  4.1 0.0 copy-done.2
  4.2 0.4 copy.30
  4.5 0.0 copy-start.6
  4.5 0.3 maximum_convert_fusion
  4.8 0.4 copy-done.6
  5.2 1.0 multiply_convert_fusion.drive_ref
  6.2 0.0 copy-start.1
  6.2 0.1 reshape.29
  6.4 0.3 subtract_convert_fusion
  6.7 1.7 %convolution_convert_fusion = bf16[320,512]{1,0:T(8,128)(2,1)S(1)} fusion(bf16[320,1024]{1,0:T(8,128)(2,1)S(1)} %reshape.29, bf16[1024,512]{1,0:T(8,128)(2,1)} %param.22), kind=kOutput, calls=%fused_computation.12 | convolution fusion | flops 335708160 | bytes 2031616 | tf_op jit(solution)/shard_map/dot_general | solution.py:121
  8.5 0.1 copy.32
  8.6 0.1 copy.31
  8.7 0.1 pad_maximum_fusion
  8.8 0.1 reshape.30
  8.9 0.0 copy-start.3
  8.9 20.8 %all_to_all.28 = bf16[16,20,576]{2,1,0:T(8,128)(2,1)S(1)} all-to-all(bf16[16,20,576]{2,1,0:T(8,128)(2,1)S(1)} %reshape.30), channel_id=1, replica_groups=mesh['group'=2,'chan'=16] {'chan'}, dimensions={0} | all-to-all | bytes 737280 | tf_op jit(solution)/shard_map/all_to_all | solution.py:127
  29.7 0.1 convert_reduce_fusion
  29.8 0.0 copy-start.5
  29.8 0.1 subtract_convert_fusion.1
  29.9 0.1 pad_maximum_fusion.1
  30.0 0.8 broadcast_in_dim.7
  30.8 4.4 %all-to-all-start.1 = ((bf16[16,20,576]{2,1,0:T(8,128)(2,1)}), bf16[16,20,576]{2,1,0:T(8,128)(2,1)S(1)}, u32[]{:S(2)}, u32[]{:S(2)}) async-start(bf16[16,20,576]{2,1,0:T(8,128)(2,1)} %broadcast_in_dim.7), calls=%async_computation.1 | async-start | bytes 983040 | tf_op jit(solution)/shard_map/all_to_all | solution.py:136
  35.2 1.3 %copy.37.gate_ref = bf16[16,20,1024]{2,1,0:T(8,128)(2,1)} copy(bf16[16,20,1024]{2,0,1:T(8,128)(2,1)S(1)} %copy-done.3) | data formatting | bytes 1310720 | tf_op args[5]
  36.4 0.0 copy-done.5
  36.4 0.6 exponential_negate_fusion.rest_4_
  37.1 11.6 %all-to-all-done.1 = bf16[16,20,576]{2,1,0:T(8,128)(2,1)S(1)} async-done(((bf16[16,20,576]{2,1,0:T(8,128)(2,1)}), bf16[16,20,576]{2,1,0:T(8,128)(2,1)S(1)}, u32[]{:S(2)}, u32[]{:S(2)}) %all-to-all-start.1) | async-done | bytes 368672 | tf_op jit(solution)/shard_map/all_to_all | solution.py:136
  48.7 0.2 reshape.31
  48.8 0.1 fusion.7
  48.9 0.1 copy.39
  49.0 0.1 copy.40
  49.1 0.2 reshape.33
  49.3 0.0 copy-done
  49.3 0.0 copy-done.7
  49.3 1.0 compare_select_fusion
  50.4 1.3 %reshape.32.rate_ref = f32[16,20,1024]{2,1,0:T(8,128)} reshape(f32[320,1024]{1,0:T(8,128)S(1)} %compare_select_fusion) | data formatting | bytes 2621440 | tf_op jit(solution)/shard_map/reshape | solution.py:146
  51.7 0.8 copy_bitcast_fusion
  52.5 13.2 %shard_map.149 = bf16[16,36,1024]{2,1,0:T(8,128)(2,1)} custom-call(s32[16]{0:T(128)} %lens_ref.1, s32[16]{0:T(128)} %fmap_ref.1, f32[16,20,1024]{2,1,0:T(8,128)} %reshape.32.rate_ref, bf16[16,20,1024]{2,1,0:T(8,128)(2,1)} %copy-done.1, bf16[16,20,1024]{2,1,0:T(8,128)(2,1)} %copy.37.gate_ref, f32[16,16,20]{2,1,0:T(8,128)} %get-tuple-element.15.b_ref, ...), custom_call_target="tpu_custom_call" | custom-call | tf_op jit(solution)/shard_map/pallas_call | solution.py:89
  65.7 36.3 %all_to_all.29 = bf16[16,36,1024]{2,1,0:T(8,128)(2,1)S(1)} all-to-all(bf16[16,36,1024]{2,1,0:T(8,128)(2,1)} %shard_map.149), channel_id=1, replica_groups=mesh['group'=2,'chan'=16] {'chan'}, dimensions={0} | all-to-all | bytes 2359296 | tf_op jit(solution)/shard_map/all_to_all | solution.py:154
  101.9 0.7 copy.38
  102.6 0.6 all_to_all.24
  103.2 0.9 slice.91
  104.2 1.0 slice_convert_fusion
  (8 shorter events, 0.0 us)
Async XLA Ops:
  0.6 48.7 %copy-start = (bf16[512,1024]{1,0:T(8,128)(2,1)S(1)}, bf16[512,1024]{1,0:T(8,128)(2,1)}, u32[]{:S(2)}) copy-start(bf16[512,1024]{1,0:T(8,128)(2,1)} %param.24) | copy-start | bytes 3145732
  0.6 3.5 %copy-start.2 = (bf16[16,20,1024]{2,0,1:T(8,128)(2,1)S(1)}, bf16[16,20,1024]{2,0,1:T(8,128)(2,1)}, u32[]{:S(2)}) copy-start(bf16[16,20,1024]{2,0,1:T(8,128)(2,1)} %param.18) | copy-start | bytes 1966084
  4.5 0.7 copy-start.6
  5.2 1.2 %copy-start.4 = (bf16[1024,32]{0,1:T(8,128)(2,1)S(1)}, bf16[1024,32]{0,1:T(8,128)(2,1)}, u32[]{:S(2)}) copy-start(bf16[1024,32]{0,1:T(8,128)(2,1)} %param.23) | copy-start | bytes 196612
  6.2 2.2 %copy-start.1 = (bf16[16,20,1024]{2,1,0:T(8,128)(2,1)}, bf16[16,20,1024]{2,1,0:T(8,128)(2,1)S(1)}, u32[]{:S(2)}) copy-start(bf16[16,20,1024]{2,1,0:T(8,128)(2,1)S(1)} %multiply_convert_fusion.drive_ref) | copy-start | bytes 1966084
  8.9 26.2 %copy-start.3 = (bf16[16,20,1024]{2,0,1:T(8,128)(2,1)S(1)}, bf16[16,20,1024]{2,0,1:T(8,128)(2,1)}, u32[]{:S(2)}) copy-start(bf16[16,20,1024]{2,0,1:T(8,128)(2,1)} %param.19) | copy-start | bytes 1966084
  29.8 6.6 %copy-start.5 = (f32[16,1024]{1,0:T(8,128)S(1)}, f32[16,1024]{1,0:T(8,128)}, u32[]{:S(2)}) copy-start(f32[16,1024]{1,0:T(8,128)} %param.26) | copy-start | bytes 196612
  30.8 17.9 %all-to-all-start.1 = ((bf16[16,20,576]{2,1,0:T(8,128)(2,1)}), bf16[16,20,576]{2,1,0:T(8,128)(2,1)S(1)}, u32[]{:S(2)}, u32[]{:S(2)}) async-start(bf16[16,20,576]{2,1,0:T(8,128)(2,1)} %broadcast_in_dim.7), calls=%async_computation.1 | async-start | bytes 983040 | tf_op jit(solution)/shard_map/all_to_all | solution.py:136
  36.4 12.9 %copy-start.7 = (f32[1024]{0:T(1024)S(1)}, f32[1024]{0:T(1024)}, u32[]{:S(2)}) copy-start(f32[1024]{0:T(1024)} %param.25) | copy-start | bytes 12292

commit v9 on v7

--- a/solution.py
+++ b/solution.py
@@ -24,12 +24,14 @@
 def scan_kernel(
     lens_ref, fmap_ref, rate_ref, drive_ref, gate_ref, b_ref, c_ref, *rest
 ):
-    pair = len(rest) - 6
-    h0_refs, (a_ref, skip_ref, packed_ref, r_scr, u_scr, y_scr) = rest[:pair], rest[pair:]
+    pair = len(rest) - 8
+    h0_refs = rest[:pair]
+    a_ref, skip_ref, packed_ref, r_scr, u_scr, y_scr, bb_scr, cb_scr = rest[pair:]
     positions = rate_ref.shape[1]
-    state_size = h0_refs[0].shape[1]
-    decay = a_ref[...]
-    states, lives = [], []
+    state_size, width_local = h0_refs[0].shape[1], h0_refs[0].shape[2]
+    lanes = bb_scr.shape[-1]
+    block = 4 if positions % 4 == 0 else 1
+    states, lives, longest = [], [], 0
     for k in range(pair):
         live = jnp.clip(lens_ref[pl.program_id(0) * pair + k] + GEN, 0, positions)
         inflow = drive_ref[k].astype(jnp.float32)
@@ -37,16 +39,34 @@
         rate = jnp.where(alive, rate_ref[k], 0.0)
         r_scr[k] = rate
         u_scr[k] = rate * inflow
+        b_all = b_ref[k]
+        c_all = c_ref[k]
+        for p in range(positions):
+            bb_scr[k, p] = jnp.broadcast_to(b_all[:, p : p + 1], (state_size, lanes))
+            cb_scr[k, p] = jnp.broadcast_to(c_all[:, p : p + 1], (state_size, lanes))
         states.append(h0_refs[k][0])
         lives.append(alive)
-    for p in range(positions):
-        for k in range(pair):
-            b_col = b_ref[k][:, p : p + 1]
-            c_col = c_ref[k][:, p : p + 1]
-            h = states[k]
-            h = jnp.exp(r_scr[k, p : p + 1, :] * decay) * h + u_scr[k, p : p + 1, :] * b_col
-            y_scr[k, p : p + 1, :] = jnp.sum(c_col * h, axis=0, keepdims=True)
-            states[k] = h
+        longest = jnp.maximum(longest, live)
+    decay = a_ref[...]
+    tiles = width_local // lanes
+
+    def advance(blk, carried):
+        carried = list(carried)
+        for i in range(block):
+            p = blk * block + i
+            for k in range(pair):
+                b_col = jnp.tile(bb_scr[k, p], (1, tiles))
+                c_col = jnp.tile(cb_scr[k, p], (1, tiles))
+                h = carried[k]
+                h = (
+                    jnp.exp(r_scr[k, pl.ds(p, 1), :] * decay) * h
+                    + u_scr[k, pl.ds(p, 1), :] * b_col
+                )
+                y_scr[k, pl.ds(p, 1), :] = jnp.sum(c_col * h, axis=0, keepdims=True)
+                carried[k] = h
+        return tuple(carried)
+
+    states = lax.fori_loop(0, (longest + block - 1) // block, advance, tuple(states))
     for k in range(pair):
         packed_ref[k, :state_size, :] = states[k].astype(packed_ref.dtype)
         inflow = drive_ref[k].astype(jnp.float32)
@@ -84,7 +104,8 @@
             pl.BlockSpec((1, width_local), whole),
         ],
         out_specs=pl.BlockSpec((pair, state_size + positions, width_local), row_block),
-        scratch_shapes=[pltpu.VMEM((pair, positions, width_local), jnp.float32)] * 3,
+        scratch_shapes=[pltpu.VMEM((pair, positions, width_local), jnp.float32)] * 3
+        + [pltpu.VMEM((pair, positions, state_size, min(128, width_local)), jnp.float32)] * 2,
     )
     return pl.pallas_call(
         scan_kernel,

time: 106 us -> 106 us (level)
  no operation moved by 1% of the time
where the time goes in v9:
time: 106 us
  blocking collectives  57 us (54%)
  Pallas kernels  13.7 us (13%)
  waiting for transfers between devices  11.6 us (11%)
  local copies, waits for them, and re-layouts  11 us (10%)
  starting transfers between devices  4.39 us (4%)
  other arithmetic  4.08 us (4%)
  matrix products  3.08 us (3%)
    all_to_all x1, blocking collectives, body(): lax.all_to_all(packed_local, 'chan', split_axis=0, concat_axis=2, tiled=T...  36.3 us
    all_to_all x1, blocking collectives, body(): lax.all_to_all(partial.reshape(devices, -1, partial.shape[1]), 'chan', 0,...  20.8 us
    pallas_call x1, Pallas kernels, run_scan(): pl.pallas_call(scan_kernel, grid_spec=grid_spec, out_shape=jax.ShapeDtype...  13.7 us
    all_to_all x1, waiting for transfers between devices, body(): lax.all_to_all(jnp.broadcast_to(mine[None], (devices,) + mine.shape), 'ch...  11.6 us
    all_to_all x1, starting transfers between devices, body(): lax.all_to_all(jnp.broadcast_to(mine[None], (devices,) + mine.shape), 'ch...  4.39 us
    unnamed x20, local copies, waits for them, and re-layouts  2.25 us
  transfers between devices with their start and end apart: 1, of which 1 were waited for; matrix products, arithmetic and copies ran while one was open for 2% of the time, Pallas kernels for 0%

profile of v9, /device:TPU:1, one launch (start us, length us, event | category | flops | bytes accessed | tf_op | source)
XLA Modules:
  0.0 105.7 jit_solution(8466931267018207981)
XLA Ops:
  0.6 0.0 copy-start
  0.6 0.0 copy-start.2
  0.7 0.8 pad_clamp_fusion
  1.4 0.9 fusion.9
  2.3 1.7 %gather_fusion = bf16[16,3,1024]{2,0,1:T(8,128)(2,1)S(1)} fusion(bf16[16,3,1024]{2,0,1:T(8,128)(2,1)} %param.15, s32[1024]{0:T(1024)S(1)} %pad_clamp_fusion), kind=kCustom, calls=%fused_computation | custom fusion | bytes 196672 | tf_op jit(solution)/shard_map/jit(_take)/gather | solution.py:13
  4.0 0.1 copy.29
  4.1 0.0 copy-done.2
  4.2 0.4 copy.30
  4.5 0.0 copy-start.6
  4.5 0.3 maximum_convert_fusion
  4.8 0.4 copy-done.6
  5.2 1.0 multiply_convert_fusion.drive_ref
  6.2 0.0 copy-start.1
  6.2 0.1 reshape.29
  6.4 0.0 copy-done.4
  6.4 0.3 subtract_convert_fusion
  6.7 1.7 %convolution_convert_fusion = bf16[320,512]{1,0:T(8,128)(2,1)S(1)} fusion(bf16[320,1024]{1,0:T(8,128)(2,1)S(1)} %reshape.29, bf16[1024,512]{1,0:T(8,128)(2,1)} %param.22), kind=kOutput, calls=%fused_computation.12 | convolution fusion | flops 335708160 | bytes 2031616 | tf_op jit(solution)/shard_map/dot_general | solution.py:142
  8.5 0.0 copy-done.1
  8.5 0.1 copy.32
  8.6 0.1 copy.31
  8.7 0.1 pad_maximum_fusion
  8.8 0.1 reshape.30
  8.9 0.0 copy-start.3
  8.9 20.8 %all_to_all.28 = bf16[16,20,576]{2,1,0:T(8,128)(2,1)S(1)} all-to-all(bf16[16,20,576]{2,1,0:T(8,128)(2,1)S(1)} %reshape.30), channel_id=1, replica_groups=mesh['group'=2,'chan'=16] {'chan'}, dimensions={0} | all-to-all | bytes 737280 | tf_op jit(solution)/shard_map/all_to_all | solution.py:148
  29.7 0.1 convert_reduce_fusion
  29.8 0.0 copy-start.5
  29.8 0.1 subtract_convert_fusion.1
  29.9 0.1 pad_maximum_fusion.1
  30.0 0.8 broadcast_in_dim.7
  30.8 4.4 %all-to-all-start.1 = ((bf16[16,20,576]{2,1,0:T(8,128)(2,1)}), bf16[16,20,576]{2,1,0:T(8,128)(2,1)S(1)}, u32[]{:S(2)}, u32[]{:S(2)}) async-start(bf16[16,20,576]{2,1,0:T(8,128)(2,1)} %broadcast_in_dim.7), calls=%async_computation.1 | async-start | bytes 983040 | tf_op jit(solution)/shard_map/all_to_all | solution.py:157
  35.2 0.0 copy-done.3
  35.2 1.3 %copy.37.gate_ref = bf16[16,20,1024]{2,1,0:T(8,128)(2,1)} copy(bf16[16,20,1024]{2,0,1:T(8,128)(2,1)S(1)} %copy-done.3) | data formatting | bytes 1310720 | tf_op args[5]
  36.4 0.6 exponential_negate_fusion.rest_2_
  37.1 11.6 %all-to-all-done.1 = bf16[16,20,576]{2,1,0:T(8,128)(2,1)S(1)} async-done(((bf16[16,20,576]{2,1,0:T(8,128)(2,1)}), bf16[16,20,576]{2,1,0:T(8,128)(2,1)S(1)}, u32[]{:S(2)}, u32[]{:S(2)}) %all-to-all-start.1) | async-done | bytes 368672 | tf_op jit(solution)/shard_map/all_to_all | solution.py:157
  48.7 0.2 reshape.31
  48.8 0.1 fusion.7
  48.9 0.1 copy.39
  49.0 0.1 copy.40
  49.1 0.2 reshape.33
  49.3 1.0 compare_select_fusion
  50.4 1.3 %reshape.32.rate_ref = f32[16,20,1024]{2,1,0:T(8,128)} reshape(f32[320,1024]{1,0:T(8,128)S(1)} %compare_select_fusion) | data formatting | bytes 2621440 | tf_op jit(solution)/shard_map/reshape | solution.py:167
  51.7 0.8 copy_bitcast_fusion
  52.5 13.7 %shard_map.149 = bf16[16,36,1024]{2,1,0:T(8,128)(2,1)} custom-call(s32[16]{0:T(128)} %lens_ref.1, s32[16]{0:T(128)} %fmap_ref.1, f32[16,20,1024]{2,1,0:T(8,128)} %reshape.32.rate_ref, bf16[16,20,1024]{2,1,0:T(8,128)(2,1)} %copy-done.1, bf16[16,20,1024]{2,1,0:T(8,128)(2,1)} %copy.37.gate_ref, f32[16,16,20]{2,1,0:T(8,128)} %get-tuple-element.15.b_ref, ...), custom_call_target="tpu_custom_call" | custom-call | tf_op jit(solution)/shard_map/pallas_call | solution.py:110
  66.2 36.3 %all_to_all.29 = bf16[16,36,1024]{2,1,0:T(8,128)(2,1)S(1)} all-to-all(bf16[16,36,1024]{2,1,0:T(8,128)(2,1)} %shard_map.149), channel_id=1, replica_groups=mesh['group'=2,'chan'=16] {'chan'}, dimensions={0} | all-to-all | bytes 2359296 | tf_op jit(solution)/shard_map/all_to_all | solution.py:175
  102.4 0.7 copy.38
  103.1 0.6 all_to_all.24
  103.7 0.9 slice.91
  104.7 1.0 slice_convert_fusion
  (8 shorter events, 0.0 us)
Async XLA Ops:
  0.6 48.7 %copy-start = (bf16[512,1024]{1,0:T(8,128)(2,1)S(1)}, bf16[512,1024]{1,0:T(8,128)(2,1)}, u32[]{:S(2)}) copy-start(bf16[512,1024]{1,0:T(8,128)(2,1)} %param.24) | copy-start | bytes 3145732
  0.6 3.5 %copy-start.2 = (bf16[16,20,1024]{2,0,1:T(8,128)(2,1)S(1)}, bf16[16,20,1024]{2,0,1:T(8,128)(2,1)}, u32[]{:S(2)}) copy-start(bf16[16,20,1024]{2,0,1:T(8,128)(2,1)} %param.18) | copy-start | bytes 1966084
  4.5 0.7 copy-start.6
  5.2 1.2 %copy-start.4 = (bf16[1024,32]{0,1:T(8,128)(2,1)S(1)}, bf16[1024,32]{0,1:T(8,128)(2,1)}, u32[]{:S(2)}) copy-start(bf16[1024,32]{0,1:T(8,128)(2,1)} %param.23) | copy-start | bytes 196612
  6.2 2.2 %copy-start.1 = (bf16[16,20,1024]{2,1,0:T(8,128)(2,1)}, bf16[16,20,1024]{2,1,0:T(8,128)(2,1)S(1)}, u32[]{:S(2)}) copy-start(bf16[16,20,1024]{2,1,0:T(8,128)(2,1)S(1)} %multiply_convert_fusion.drive_ref) | copy-start | bytes 1966084
  8.9 26.2 %copy-start.3 = (bf16[16,20,1024]{2,0,1:T(8,128)(2,1)S(1)}, bf16[16,20,1024]{2,0,1:T(8,128)(2,1)}, u32[]{:S(2)}) copy-start(bf16[16,20,1024]{2,0,1:T(8,128)(2,1)} %param.19) | copy-start | bytes 1966084
  29.8 6.6 %copy-start.5 = (f32[16,1024]{1,0:T(8,128)S(1)}, f32[16,1024]{1,0:T(8,128)}, u32[]{:S(2)}) copy-start(f32[16,1024]{1,0:T(8,128)} %param.26) | copy-start | bytes 196612
  30.8 17.9 %all-to-all-start.1 = ((bf16[16,20,576]{2,1,0:T(8,128)(2,1)}), bf16[16,20,576]{2,1,0:T(8,128)(2,1)S(1)}, u32[]{:S(2)}, u32[]{:S(2)}) async-start(bf16[16,20,576]{2,1,0:T(8,128)(2,1)} %broadcast_in_dim.7), calls=%async_computation.1 | async-start | bytes 983040 | tf_op jit(solution)/shard_map/all_to_all | solution.py:157
  36.4 12.9 %copy-start.7 = (f32[1024]{0:T(1024)S(1)}, f32[1024]{0:T(1024)}, u32[]{:S(2)}) copy-start(f32[1024]{0:T(1024)} %param.25) | copy-start | bytes 12292

commit v10 on v7

--- a/solution.py
+++ b/solution.py
@@ -44,7 +44,9 @@
             b_col = b_ref[k][:, p : p + 1]
             c_col = c_ref[k][:, p : p + 1]
             h = states[k]
-            h = jnp.exp(r_scr[k, p : p + 1, :] * decay) * h + u_scr[k, p : p + 1, :] * b_col
+            rate_rows = r_scr[k, pl.ds(p, state_size, stride=0), :]
+            push_rows = u_scr[k, pl.ds(p, state_size, stride=0), :]
+            h = jnp.exp2(rate_rows * decay) * h + push_rows * b_col
             y_scr[k, p : p + 1, :] = jnp.sum(c_col * h, axis=0, keepdims=True)
             states[k] = h
     for k in range(pair):
@@ -146,7 +148,7 @@
     ).reshape(thought_count, positions, width_local)
     b_t = jnp.swapaxes(selection[:, :, :state_size], 1, 2)
     c_t = jnp.swapaxes(selection[:, :, state_size:], 1, 2)
-    decay_rate = -jnp.exp(decay_log)
+    decay_rate = -jnp.exp(decay_log) * 1.4426950408889634
     packed_local = run_scan(
         judge_lengths, fork_map, step_rate, driven, gate_input, b_t, c_t, parent_state,
         decay_rate, skip_gain,

time: 106 us -> 104 us (0.981)
  Pallas kernels: 13.2 us -> 11.4 us
    pallas_call x1, Pallas kernels: 13.2 us -> 11.4 us  [run_scan(): pl.pallas_call(scan_kernel, grid_spec=grid_spec, out_shape=jax.ShapeDtype...]
where the time goes in v10:
time: 104 us; the launch traced here: 103 us
  blocking collectives  57 us (55%)
  waiting for transfers between devices  11.6 us (11%)
  Pallas kernels  11.4 us (11%)
  local copies, waits for them, and re-layouts  11 us (11%)
  starting transfers between devices  4.39 us (4%)
  other arithmetic  4.08 us (4%)
  matrix products  3.08 us (3%)
    all_to_all x1, blocking collectives, body(): lax.all_to_all(packed_local, 'chan', split_axis=0, concat_axis=2, tiled=T...  36.3 us
    all_to_all x1, blocking collectives, body(): lax.all_to_all(partial.reshape(devices, -1, partial.shape[1]), 'chan', 0,...  20.8 us
    all_to_all x1, waiting for transfers between devices, body(): lax.all_to_all(jnp.broadcast_to(mine[None], (devices,) + mine.shape), 'ch...  11.6 us
    pallas_call x1, Pallas kernels, run_scan(): pl.pallas_call(scan_kernel, grid_spec=grid_spec, out_shape=jax.ShapeDtype...  11.4 us
    all_to_all x1, starting transfers between devices, body(): lax.all_to_all(jnp.broadcast_to(mine[None], (devices,) + mine.shape), 'ch...  4.39 us
    unnamed x20, local copies, waits for them, and re-layouts  2.25 us
  transfers between devices with their start and end apart: 1, of which 1 were waited for; matrix products, arithmetic and copies ran while one was open for 2% of the time, Pallas kernels for 0%

profile of v10, /device:TPU:1, one launch (start us, length us, event | category | flops | bytes accessed | tf_op | source)
XLA Modules:
  0.0 103.4 jit_solution(17726445166510427368)
XLA Ops:
  0.6 0.0 copy-start
  0.6 0.0 copy-start.2
  0.7 0.8 pad_clamp_fusion
  1.4 0.9 fusion.9
  2.3 1.7 %gather_fusion = bf16[16,3,1024]{2,0,1:T(8,128)(2,1)S(1)} fusion(bf16[16,3,1024]{2,0,1:T(8,128)(2,1)} %param.15, s32[1024]{0:T(1024)S(1)} %pad_clamp_fusion), kind=kCustom, calls=%fused_computation | custom fusion | bytes 196672 | tf_op jit(solution)/shard_map/jit(_take)/gather | solution.py:13
  4.0 0.1 copy.29
  4.1 0.0 copy-done.2
  4.2 0.4 copy.30
  4.5 0.0 copy-start.6
  4.5 0.3 maximum_convert_fusion
  4.8 0.4 copy-done.6
  5.2 1.0 multiply_convert_fusion.drive_ref
  6.2 0.0 copy-start.1
  6.2 0.1 reshape.29
  6.4 0.3 subtract_convert_fusion
  6.7 1.7 %convolution_convert_fusion = bf16[320,512]{1,0:T(8,128)(2,1)S(1)} fusion(bf16[320,1024]{1,0:T(8,128)(2,1)S(1)} %reshape.29, bf16[1024,512]{1,0:T(8,128)(2,1)} %param.22), kind=kOutput, calls=%fused_computation.12 | convolution fusion | flops 335708160 | bytes 2031616 | tf_op jit(solution)/shard_map/dot_general | solution.py:123
  8.5 0.1 copy.32
  8.6 0.1 copy.31
  8.7 0.1 pad_maximum_fusion
  8.8 0.1 reshape.30
  8.9 0.0 copy-start.3
  8.9 20.8 %all_to_all.28 = bf16[16,20,576]{2,1,0:T(8,128)(2,1)S(1)} all-to-all(bf16[16,20,576]{2,1,0:T(8,128)(2,1)S(1)} %reshape.30), channel_id=1, replica_groups=mesh['group'=2,'chan'=16] {'chan'}, dimensions={0} | all-to-all | bytes 737280 | tf_op jit(solution)/shard_map/all_to_all | solution.py:129
  29.7 0.1 convert_reduce_fusion
  29.8 0.0 copy-start.5
  29.8 0.1 subtract_convert_fusion.1
  29.9 0.1 pad_maximum_fusion.1
  30.0 0.8 broadcast_in_dim.7
  30.8 4.4 %all-to-all-start.1 = ((bf16[16,20,576]{2,1,0:T(8,128)(2,1)}), bf16[16,20,576]{2,1,0:T(8,128)(2,1)S(1)}, u32[]{:S(2)}, u32[]{:S(2)}) async-start(bf16[16,20,576]{2,1,0:T(8,128)(2,1)} %broadcast_in_dim.7), calls=%async_computation.1 | async-start | bytes 983040 | tf_op jit(solution)/shard_map/all_to_all | solution.py:138
  35.2 1.3 %copy.37.gate_ref = bf16[16,20,1024]{2,1,0:T(8,128)(2,1)} copy(bf16[16,20,1024]{2,0,1:T(8,128)(2,1)S(1)} %copy-done.3) | data formatting | bytes 1310720 | tf_op args[5]
  36.4 0.0 copy-done.5
  36.4 0.6 negate_multiply_fusion.rest_2_
  37.1 11.6 %all-to-all-done.1 = bf16[16,20,576]{2,1,0:T(8,128)(2,1)S(1)} async-done(((bf16[16,20,576]{2,1,0:T(8,128)(2,1)}), bf16[16,20,576]{2,1,0:T(8,128)(2,1)S(1)}, u32[]{:S(2)}, u32[]{:S(2)}) %all-to-all-start.1) | async-done | bytes 368672 | tf_op jit(solution)/shard_map/all_to_all | solution.py:138
  48.7 0.2 reshape.31
  48.8 0.1 fusion.7
  48.9 0.1 copy.39
  49.0 0.1 copy.40
  49.1 0.2 reshape.33
  49.3 0.0 copy-done
  49.3 0.0 copy-done.7
  49.3 1.0 compare_select_fusion
  50.4 1.3 %reshape.32.rate_ref = f32[16,20,1024]{2,1,0:T(8,128)} reshape(f32[320,1024]{1,0:T(8,128)S(1)} %compare_select_fusion) | data formatting | bytes 2621440 | tf_op jit(solution)/shard_map/reshape | solution.py:148
  51.7 0.8 copy_bitcast_fusion
  52.5 11.4 %shard_map.149 = bf16[16,36,1024]{2,1,0:T(8,128)(2,1)} custom-call(s32[16]{0:T(128)} %lens_ref.1, s32[16]{0:T(128)} %fmap_ref.1, f32[16,20,1024]{2,1,0:T(8,128)} %reshape.32.rate_ref, bf16[16,20,1024]{2,1,0:T(8,128)(2,1)} %copy-done.1, bf16[16,20,1024]{2,1,0:T(8,128)(2,1)} %copy.37.gate_ref, f32[16,16,20]{2,1,0:T(8,128)} %get-tuple-element.15.b_ref, ...), custom_call_target="tpu_custom_call" | custom-call | tf_op jit(solution)/shard_map/pallas_call | solution.py:91
  63.9 36.3 %all_to_all.29 = bf16[16,36,1024]{2,1,0:T(8,128)(2,1)S(1)} all-to-all(bf16[16,36,1024]{2,1,0:T(8,128)(2,1)} %shard_map.149), channel_id=1, replica_groups=mesh['group'=2,'chan'=16] {'chan'}, dimensions={0} | all-to-all | bytes 2359296 | tf_op jit(solution)/shard_map/all_to_all | solution.py:156
  100.2 0.7 copy.38
  100.8 0.6 all_to_all.24
  101.5 0.9 slice.91
  102.4 1.0 %slice_convert_fusion = f32[1,16,16384]{2,1,0:T(8,128)} fusion(bf16[1,36,16384]{2,1,0:T(8,128)(2,1)S(1)} %all_to_all.24), kind=kLoop, calls=%fused_computation.15 | loop fusion | flops 262144 | bytes 1572864 | tf_op jit(solution)/shard_map/convert_element_type | solution.py:157
  (8 shorter events, 0.0 us)
Async XLA Ops:
  0.6 48.7 %copy-start = (bf16[512,1024]{1,0:T(8,128)(2,1)S(1)}, bf16[512,1024]{1,0:T(8,128)(2,1)}, u32[]{:S(2)}) copy-start(bf16[512,1024]{1,0:T(8,128)(2,1)} %param.24) | copy-start | bytes 3145732
  0.6 3.5 %copy-start.2 = (bf16[16,20,1024]{2,0,1:T(8,128)(2,1)S(1)}, bf16[16,20,1024]{2,0,1:T(8,128)(2,1)}, u32[]{:S(2)}) copy-start(bf16[16,20,1024]{2,0,1:T(8,128)(2,1)} %param.18) | copy-start | bytes 1966084
  4.5 0.7 copy-start.6
  5.2 1.2 %copy-start.4 = (bf16[1024,32]{0,1:T(8,128)(2,1)S(1)}, bf16[1024,32]{0,1:T(8,128)(2,1)}, u32[]{:S(2)}) copy-start(bf16[1024,32]{0,1:T(8,128)(2,1)} %param.23) | copy-start | bytes 196612
  6.2 2.2 %copy-start.1 = (bf16[16,20,1024]{2,1,0:T(8,128)(2,1)}, bf16[16,20,1024]{2,1,0:T(8,128)(2,1)S(1)}, u32[]{:S(2)}) copy-start(bf16[16,20,1024]{2,1,0:T(8,128)(2,1)S(1)} %multiply_convert_fusion.drive_ref) | copy-start | bytes 1966084
  8.9 26.2 %copy-start.3 = (bf16[16,20,1024]{2,0,1:T(8,128)(2,1)S(1)}, bf16[16,20,1024]{2,0,1:T(8,128)(2,1)}, u32[]{:S(2)}) copy-start(bf16[16,20,1024]{2,0,1:T(8,128)(2,1)} %param.19) | copy-start | bytes 1966084
  29.8 6.6 %copy-start.5 = (f32[16,1024]{1,0:T(8,128)S(1)}, f32[16,1024]{1,0:T(8,128)}, u32[]{:S(2)}) copy-start(f32[16,1024]{1,0:T(8,128)} %param.26) | copy-start | bytes 196612
  30.8 17.9 %all-to-all-start.1 = ((bf16[16,20,576]{2,1,0:T(8,128)(2,1)}), bf16[16,20,576]{2,1,0:T(8,128)(2,1)S(1)}, u32[]{:S(2)}, u32[]{:S(2)}) async-start(bf16[16,20,576]{2,1,0:T(8,128)(2,1)} %broadcast_in_dim.7), calls=%async_computation.1 | async-start | bytes 983040 | tf_op jit(solution)/shard_map/all_to_all | solution.py:138
  36.4 12.9 %copy-start.7 = (f32[1024]{0:T(1024)S(1)}, f32[1024]{0:T(1024)}, u32[]{:S(2)}) copy-start(f32[1024]{0:T(1024)} %param.25) | copy-start | bytes 12292

commit v11 on v10

--- a/solution.py
+++ b/solution.py
@@ -8,17 +8,75 @@
 GEN = 4
 
 
-def convolve(parent_conv, fork_map, mixer_input, conv_weight, conv_bias):
-    positions = mixer_input.shape[1]
-    start_conv = jnp.take(parent_conv, fork_map, axis=0, mode="clip")
-    padded = jnp.concatenate([start_conv, mixer_input], axis=1).astype(jnp.float32)
-    tap_weights = conv_weight.astype(jnp.float32)
-    summed = conv_bias[None, None, :] + tap_weights[0][None, None, :] * padded[:, 0:positions, :]
-    for offset in range(1, conv_weight.shape[0]):
-        summed = (
-            summed + tap_weights[offset][None, None, :] * padded[:, offset : offset + positions, :]
-        )
-    return jax.nn.silu(summed).astype(jnp.bfloat16)
+def project_kernel(
+    fmap_ref, conv_ref, input_ref, weight_ref, bias_ref, down_ref, select_ref,
+    driven_ref, partial_ref, pad_scr, rows_scr, out_scr
+):
+    thought_count, positions, _ = input_ref.shape
+    taps = weight_ref.shape[0]
+    rank = down_ref.shape[1]
+    state_twice = select_ref.shape[1]
+    tap_weights = weight_ref[...].astype(jnp.float32)
+    for t in range(thought_count):
+        pad_scr[0 : taps - 1, :] = conv_ref[fmap_ref[t]].astype(jnp.float32)
+        pad_scr[taps - 1 : taps - 1 + positions, :] = input_ref[t].astype(jnp.float32)
+        summed = bias_ref[...] + tap_weights[0:1, :] * pad_scr[0:positions, :]
+        for offset in range(1, taps):
+            summed = summed + tap_weights[offset : offset + 1, :] * pad_scr[
+                offset : offset + positions, :
+            ]
+        driven = jax.nn.silu(summed).astype(jnp.bfloat16)
+        driven_ref[t] = driven
+        rows_scr[t * positions : (t + 1) * positions, :] = driven.astype(jnp.float32)
+    token_rows = rows_scr[...].astype(jnp.bfloat16)
+    out_scr[:, :rank] = jnp.dot(token_rows, down_ref[...], preferred_element_type=jnp.float32)
+    out_scr[:, rank:] = jnp.dot(token_rows, select_ref[...], preferred_element_type=jnp.float32)
+    for t in range(thought_count):
+        block = out_scr[t * positions : (t + 1) * positions, :]
+        select_part = block[:, rank:]
+        select_high = select_part.astype(jnp.bfloat16)
+        select_low = (select_part - select_high.astype(jnp.float32)).astype(jnp.bfloat16)
+        partial_ref[t, :, :rank] = block[:, :rank].astype(jnp.bfloat16)
+        partial_ref[t, :, rank : rank + state_twice] = select_high
+        partial_ref[t, :, rank + state_twice :] = select_low
+
+
+def project(parent_conv, fork_map, mixer_input, conv_weight, conv_bias, rate_down,
+            selection_weight):
+    thought_count, positions, width_local = mixer_input.shape
+    taps = conv_weight.shape[0]
+    rank, state_twice = rate_down.shape[1], selection_weight.shape[1]
+    full = lambda shape: pl.BlockSpec(shape, lambda i, fmap: (0,) * len(shape))
+    grid_spec = pltpu.PrefetchScalarGridSpec(
+        num_scalar_prefetch=1,
+        grid=(1,),
+        in_specs=[
+            full(parent_conv.shape),
+            full(mixer_input.shape),
+            full(conv_weight.shape),
+            full((1, width_local)),
+            full(rate_down.shape),
+            full(selection_weight.shape),
+        ],
+        out_specs=[
+            full(mixer_input.shape),
+            full((thought_count, positions, rank + 2 * state_twice)),
+        ],
+        scratch_shapes=[
+            pltpu.VMEM((taps - 1 + positions, width_local), jnp.float32),
+            pltpu.VMEM((thought_count * positions, width_local), jnp.float32),
+            pltpu.VMEM((thought_count * positions, rank + state_twice), jnp.float32),
+        ],
+    )
+    return pl.pallas_call(
+        project_kernel,
+        grid_spec=grid_spec,
+        out_shape=(
+            jax.ShapeDtypeStruct(mixer_input.shape, jnp.bfloat16),
+            jax.ShapeDtypeStruct((thought_count, positions, rank + 2 * state_twice), jnp.bfloat16),
+        ),
+    )(fork_map, parent_conv, mixer_input, conv_weight, conv_bias.reshape(1, width_local),
+      rate_down, selection_weight)
 
 
 def scan_kernel(
@@ -118,16 +176,12 @@
     thought_count, positions, width_local = mixer_input.shape
     state_size = parent_state.shape[1]
     rank = rate_down.shape[1]
-    driven = convolve(parent_conv, fork_map, mixer_input, conv_weight, conv_bias)
-    token_rows = driven.reshape(thought_count * positions, width_local)
-    low_part = jnp.dot(token_rows, rate_down, preferred_element_type=jnp.float32)
-    select_part = jnp.dot(token_rows, selection_weight, preferred_element_type=jnp.float32)
-    select_high = select_part.astype(jnp.bfloat16)
-    select_low = (select_part - select_high.astype(jnp.float32)).astype(jnp.bfloat16)
-    partial = jnp.concatenate([low_part.astype(jnp.bfloat16), select_high, select_low], axis=1)
+    driven, partial = project(
+        parent_conv, fork_map, mixer_input, conv_weight, conv_bias, rate_down, selection_weight
+    )
     devices = lax.axis_size("chan")
     pieces = lax.all_to_all(
-        partial.reshape(devices, -1, partial.shape[1]), "chan", 0, 0, tiled=True
+        partial.reshape(devices, -1, partial.shape[2]), "chan", 0, 0, tiled=True
     ).astype(jnp.float32)
     reduced = jnp.sum(pieces, axis=0)
     low_mine = reduced[:, :rank].astype(jnp.bfloat16)

time: 104 us -> 107 us (1.029)
  Pallas kernels: 11.4 us -> 16.4 us
  other arithmetic: 4.08 us -> 1.94 us
  matrix products: 3.08 us -> 1.02 us
  local copies, waits for them, and re-layouts: 11 us -> 12.7 us
    pallas_call x0 -> x1, Pallas kernels: none -> 5 us  [project(): pl.pallas_call(project_kernel, grid_spec=grid_spec, out_shape=(jax.ShapeD...]
    unnamed x20 -> x14, local copies, waits for them, and re-layouts: 2.25 us -> 7.18 us
    dot_general x2 -> x0, matrix products: 2.06 us -> none  [the longest x1 1.74 us: body(): jnp.dot(token_rows, rate_down, preferred_element_type=jnp.float32)]
    gather x2 -> x0, local copies, waits for them, and re-layouts: 1.83 us -> none  [convolve(): start_conv = jnp.take(parent_conv, fork_map, axis=0, mode='clip')]
    convert_element_type x2 -> x0, other arithmetic: 1.27 us -> none  [the longest x1 1.01 us: convolve(): return jax.nn.silu(summed).astype(jnp.bfloat16)]
where the time goes in v11:
time: 107 us; the launch traced here: 106 us
  blocking collectives  57.1 us (53%)
  Pallas kernels  16.4 us (15%)
  local copies, waits for them, and re-layouts  12.7 us (12%)
  waiting for transfers between devices  11.6 us (11%)
  starting transfers between devices  4.52 us (4%)
  other arithmetic  1.94 us (2%)
    all_to_all x1, blocking collectives, body(): lax.all_to_all(packed_local, 'chan', split_axis=0, concat_axis=2, tiled=T...  36.3 us
    all_to_all x1, blocking collectives, body(): lax.all_to_all(partial.reshape(devices, -1, partial.shape[2]), 'chan', 0,...  20.8 us
    all_to_all x1, waiting for transfers between devices, body(): lax.all_to_all(jnp.broadcast_to(mine[None], (devices,) + mine.shape), 'ch...  11.6 us
    pallas_call x1, Pallas kernels, run_scan(): pl.pallas_call(scan_kernel, grid_spec=grid_spec, out_shape=jax.ShapeDtype...  11.4 us
    unnamed x14, local copies, waits for them, and re-layouts  7.18 us
    pallas_call x1, Pallas kernels, project(): pl.pallas_call(project_kernel, grid_spec=grid_spec, out_shape=(jax.ShapeD...  5 us
    all_to_all x1, starting transfers between devices, body(): lax.all_to_all(jnp.broadcast_to(mine[None], (devices,) + mine.shape), 'ch...  4.52 us
  transfers between devices with their start and end apart: 1, of which 1 were waited for; matrix products, arithmetic and copies ran while one was open for 2% of the time, Pallas kernels for 0%

profile of v11, /device:TPU:1, one launch (start us, length us, event | category | flops | bytes accessed | tf_op | source)
XLA Modules:
  0.0 106.0 jit_solution(2321014918190612843)
XLA Ops:
  0.6 0.0 copy-start
  0.6 1.7 %copy.28.conv_ref = bf16[16,3,1024]{2,1,0:T(4,128)(2,1)} copy(bf16[16,3,1024]{2,0,1:T(8,128)(2,1)} %param.15) | data formatting | bytes 196608 | tf_op args[1]
  2.4 1.7 %copy.30.select_ref = bf16[1024,32]{1,0:T(8,128)(2,1)} copy(bf16[1024,32]{0,1:T(8,128)(2,1)} %param.23) | data formatting | bytes 131072 | tf_op args[9]
  4.0 2.3 %copy.29.input_ref = bf16[16,20,1024]{2,1,0:T(8,128)(2,1)} copy(bf16[16,20,1024]{2,0,1:T(8,128)(2,1)} %param.18) | data formatting | bytes 1310720 | tf_op args[4]
  6.4 5.0 %shard_map.149 = (bf16[16,20,1024]{2,1,0:T(8,128)(2,1)}, bf16[16,20,576]{2,1,0:T(8,128)(2,1)}) custom-call(s32[16]{0:T(128)} %fmap_ref.3, bf16[16,3,1024]{2,1,0:T(4,128)(2,1)} %copy.28.conv_ref, bf16[16,20,1024]{2,1,0:T(8,128)(2,1)} %copy.29.input_ref, bf16[4,1024]{1,0:T(4,128)(2,1)} %weight_ref.1, f32[1,1024]{1,0:T(1,128)} %bitcast.15, ...), custom_call_target="tpu_custom_call" | custom-call | tf_op jit(solution)/shard_map/pallas_call | solution.py:71
  11.4 20.8 %all_to_all.28 = bf16[16,20,576]{2,1,0:T(8,128)(2,1)S(1)} all-to-all(bf16[16,20,576]{2,1,0:T(8,128)(2,1)} %get-tuple-element.4), channel_id=1, replica_groups=mesh['group'=2,'chan'=16] {'chan'}, dimensions={0} | all-to-all | bytes 737280 | tf_op jit(solution)/shard_map/all_to_all | solution.py:183
  32.2 0.0 copy-start.1
  32.2 0.1 convert_reduce_fusion
  32.3 0.1 subtract_convert_fusion
  32.4 0.1 pad_maximum_fusion
  32.5 0.8 broadcast_in_dim.2
  33.3 0.0 copy-start.2
  33.3 4.5 %all-to-all-start.1 = ((bf16[16,20,576]{2,1,0:T(8,128)(2,1)}), bf16[16,20,576]{2,1,0:T(8,128)(2,1)S(1)}, u32[]{:S(2)}, u32[]{:S(2)}) async-start(bf16[16,20,576]{2,1,0:T(8,128)(2,1)} %broadcast_in_dim.2), calls=%async_computation.1 | async-start | bytes 983040 | tf_op jit(solution)/shard_map/all_to_all | solution.py:192
  37.8 0.0 copy-done.1
  37.8 1.3 %copy.35.gate_ref = bf16[16,20,1024]{2,1,0:T(8,128)(2,1)} copy(bf16[16,20,1024]{2,0,1:T(8,128)(2,1)S(1)} %copy-done.1) | data formatting | bytes 1310720 | tf_op args[5]
  39.1 0.0 copy-done.2
  39.1 0.0 copy-start.3
  39.1 0.6 negate_multiply_fusion.rest_2_
  39.7 11.6 %all-to-all-done.1 = bf16[16,20,576]{2,1,0:T(8,128)(2,1)S(1)} async-done(((bf16[16,20,576]{2,1,0:T(8,128)(2,1)}), bf16[16,20,576]{2,1,0:T(8,128)(2,1)S(1)}, u32[]{:S(2)}, u32[]{:S(2)}) %all-to-all-start.1) | async-done | bytes 368672 | tf_op jit(solution)/shard_map/all_to_all | solution.py:192
  51.3 0.2 reshape.22
  51.4 0.1 fusion.3
  51.5 0.1 copy.37
  51.6 0.1 copy.38
  51.7 0.2 reshape.24
  52.0 0.0 copy-done
  52.0 0.0 copy-done.3
  52.0 1.0 compare_select_fusion
  53.0 1.3 %reshape.23.rate_ref = f32[16,20,1024]{2,1,0:T(8,128)} reshape(f32[320,1024]{1,0:T(8,128)S(1)} %compare_select_fusion) | data formatting | bytes 2621440 | tf_op jit(solution)/shard_map/reshape | solution.py:202
  54.3 0.8 copy_bitcast_fusion
  55.1 11.4 %shard_map.150 = bf16[16,36,1024]{2,1,0:T(8,128)(2,1)} custom-call(s32[16]{0:T(128)} %lens_ref.1, s32[16]{0:T(128)} %fmap_ref.3, f32[16,20,1024]{2,1,0:T(8,128)} %reshape.23.rate_ref, bf16[16,20,1024]{2,1,0:T(8,128)(2,1)} %get-tuple-element.5.drive_ref, bf16[16,20,1024]{2,1,0:T(8,128)(2,1)} %copy.35.gate_ref, f32[16,16,20]{2,1,0:T(8,128)} %get-tuple-element.13.b_ref, ...), custom_call_target="tpu_custom_call" | custom-call | tf_op jit(solution)/shard_map/pallas_call | solution.py:149
  66.5 36.3 %all_to_all.29 = bf16[16,36,1024]{2,1,0:T(8,128)(2,1)S(1)} all-to-all(bf16[16,36,1024]{2,1,0:T(8,128)(2,1)} %shard_map.150), channel_id=1, replica_groups=mesh['group'=2,'chan'=16] {'chan'}, dimensions={0} | all-to-all | bytes 2359296 | tf_op jit(solution)/shard_map/all_to_all | solution.py:210
  102.8 0.7 copy.36
  103.4 0.6 all_to_all.24
  104.1 0.9 slice.49
  105.0 1.0 slice_convert_fusion
  (3 shorter events, 0.0 us)
Async XLA Ops:
  0.6 51.3 %copy-start = (bf16[512,1024]{1,0:T(8,128)(2,1)S(1)}, bf16[512,1024]{1,0:T(8,128)(2,1)}, u32[]{:S(2)}) copy-start(bf16[512,1024]{1,0:T(8,128)(2,1)} %param.24) | copy-start | bytes 3145732
  32.2 5.6 %copy-start.1 = (bf16[16,20,1024]{2,0,1:T(8,128)(2,1)S(1)}, bf16[16,20,1024]{2,0,1:T(8,128)(2,1)}, u32[]{:S(2)}) copy-start(bf16[16,20,1024]{2,0,1:T(8,128)(2,1)} %param.19) | copy-start | bytes 1966084
  33.3 5.8 %copy-start.2 = (f32[16,1024]{1,0:T(8,128)S(1)}, f32[16,1024]{1,0:T(8,128)}, u32[]{:S(2)}) copy-start(f32[16,1024]{1,0:T(8,128)} %param.26) | copy-start | bytes 196612
  33.3 18.0 %all-to-all-start.1 = ((bf16[16,20,576]{2,1,0:T(8,128)(2,1)}), bf16[16,20,576]{2,1,0:T(8,128)(2,1)S(1)}, u32[]{:S(2)}, u32[]{:S(2)}) async-start(bf16[16,20,576]{2,1,0:T(8,128)(2,1)} %broadcast_in_dim.2), calls=%async_computation.1 | async-start | bytes 983040 | tf_op jit(solution)/shard_map/all_to_all | solution.py:192
  39.1 12.9 %copy-start.3 = (f32[1024]{0:T(1024)S(1)}, f32[1024]{0:T(1024)}, u32[]{:S(2)}) copy-start(f32[1024]{0:T(1024)} %param.25) | copy-start | bytes 12292

commit v12 on v11

--- a/solution.py
+++ b/solution.py
@@ -12,14 +12,17 @@
     fmap_ref, conv_ref, input_ref, weight_ref, bias_ref, down_ref, select_ref,
     driven_ref, partial_ref, pad_scr, rows_scr, out_scr
 ):
-    thought_count, positions, _ = input_ref.shape
+    positions, thought_count, _ = input_ref.shape
     taps = weight_ref.shape[0]
     rank = down_ref.shape[1]
-    state_twice = select_ref.shape[1]
+    state_twice = select_ref.shape[0]
     tap_weights = weight_ref[...].astype(jnp.float32)
     for t in range(thought_count):
-        pad_scr[0 : taps - 1, :] = conv_ref[fmap_ref[t]].astype(jnp.float32)
-        pad_scr[taps - 1 : taps - 1 + positions, :] = input_ref[t].astype(jnp.float32)
+        for tap in range(taps - 1):
+            pad_scr[tap : tap + 1, :] = conv_ref[tap, pl.ds(fmap_ref[t], 1), :].astype(
+                jnp.float32
+            )
+        pad_scr[taps - 1 : taps - 1 + positions, :] = input_ref[:, t, :].astype(jnp.float32)
         summed = bias_ref[...] + tap_weights[0:1, :] * pad_scr[0:positions, :]
         for offset in range(1, taps):
             summed = summed + tap_weights[offset : offset + 1, :] * pad_scr[
@@ -30,7 +33,10 @@
         rows_scr[t * positions : (t + 1) * positions, :] = driven.astype(jnp.float32)
     token_rows = rows_scr[...].astype(jnp.bfloat16)
     out_scr[:, :rank] = jnp.dot(token_rows, down_ref[...], preferred_element_type=jnp.float32)
-    out_scr[:, rank:] = jnp.dot(token_rows, select_ref[...], preferred_element_type=jnp.float32)
+    out_scr[:, rank:] = lax.dot_general(
+        token_rows, select_ref[...], (((1,), (1,)), ((), ())),
+        preferred_element_type=jnp.float32,
+    )
     for t in range(thought_count):
         block = out_scr[t * positions : (t + 1) * positions, :]
         select_part = block[:, rank:]
@@ -46,17 +52,20 @@
     thought_count, positions, width_local = mixer_input.shape
     taps = conv_weight.shape[0]
     rank, state_twice = rate_down.shape[1], selection_weight.shape[1]
+    conv_view = jnp.transpose(parent_conv, (1, 0, 2)).astype(jnp.float32)
+    input_view = jnp.transpose(mixer_input, (1, 0, 2))
+    select_view = jnp.transpose(selection_weight)
     full = lambda shape: pl.BlockSpec(shape, lambda i, fmap: (0,) * len(shape))
     grid_spec = pltpu.PrefetchScalarGridSpec(
         num_scalar_prefetch=1,
         grid=(1,),
         in_specs=[
-            full(parent_conv.shape),
-            full(mixer_input.shape),
+            full(conv_view.shape),
+            full(input_view.shape),
             full(conv_weight.shape),
             full((1, width_local)),
             full(rate_down.shape),
-            full(selection_weight.shape),
+            full(select_view.shape),
         ],
         out_specs=[
             full(mixer_input.shape),
@@ -75,8 +84,8 @@
             jax.ShapeDtypeStruct(mixer_input.shape, jnp.bfloat16),
             jax.ShapeDtypeStruct((thought_count, positions, rank + 2 * state_twice), jnp.bfloat16),
         ),
-    )(fork_map, parent_conv, mixer_input, conv_weight, conv_bias.reshape(1, width_local),
-      rate_down, selection_weight)
+    )(fork_map, conv_view, input_view, conv_weight, conv_bias.reshape(1, width_local),
+      rate_down, select_view)
 
 
 def scan_kernel(

time: 107 us -> 104 us (0.972)
  local copies, waits for them, and re-layouts: 12.7 us -> 7 us
  other arithmetic: 1.94 us -> 3.6 us
  Pallas kernels: 16.4 us -> 17.5 us
    unnamed x14 -> x11, local copies, waits for them, and re-layouts: 7.18 us -> 1.45 us
    convert_element_type x0 -> x1, other arithmetic: none -> 1.66 us  [project(): conv_view = jnp.transpose(parent_conv, (1, 0, 2)).astype(jnp.float32)]
where the time goes in v12:
time: 104 us; the launch traced here: 103 us
  blocking collectives  57.1 us (55%)
  Pallas kernels  17.5 us (17%)
  waiting for transfers between devices  11.6 us (11%)
  local copies, waits for them, and re-layouts  7 us (7%)
  starting transfers between devices  4.52 us (4%)
  other arithmetic  3.6 us (3%)
    all_to_all x1, blocking collectives, body(): lax.all_to_all(packed_local, 'chan', split_axis=0, concat_axis=2, tiled=T...  36.3 us
    all_to_all x1, blocking collectives, body(): lax.all_to_all(partial.reshape(devices, -1, partial.shape[2]), 'chan', 0,...  20.8 us
    all_to_all x1, waiting for transfers between devices, body(): lax.all_to_all(jnp.broadcast_to(mine[None], (devices,) + mine.shape), 'ch...  11.6 us
    pallas_call x1, Pallas kernels, run_scan(): pl.pallas_call(scan_kernel, grid_spec=grid_spec, out_shape=jax.ShapeDtype...  11.4 us
    pallas_call x1, Pallas kernels, project(): pl.pallas_call(project_kernel, grid_spec=grid_spec, out_shape=(jax.ShapeD...  6.02 us
    all_to_all x1, starting transfers between devices, body(): lax.all_to_all(jnp.broadcast_to(mine[None], (devices,) + mine.shape), 'ch...  4.52 us
  transfers between devices with their start and end apart: 1, of which 1 were waited for; matrix products, arithmetic and copies ran while one was open for 2% of the time, Pallas kernels for 0%

profile of v12, /device:TPU:1, one launch (start us, length us, event | category | flops | bytes accessed | tf_op | source)
XLA Modules:
  0.0 103.0 jit_solution(17387936045044750707)
XLA Ops:
  0.6 0.0 copy-start
  0.6 1.7 %convert_bitcast_fusion.conv_ref = f32[3,16,1024]{2,1,0:T(8,128)} fusion(bf16[16,3,1024]{2,0,1:T(8,128)(2,1)} %param.15), kind=kLoop, calls=%fused_computation.5 | loop fusion | flops 49152 | bytes 294912 | tf_op jit(solution)/shard_map/convert_element_type | solution.py:55
  2.3 6.0 %shard_map.149 = (bf16[16,20,1024]{2,1,0:T(8,128)(2,1)}, bf16[16,20,576]{2,1,0:T(8,128)(2,1)}) custom-call(s32[16]{0:T(128)} %fmap_ref.3, f32[3,16,1024]{2,1,0:T(8,128)} %convert_bitcast_fusion.conv_ref, bf16[20,16,1024]{2,1,0:T(8,128)(2,1)} %bitcast.19, bf16[4,1024]{1,0:T(4,128)(2,1)} %weight_ref.1, f32[1,1024]{1,0:T(1,128)} %bitcast.21, ...), custom_call_target="tpu_custom_call" | custom-call | tf_op jit(solution)/shard_map/pallas_call | solution.py:80
  8.3 20.8 %all_to_all.28 = bf16[16,20,576]{2,1,0:T(8,128)(2,1)S(1)} all-to-all(bf16[16,20,576]{2,1,0:T(8,128)(2,1)} %get-tuple-element.4), channel_id=1, replica_groups=mesh['group'=2,'chan'=16] {'chan'}, dimensions={0} | all-to-all | bytes 737280 | tf_op jit(solution)/shard_map/all_to_all | solution.py:192
  29.2 0.0 copy-start.1
  29.2 0.1 convert_reduce_fusion
  29.2 0.1 subtract_convert_fusion
  29.3 0.1 pad_maximum_fusion
  29.4 0.8 broadcast_in_dim.2
  30.2 0.0 copy-start.2
  30.2 4.5 %all-to-all-start.1 = ((bf16[16,20,576]{2,1,0:T(8,128)(2,1)}), bf16[16,20,576]{2,1,0:T(8,128)(2,1)S(1)}, u32[]{:S(2)}, u32[]{:S(2)}) async-start(bf16[16,20,576]{2,1,0:T(8,128)(2,1)} %broadcast_in_dim.2), calls=%async_computation.1 | async-start | bytes 983040 | tf_op jit(solution)/shard_map/all_to_all | solution.py:201
  34.8 0.0 copy-done.1
  34.8 1.3 %copy.26.gate_ref = bf16[16,20,1024]{2,1,0:T(8,128)(2,1)} copy(bf16[16,20,1024]{2,0,1:T(8,128)(2,1)S(1)} %copy-done.1) | data formatting | bytes 1310720 | tf_op args[5]
  36.0 0.0 copy-done.2
  36.0 0.0 copy-start.3
  36.0 0.6 negate_multiply_fusion.rest_2_
  36.7 11.6 %all-to-all-done.1 = bf16[16,20,576]{2,1,0:T(8,128)(2,1)S(1)} async-done(((bf16[16,20,576]{2,1,0:T(8,128)(2,1)}), bf16[16,20,576]{2,1,0:T(8,128)(2,1)S(1)}, u32[]{:S(2)}, u32[]{:S(2)}) %all-to-all-start.1) | async-done | bytes 368672 | tf_op jit(solution)/shard_map/all_to_all | solution.py:201
  48.2 0.2 reshape.22
  48.4 0.1 fusion.3
  48.5 0.1 copy.28
  48.6 0.1 copy.29
  48.7 0.2 reshape.24
  48.9 0.0 copy-done
  48.9 0.0 copy-done.3
  48.9 1.0 compare_select_fusion
  49.9 1.3 %reshape.23.rate_ref = f32[16,20,1024]{2,1,0:T(8,128)} reshape(f32[320,1024]{1,0:T(8,128)S(1)} %compare_select_fusion) | data formatting | bytes 2621440 | tf_op jit(solution)/shard_map/reshape | solution.py:211
  51.2 0.8 copy_bitcast_fusion
  52.0 11.4 %shard_map.150 = bf16[16,36,1024]{2,1,0:T(8,128)(2,1)} custom-call(s32[16]{0:T(128)} %lens_ref.1, s32[16]{0:T(128)} %fmap_ref.3, f32[16,20,1024]{2,1,0:T(8,128)} %reshape.23.rate_ref, bf16[16,20,1024]{2,1,0:T(8,128)(2,1)} %get-tuple-element.5.drive_ref, bf16[16,20,1024]{2,1,0:T(8,128)(2,1)} %copy.26.gate_ref, f32[16,16,20]{2,1,0:T(8,128)} %get-tuple-element.13.b_ref, ...), custom_call_target="tpu_custom_call" | custom-call | tf_op jit(solution)/shard_map/pallas_call | solution.py:158
  63.4 36.3 %all_to_all.29 = bf16[16,36,1024]{2,1,0:T(8,128)(2,1)S(1)} all-to-all(bf16[16,36,1024]{2,1,0:T(8,128)(2,1)} %shard_map.150), channel_id=1, replica_groups=mesh['group'=2,'chan'=16] {'chan'}, dimensions={0} | all-to-all | bytes 2359296 | tf_op jit(solution)/shard_map/all_to_all | solution.py:219
  99.7 0.7 copy.27
  100.4 0.6 all_to_all.24
  101.0 0.9 slice.49
  101.9 1.0 %slice_convert_fusion = f32[1,16,16384]{2,1,0:T(8,128)} fusion(bf16[1,36,16384]{2,1,0:T(8,128)(2,1)S(1)} %all_to_all.24), kind=kLoop, calls=%fused_computation.3 | loop fusion | flops 262144 | bytes 1572864 | tf_op jit(solution)/shard_map/convert_element_type | solution.py:220
  (3 shorter events, 0.0 us)
Async XLA Ops:
  0.6 48.3 %copy-start = (bf16[512,1024]{1,0:T(8,128)(2,1)S(1)}, bf16[512,1024]{1,0:T(8,128)(2,1)}, u32[]{:S(2)}) copy-start(bf16[512,1024]{1,0:T(8,128)(2,1)} %param.24) | copy-start | bytes 3145732
  29.2 5.6 %copy-start.1 = (bf16[16,20,1024]{2,0,1:T(8,128)(2,1)S(1)}, bf16[16,20,1024]{2,0,1:T(8,128)(2,1)}, u32[]{:S(2)}) copy-start(bf16[16,20,1024]{2,0,1:T(8,128)(2,1)} %param.19) | copy-start | bytes 1966084
  30.2 5.8 %copy-start.2 = (f32[16,1024]{1,0:T(8,128)S(1)}, f32[16,1024]{1,0:T(8,128)}, u32[]{:S(2)}) copy-start(f32[16,1024]{1,0:T(8,128)} %param.26) | copy-start | bytes 196612
  30.2 18.0 %all-to-all-start.1 = ((bf16[16,20,576]{2,1,0:T(8,128)(2,1)}), bf16[16,20,576]{2,1,0:T(8,128)(2,1)S(1)}, u32[]{:S(2)}, u32[]{:S(2)}) async-start(bf16[16,20,576]{2,1,0:T(8,128)(2,1)} %broadcast_in_dim.2), calls=%async_computation.1 | async-start | bytes 983040 | tf_op jit(solution)/shard_map/all_to_all | solution.py:201
  36.0 12.9 %copy-start.3 = (f32[1024]{0:T(1024)S(1)}, f32[1024]{0:T(1024)}, u32[]{:S(2)}) copy-start(f32[1024]{0:T(1024)} %param.25) | copy-start | bytes 12292

commit v13 on v12

--- a/solution.py
+++ b/solution.py
@@ -17,11 +17,20 @@
     rank = down_ref.shape[1]
     state_twice = select_ref.shape[0]
     tap_weights = weight_ref[...].astype(jnp.float32)
+    parents = conv_ref.shape[1]
+    row = lax.broadcasted_iota(jnp.int32, (thought_count, parents), 0)
+    col = lax.broadcasted_iota(jnp.int32, (thought_count, parents), 1)
+    pick = jnp.zeros((thought_count, parents), jnp.float32)
+    for t in range(thought_count):
+        pick = jnp.where((row == t) & (col == fmap_ref[t]), 1.0, pick)
+    pick = pick.astype(jnp.bfloat16)
+    starts = [
+        jnp.dot(pick, conv_ref[tap], preferred_element_type=jnp.float32)
+        for tap in range(taps - 1)
+    ]
     for t in range(thought_count):
         for tap in range(taps - 1):
-            pad_scr[tap : tap + 1, :] = conv_ref[tap, pl.ds(fmap_ref[t], 1), :].astype(
-                jnp.float32
-            )
+            pad_scr[tap : tap + 1, :] = starts[tap][t : t + 1, :]
         pad_scr[taps - 1 : taps - 1 + positions, :] = input_ref[:, t, :].astype(jnp.float32)
         summed = bias_ref[...] + tap_weights[0:1, :] * pad_scr[0:positions, :]
         for offset in range(1, taps):
@@ -52,7 +61,7 @@
     thought_count, positions, width_local = mixer_input.shape
     taps = conv_weight.shape[0]
     rank, state_twice = rate_down.shape[1], selection_weight.shape[1]
-    conv_view = jnp.transpose(parent_conv, (1, 0, 2)).astype(jnp.float32)
+    conv_view = jnp.transpose(parent_conv, (1, 0, 2))
     input_view = jnp.transpose(mixer_input, (1, 0, 2))
     select_view = jnp.transpose(selection_weight)
     full = lambda shape: pl.BlockSpec(shape, lambda i, fmap: (0,) * len(shape))

time: 104 us -> 102 us (0.981)
  other arithmetic: 3.6 us -> 1.94 us
    convert_element_type x1 -> x0, other arithmetic: 1.66 us -> none  [project(): conv_view = jnp.transpose(parent_conv, (1, 0, 2)).astype(jnp.float32)]
where the time goes in v13:
time: 102 us
  blocking collectives  57.1 us (56%)
  Pallas kernels  17.6 us (17%)
  waiting for transfers between devices  11.6 us (11%)
  local copies, waits for them, and re-layouts  7 us (7%)
  starting transfers between devices  4.52 us (4%)
  other arithmetic  1.94 us (2%)
  matrix products  1.02 us (1%)
    all_to_all x1, blocking collectives, body(): lax.all_to_all(packed_local, 'chan', split_axis=0, concat_axis=2, tiled=T...  36.3 us
    all_to_all x1, blocking collectives, body(): lax.all_to_all(partial.reshape(devices, -1, partial.shape[2]), 'chan', 0,...  20.8 us
    all_to_all x1, waiting for transfers between devices, body(): lax.all_to_all(jnp.broadcast_to(mine[None], (devices,) + mine.shape), 'ch...  11.6 us
    pallas_call x1, Pallas kernels, run_scan(): pl.pallas_call(scan_kernel, grid_spec=grid_spec, out_shape=jax.ShapeDtype...  11.4 us
    pallas_call x1, Pallas kernels, project(): pl.pallas_call(project_kernel, grid_spec=grid_spec, out_shape=(jax.ShapeD...  6.21 us
    all_to_all x1, starting transfers between devices, body(): lax.all_to_all(jnp.broadcast_to(mine[None], (devices,) + mine.shape), 'ch...  4.52 us
  transfers between devices with their start and end apart: 1, of which 1 were waited for; matrix products, arithmetic and copies ran while one was open for 2% of the time, Pallas kernels for 0%

profile of v13, /device:TPU:1, one launch (start us, length us, event | category | flops | bytes accessed | tf_op | source)
XLA Modules:
  0.0 101.5 jit_solution(15064931771749781808)
XLA Ops:
  0.6 0.0 copy-start
  0.6 6.2 %shard_map.149 = (bf16[16,20,1024]{2,1,0:T(8,128)(2,1)}, bf16[16,20,576]{2,1,0:T(8,128)(2,1)}) custom-call(s32[16]{0:T(128)} %fmap_ref.3, bf16[3,16,1024]{2,1,0:T(8,128)(2,1)} %bitcast.19, bf16[20,16,1024]{2,1,0:T(8,128)(2,1)} %bitcast.18, bf16[4,1024]{1,0:T(4,128)(2,1)} %weight_ref.1, f32[1,1024]{1,0:T(1,128)} %bitcast.21, bf16[1024,512]{1,0:T(8,128)(2,1)} %down_ref.1, ...), custom_call_target="tpu_custom_call" | custom-call | tf_op jit(solution)/shard_map/pallas_call | solution.py:89
  6.9 20.8 %all_to_all.28 = bf16[16,20,576]{2,1,0:T(8,128)(2,1)S(1)} all-to-all(bf16[16,20,576]{2,1,0:T(8,128)(2,1)} %get-tuple-element.4), channel_id=1, replica_groups=mesh['group'=2,'chan'=16] {'chan'}, dimensions={0} | all-to-all | bytes 737280 | tf_op jit(solution)/shard_map/all_to_all | solution.py:201
  27.7 0.0 copy-start.1
  27.7 0.1 convert_reduce_fusion
  27.8 0.1 subtract_convert_fusion
  27.9 0.1 pad_maximum_fusion
  27.9 0.8 broadcast_in_dim.2
  28.8 0.0 copy-start.2
  28.8 4.5 %all-to-all-start.1 = ((bf16[16,20,576]{2,1,0:T(8,128)(2,1)}), bf16[16,20,576]{2,1,0:T(8,128)(2,1)S(1)}, u32[]{:S(2)}, u32[]{:S(2)}) async-start(bf16[16,20,576]{2,1,0:T(8,128)(2,1)} %broadcast_in_dim.2), calls=%async_computation.1 | async-start | bytes 983040 | tf_op jit(solution)/shard_map/all_to_all | solution.py:210
  33.3 0.0 copy-done.1
  33.3 1.3 %copy.26.gate_ref = bf16[16,20,1024]{2,1,0:T(8,128)(2,1)} copy(bf16[16,20,1024]{2,0,1:T(8,128)(2,1)S(1)} %copy-done.1) | data formatting | bytes 1310720 | tf_op args[5]
  34.5 0.0 copy-done.2
  34.5 0.0 copy-start.3
  34.5 0.6 negate_multiply_fusion.rest_2_
  35.2 11.6 %all-to-all-done.1 = bf16[16,20,576]{2,1,0:T(8,128)(2,1)S(1)} async-done(((bf16[16,20,576]{2,1,0:T(8,128)(2,1)}), bf16[16,20,576]{2,1,0:T(8,128)(2,1)S(1)}, u32[]{:S(2)}, u32[]{:S(2)}) %all-to-all-start.1) | async-done | bytes 368672 | tf_op jit(solution)/shard_map/all_to_all | solution.py:210
  46.8 0.2 reshape.22
  46.9 0.1 fusion.3
  47.0 0.1 copy.28
  47.1 0.1 copy.29
  47.2 0.2 reshape.24
  47.4 0.0 copy-done
  47.4 0.0 copy-done.3
  47.4 1.0 %compare_select_fusion = f32[320,1024]{1,0:T(8,128)S(1)} fusion(bf16[512,1024]{1,0:T(8,128)(2,1)S(1)} %copy-done, f32[1024]{0:T(1024)S(1)} %copy-done.3, bf16[320,576]{1,0:T(8,128)(2,1)S(1)} %reshape.22), kind=kOutput, calls=%fused_computation | convolution fusion | flops 337838080 | bytes 2691072 | tf_op jit(solution)/shard_map/dot_general | solution.py:219
  48.5 1.3 %reshape.23.rate_ref = f32[16,20,1024]{2,1,0:T(8,128)} reshape(f32[320,1024]{1,0:T(8,128)S(1)} %compare_select_fusion) | data formatting | bytes 2621440 | tf_op jit(solution)/shard_map/reshape | solution.py:220
  49.8 0.8 copy_bitcast_fusion
  50.5 11.4 %shard_map.150 = bf16[16,36,1024]{2,1,0:T(8,128)(2,1)} custom-call(s32[16]{0:T(128)} %lens_ref.1, s32[16]{0:T(128)} %fmap_ref.3, f32[16,20,1024]{2,1,0:T(8,128)} %reshape.23.rate_ref, bf16[16,20,1024]{2,1,0:T(8,128)(2,1)} %get-tuple-element.5.drive_ref, bf16[16,20,1024]{2,1,0:T(8,128)(2,1)} %copy.26.gate_ref, f32[16,16,20]{2,1,0:T(8,128)} %get-tuple-element.13.b_ref, ...), custom_call_target="tpu_custom_call" | custom-call | tf_op jit(solution)/shard_map/pallas_call | solution.py:167
  62.0 36.3 %all_to_all.29 = bf16[16,36,1024]{2,1,0:T(8,128)(2,1)S(1)} all-to-all(bf16[16,36,1024]{2,1,0:T(8,128)(2,1)} %shard_map.150), channel_id=1, replica_groups=mesh['group'=2,'chan'=16] {'chan'}, dimensions={0} | all-to-all | bytes 2359296 | tf_op jit(solution)/shard_map/all_to_all | solution.py:228
  98.2 0.7 copy.27
  98.9 0.6 all_to_all.24
  99.5 0.9 slice.49
  100.5 1.0 %slice_convert_fusion = f32[1,16,16384]{2,1,0:T(8,128)} fusion(bf16[1,36,16384]{2,1,0:T(8,128)(2,1)S(1)} %all_to_all.24), kind=kLoop, calls=%fused_computation.3 | loop fusion | flops 262144 | bytes 1572864 | tf_op jit(solution)/shard_map/convert_element_type | solution.py:229
  (3 shorter events, 0.0 us)
Async XLA Ops:
  0.6 46.8 %copy-start = (bf16[512,1024]{1,0:T(8,128)(2,1)S(1)}, bf16[512,1024]{1,0:T(8,128)(2,1)}, u32[]{:S(2)}) copy-start(bf16[512,1024]{1,0:T(8,128)(2,1)} %param.24) | copy-start | bytes 3145732
  27.7 5.6 %copy-start.1 = (bf16[16,20,1024]{2,0,1:T(8,128)(2,1)S(1)}, bf16[16,20,1024]{2,0,1:T(8,128)(2,1)}, u32[]{:S(2)}) copy-start(bf16[16,20,1024]{2,0,1:T(8,128)(2,1)} %param.19) | copy-start | bytes 1966084
  28.8 5.8 %copy-start.2 = (f32[16,1024]{1,0:T(8,128)S(1)}, f32[16,1024]{1,0:T(8,128)}, u32[]{:S(2)}) copy-start(f32[16,1024]{1,0:T(8,128)} %param.26) | copy-start | bytes 196612
  28.8 18.0 %all-to-all-start.1 = ((bf16[16,20,576]{2,1,0:T(8,128)(2,1)}), bf16[16,20,576]{2,1,0:T(8,128)(2,1)S(1)}, u32[]{:S(2)}, u32[]{:S(2)}) async-start(bf16[16,20,576]{2,1,0:T(8,128)(2,1)} %broadcast_in_dim.2), calls=%async_computation.1 | async-start | bytes 983040 | tf_op jit(solution)/shard_map/all_to_all | solution.py:210
  34.5 12.9 %copy-start.3 = (f32[1024]{0:T(1024)S(1)}, f32[1024]{0:T(1024)}, u32[]{:S(2)}) copy-start(f32[1024]{0:T(1024)} %param.25) | copy-start | bytes 12292

commit v14 on v13

--- a/solution.py
+++ b/solution.py
@@ -102,7 +102,7 @@
 ):
     pair = len(rest) - 6
     h0_refs, (a_ref, skip_ref, packed_ref, r_scr, u_scr, y_scr) = rest[:pair], rest[pair:]
-    positions = rate_ref.shape[1]
+    positions = drive_ref.shape[1]
     state_size = h0_refs[0].shape[1]
     decay = a_ref[...]
     states, lives = [], []
@@ -110,7 +110,7 @@
         live = jnp.clip(lens_ref[pl.program_id(0) * pair + k] + GEN, 0, positions)
         inflow = drive_ref[k].astype(jnp.float32)
         alive = lax.broadcasted_iota(jnp.int32, inflow.shape, 0) < live
-        rate = jnp.where(alive, rate_ref[k], 0.0)
+        rate = jnp.where(alive, rate_ref[k * positions : (k + 1) * positions, :], 0.0)
         r_scr[k] = rate
         u_scr[k] = rate * inflow
         states.append(h0_refs[k][0])
@@ -150,7 +150,7 @@
         num_scalar_prefetch=2,
         grid=(thought_count // pair,),
         in_specs=[
-            pl.BlockSpec((pair, positions, width_local), row_block),
+            pl.BlockSpec((pair * positions, width_local), lambda t, lens, fmap: (t, 0)),
             pl.BlockSpec((pair, positions, width_local), row_block),
             pl.BlockSpec((pair, positions, width_local), row_block),
             pl.BlockSpec((pair, state_size, positions), row_block),
@@ -217,7 +217,7 @@
     ).reshape(thought_count, positions, 2 * state_size)
     step_rate = jax.nn.softplus(
         jnp.dot(rate_low, rate_up, preferred_element_type=jnp.float32) + rate_bias[None, :]
-    ).reshape(thought_count, positions, width_local)
+    )
     b_t = jnp.swapaxes(selection[:, :, :state_size], 1, 2)
     c_t = jnp.swapaxes(selection[:, :, state_size:], 1, 2)
     decay_rate = -jnp.exp(decay_log) * 1.4426950408889634

time: 102 us -> 102 us (level)
  local copies, waits for them, and re-layouts: 7 us -> 5.71 us
  matrix products: 1.02 us -> 2.09 us
    reshape x1 -> x0, local copies, waits for them, and re-layouts: 1.28 us -> none  [body(): step_rate = jax.nn.softplus(jnp.dot(rate_low, rate_up, preferred_element_...]
    dot_general x1, matrix products: 1.02 us -> 2.09 us  [body(): jnp.dot(rate_low, rate_up, preferred_element_type=jnp.float32)]
where the time goes in v14:
time: 102 us; the launch traced here: 101 us
  blocking collectives  57.1 us (56%)
  Pallas kernels  17.6 us (17%)
  waiting for transfers between devices  11.6 us (11%)
  local copies, waits for them, and re-layouts  5.71 us (6%)
  starting transfers between devices  4.52 us (4%)
  matrix products  2.09 us (2%)
  other arithmetic  1.95 us (2%)
    all_to_all x1, blocking collectives, body(): lax.all_to_all(packed_local, 'chan', split_axis=0, concat_axis=2, tiled=T...  36.3 us
    all_to_all x1, blocking collectives, body(): lax.all_to_all(partial.reshape(devices, -1, partial.shape[2]), 'chan', 0,...  20.8 us
    all_to_all x1, waiting for transfers between devices, body(): lax.all_to_all(jnp.broadcast_to(mine[None], (devices,) + mine.shape), 'ch...  11.6 us
    pallas_call x1, Pallas kernels, run_scan(): pl.pallas_call(scan_kernel, grid_spec=grid_spec, out_shape=jax.ShapeDtype...  11.4 us
    pallas_call x1, Pallas kernels, project(): pl.pallas_call(project_kernel, grid_spec=grid_spec, out_shape=(jax.ShapeD...  6.21 us
    all_to_all x1, starting transfers between devices, body(): lax.all_to_all(jnp.broadcast_to(mine[None], (devices,) + mine.shape), 'ch...  4.52 us
    dot_general x1, matrix products, body(): jnp.dot(rate_low, rate_up, preferred_element_type=jnp.float32)  2.09 us
  transfers between devices with their start and end apart: 1, of which 1 were waited for; matrix products, arithmetic and copies ran while one was open for 2% of the time, Pallas kernels for 0%

profile of v14, /device:TPU:1, one launch (start us, length us, event | category | flops | bytes accessed | tf_op | source)
XLA Modules:
  0.0 101.3 jit_solution(10753626491276354156)
XLA Ops:
  0.6 0.0 copy-start
  0.6 6.2 %shard_map.149 = (bf16[16,20,1024]{2,1,0:T(8,128)(2,1)}, bf16[16,20,576]{2,1,0:T(8,128)(2,1)}) custom-call(s32[16]{0:T(128)} %fmap_ref.3, bf16[3,16,1024]{2,1,0:T(8,128)(2,1)} %bitcast.19, bf16[20,16,1024]{2,1,0:T(8,128)(2,1)} %bitcast.18, bf16[4,1024]{1,0:T(4,128)(2,1)} %weight_ref.1, f32[1,1024]{1,0:T(1,128)} %bitcast.21, bf16[1024,512]{1,0:T(8,128)(2,1)} %down_ref.1, ...), custom_call_target="tpu_custom_call" | custom-call | tf_op jit(solution)/shard_map/pallas_call | solution.py:89
  6.9 20.8 %all_to_all.28 = bf16[16,20,576]{2,1,0:T(8,128)(2,1)S(1)} all-to-all(bf16[16,20,576]{2,1,0:T(8,128)(2,1)} %get-tuple-element.4), channel_id=1, replica_groups=mesh['group'=2,'chan'=16] {'chan'}, dimensions={0} | all-to-all | bytes 737280 | tf_op jit(solution)/shard_map/all_to_all | solution.py:201
  27.7 0.0 copy-start.1
  27.7 0.1 convert_reduce_fusion
  27.8 0.1 subtract_convert_fusion
  27.9 0.1 pad_maximum_fusion
  27.9 0.8 broadcast_in_dim.2
  28.8 0.0 copy-start.2
  28.8 4.5 %all-to-all-start.1 = ((bf16[16,20,576]{2,1,0:T(8,128)(2,1)}), bf16[16,20,576]{2,1,0:T(8,128)(2,1)S(1)}, u32[]{:S(2)}, u32[]{:S(2)}) async-start(bf16[16,20,576]{2,1,0:T(8,128)(2,1)} %broadcast_in_dim.2), calls=%async_computation.1 | async-start | bytes 983040 | tf_op jit(solution)/shard_map/all_to_all | solution.py:210
  33.3 0.0 copy-done.1
  33.3 1.3 %copy.26.gate_ref = bf16[16,20,1024]{2,1,0:T(8,128)(2,1)} copy(bf16[16,20,1024]{2,0,1:T(8,128)(2,1)S(1)} %copy-done.1) | data formatting | bytes 1310720 | tf_op args[5]
  34.5 0.0 copy-done.2
  34.5 0.7 negate_multiply_fusion.rest_2_
  35.2 0.0 copy-start.3
  35.2 11.6 %all-to-all-done.1 = bf16[16,20,576]{2,1,0:T(8,128)(2,1)S(1)} async-done(((bf16[16,20,576]{2,1,0:T(8,128)(2,1)}), bf16[16,20,576]{2,1,0:T(8,128)(2,1)S(1)}, u32[]{:S(2)}, u32[]{:S(2)}) %all-to-all-start.1) | async-done | bytes 368672 | tf_op jit(solution)/shard_map/all_to_all | solution.py:210
  46.8 0.2 reshape.19
  46.9 0.1 fusion.3
  47.0 0.1 copy.28
  47.1 0.1 copy.29
  47.2 0.2 reshape.20
  47.4 0.8 copy_bitcast_fusion
  48.2 0.0 copy-done
  48.2 0.0 copy-done.3
  48.2 2.1 %compare_select_fusion.rate_ref = f32[320,1024]{1,0:T(8,128)} fusion(bf16[512,1024]{1,0:T(8,128)(2,1)S(1)} %copy-done, f32[1024]{0:T(1024)S(1)} %copy-done.3, bf16[320,576]{1,0:T(8,128)(2,1)S(1)} %reshape.19), kind=kOutput, calls=%fused_computation | convolution fusion | flops 337838080 | bytes 2691072 | tf_op jit(solution)/shard_map/dot_general | solution.py:219
  50.3 11.4 %shard_map.150 = bf16[16,36,1024]{2,1,0:T(8,128)(2,1)} custom-call(s32[16]{0:T(128)} %lens_ref.1, s32[16]{0:T(128)} %fmap_ref.3, f32[320,1024]{1,0:T(8,128)} %compare_select_fusion.rate_ref, bf16[16,20,1024]{2,1,0:T(8,128)(2,1)} %get-tuple-element.5.drive_ref, bf16[16,20,1024]{2,1,0:T(8,128)(2,1)} %copy.26.gate_ref, f32[16,16,20]{2,1,0:T(8,128)} %get-tuple-element.13.b_ref, ...), custom_call_target="tpu_custom_call" | custom-call | tf_op jit(solution)/shard_map/pallas_call | solution.py:167
  61.7 36.3 %all_to_all.29 = bf16[16,36,1024]{2,1,0:T(8,128)(2,1)S(1)} all-to-all(bf16[16,36,1024]{2,1,0:T(8,128)(2,1)} %shard_map.150), channel_id=1, replica_groups=mesh['group'=2,'chan'=16] {'chan'}, dimensions={0} | all-to-all | bytes 2359296 | tf_op jit(solution)/shard_map/all_to_all | solution.py:228
  98.0 0.7 copy.27
  98.6 0.6 all_to_all.24
  99.3 0.9 slice.49
  100.2 1.0 %slice_convert_fusion = f32[1,16,16384]{2,1,0:T(8,128)} fusion(bf16[1,36,16384]{2,1,0:T(8,128)(2,1)S(1)} %all_to_all.24), kind=kLoop, calls=%fused_computation.3 | loop fusion | flops 262144 | bytes 1572864 | tf_op jit(solution)/shard_map/convert_element_type | solution.py:229
  (3 shorter events, 0.0 us)
Async XLA Ops:
  0.6 47.6 %copy-start = (bf16[512,1024]{1,0:T(8,128)(2,1)S(1)}, bf16[512,1024]{1,0:T(8,128)(2,1)}, u32[]{:S(2)}) copy-start(bf16[512,1024]{1,0:T(8,128)(2,1)} %param.24) | copy-start | bytes 3145732
  27.7 5.6 %copy-start.1 = (bf16[16,20,1024]{2,0,1:T(8,128)(2,1)S(1)}, bf16[16,20,1024]{2,0,1:T(8,128)(2,1)}, u32[]{:S(2)}) copy-start(bf16[16,20,1024]{2,0,1:T(8,128)(2,1)} %param.19) | copy-start | bytes 1966084
  28.8 5.8 %copy-start.2 = (f32[16,1024]{1,0:T(8,128)S(1)}, f32[16,1024]{1,0:T(8,128)}, u32[]{:S(2)}) copy-start(f32[16,1024]{1,0:T(8,128)} %param.26) | copy-start | bytes 196612
  28.8 18.0 %all-to-all-start.1 = ((bf16[16,20,576]{2,1,0:T(8,128)(2,1)}), bf16[16,20,576]{2,1,0:T(8,128)(2,1)S(1)}, u32[]{:S(2)}, u32[]{:S(2)}) async-start(bf16[16,20,576]{2,1,0:T(8,128)(2,1)} %broadcast_in_dim.2), calls=%async_computation.1 | async-start | bytes 983040 | tf_op jit(solution)/shard_map/all_to_all | solution.py:210
  35.2 13.0 %copy-start.3 = (f32[1024]{0:T(1024)S(1)}, f32[1024]{0:T(1024)}, u32[]{:S(2)}) copy-start(f32[1024]{0:T(1024)} %param.25) | copy-start | bytes 12292

commit v15 on v14

--- a/solution.py
+++ b/solution.py
@@ -16,6 +16,7 @@
     taps = weight_ref.shape[0]
     rank = down_ref.shape[1]
     state_twice = select_ref.shape[0]
+    step = pl.program_id(0)
     tap_weights = weight_ref[...].astype(jnp.float32)
     parents = conv_ref.shape[1]
     row = lax.broadcasted_iota(jnp.int32, (thought_count, parents), 0)
@@ -41,19 +42,32 @@
         driven_ref[t] = driven
         rows_scr[t * positions : (t + 1) * positions, :] = driven.astype(jnp.float32)
     token_rows = rows_scr[...].astype(jnp.bfloat16)
-    out_scr[:, :rank] = jnp.dot(token_rows, down_ref[...], preferred_element_type=jnp.float32)
-    out_scr[:, rank:] = lax.dot_general(
+    low = jnp.dot(token_rows, down_ref[...], preferred_element_type=jnp.float32)
+    chosen = lax.dot_general(
         token_rows, select_ref[...], (((1,), (1,)), ((), ())),
         preferred_element_type=jnp.float32,
     )
-    for t in range(thought_count):
-        block = out_scr[t * positions : (t + 1) * positions, :]
-        select_part = block[:, rank:]
-        select_high = select_part.astype(jnp.bfloat16)
-        select_low = (select_part - select_high.astype(jnp.float32)).astype(jnp.bfloat16)
-        partial_ref[t, :, :rank] = block[:, :rank].astype(jnp.bfloat16)
-        partial_ref[t, :, rank : rank + state_twice] = select_high
-        partial_ref[t, :, rank + state_twice :] = select_low
+
+    @pl.when(step == 0)
+    def _():
+        out_scr[:, :rank] = low
+        out_scr[:, rank:] = chosen
+
+    @pl.when(step > 0)
+    def _():
+        out_scr[:, :rank] += low
+        out_scr[:, rank:] += chosen
+
+    @pl.when(step == pl.num_programs(0) - 1)
+    def _():
+        for t in range(thought_count):
+            block = out_scr[t * positions : (t + 1) * positions, :]
+            select_part = block[:, rank:]
+            select_high = select_part.astype(jnp.bfloat16)
+            select_low = (select_part - select_high.astype(jnp.float32)).astype(jnp.bfloat16)
+            partial_ref[t, :, :rank] = block[:, :rank].astype(jnp.bfloat16)
+            partial_ref[t, :, rank : rank + state_twice] = select_high
+            partial_ref[t, :, rank + state_twice :] = select_low
 
 
 def project(parent_conv, fork_map, mixer_input, conv_weight, conv_bias, rate_down,
@@ -64,25 +78,29 @@
     conv_view = jnp.transpose(parent_conv, (1, 0, 2))
     input_view = jnp.transpose(mixer_input, (1, 0, 2))
     select_view = jnp.transpose(selection_weight)
-    full = lambda shape: pl.BlockSpec(shape, lambda i, fmap: (0,) * len(shape))
+    steps = 2 if width_local % 256 == 0 else 1
+    width = width_local // steps
+    parents = conv_view.shape[1]
     grid_spec = pltpu.PrefetchScalarGridSpec(
         num_scalar_prefetch=1,
-        grid=(1,),
+        grid=(steps,),
         in_specs=[
-            full(conv_view.shape),
-            full(input_view.shape),
-            full(conv_weight.shape),
-            full((1, width_local)),
-            full(rate_down.shape),
-            full(select_view.shape),
+            pl.BlockSpec((taps - 1, parents, width), lambda i, fmap: (0, 0, i)),
+            pl.BlockSpec((positions, thought_count, width), lambda i, fmap: (0, 0, i)),
+            pl.BlockSpec((taps, width), lambda i, fmap: (0, i)),
+            pl.BlockSpec((1, width), lambda i, fmap: (0, i)),
+            pl.BlockSpec((width, rank), lambda i, fmap: (i, 0)),
+            pl.BlockSpec((state_twice, width), lambda i, fmap: (0, i)),
         ],
         out_specs=[
-            full(mixer_input.shape),
-            full((thought_count, positions, rank + 2 * state_twice)),
+            pl.BlockSpec((thought_count, positions, width), lambda i, fmap: (0, 0, i)),
+            pl.BlockSpec(
+                (thought_count, positions, rank + 2 * state_twice), lambda i, fmap: (0, 0, 0)
+            ),
         ],
         scratch_shapes=[
-            pltpu.VMEM((taps - 1 + positions, width_local), jnp.float32),
-            pltpu.VMEM((thought_count * positions, width_local), jnp.float32),
+            pltpu.VMEM((taps - 1 + positions, width), jnp.float32),
+            pltpu.VMEM((thought_count * positions, width), jnp.float32),
             pltpu.VMEM((thought_count * positions, rank + state_twice), jnp.float32),
         ],
     )
@@ -93,6 +111,7 @@
             jax.ShapeDtypeStruct(mixer_input.shape, jnp.bfloat16),
             jax.ShapeDtypeStruct((thought_count, positions, rank + 2 * state_twice), jnp.bfloat16),
         ),
+        compiler_params=pltpu.CompilerParams(dimension_semantics=("arbitrary",)),
     )(fork_map, conv_view, input_view, conv_weight, conv_bias.reshape(1, width_local),
       rate_down, select_view)
 

time: 102 us -> 102 us (level)
  no operation moved by 1% of the time
where the time goes in v15:
time: 102 us
  blocking collectives  57.1 us (56%)
  Pallas kernels  17.9 us (18%)
  waiting for transfers between devices  11.6 us (11%)
  local copies, waits for them, and re-layouts  5.71 us (6%)
  starting transfers between devices  4.52 us (4%)
  matrix products  2.09 us (2%)
  other arithmetic  1.95 us (2%)
    all_to_all x1, blocking collectives, body(): lax.all_to_all(packed_local, 'chan', split_axis=0, concat_axis=2, tiled=T...  36.3 us
    all_to_all x1, blocking collectives, body(): lax.all_to_all(partial.reshape(devices, -1, partial.shape[2]), 'chan', 0,...  20.8 us
    all_to_all x1, waiting for transfers between devices, body(): lax.all_to_all(jnp.broadcast_to(mine[None], (devices,) + mine.shape), 'ch...  11.6 us
    pallas_call x1, Pallas kernels, run_scan(): pl.pallas_call(scan_kernel, grid_spec=grid_spec, out_shape=jax.ShapeDtype...  11.4 us
    pallas_call x1, Pallas kernels, project(): pl.pallas_call(project_kernel, grid_spec=grid_spec, out_shape=(jax.ShapeD...  6.51 us
    all_to_all x1, starting transfers between devices, body(): lax.all_to_all(jnp.broadcast_to(mine[None], (devices,) + mine.shape), 'ch...  4.52 us
    dot_general x1, matrix products, body(): jnp.dot(rate_low, rate_up, preferred_element_type=jnp.float32)  2.09 us
  transfers between devices with their start and end apart: 1, of which 1 were waited for; matrix products, arithmetic and copies ran while one was open for 2% of the time, Pallas kernels for 0%

profile of v15, /device:TPU:1, one launch (start us, length us, event | category | flops | bytes accessed | tf_op | source)
XLA Modules:
  0.0 101.5 jit_solution(10577065434042460703)
XLA Ops:
  0.6 0.0 copy-start
  0.6 6.5 %shard_map.149 = (bf16[16,20,1024]{2,1,0:T(8,128)(2,1)}, bf16[16,20,576]{2,1,0:T(8,128)(2,1)}) custom-call(s32[16]{0:T(128)} %fmap_ref.3, bf16[3,16,1024]{2,1,0:T(8,128)(2,1)} %bitcast.19, bf16[20,16,1024]{2,1,0:T(8,128)(2,1)} %bitcast.18, bf16[4,1024]{1,0:T(4,128)(2,1)} %weight_ref.1, f32[1,1024]{1,0:T(1,128)} %bitcast.21, bf16[1024,512]{1,0:T(8,128)(2,1)} %down_ref.1, ...), custom_call_target="tpu_custom_call" | custom-call | tf_op jit(solution)/shard_map/pallas_call | solution.py:107
  7.2 20.8 %all_to_all.28 = bf16[16,20,576]{2,1,0:T(8,128)(2,1)S(1)} all-to-all(bf16[16,20,576]{2,1,0:T(8,128)(2,1)} %get-tuple-element.4), channel_id=1, replica_groups=mesh['group'=2,'chan'=16] {'chan'}, dimensions={0} | all-to-all | bytes 737280 | tf_op jit(solution)/shard_map/all_to_all | solution.py:220
  28.0 0.0 copy-start.1
  28.0 0.1 convert_reduce_fusion
  28.1 0.1 subtract_convert_fusion
  28.2 0.1 pad_maximum_fusion
  28.2 0.8 broadcast_in_dim.2
  29.1 0.0 copy-start.2
  29.1 4.5 %all-to-all-start.1 = ((bf16[16,20,576]{2,1,0:T(8,128)(2,1)}), bf16[16,20,576]{2,1,0:T(8,128)(2,1)S(1)}, u32[]{:S(2)}, u32[]{:S(2)}) async-start(bf16[16,20,576]{2,1,0:T(8,128)(2,1)} %broadcast_in_dim.2), calls=%async_computation.1 | async-start | bytes 983040 | tf_op jit(solution)/shard_map/all_to_all | solution.py:229
  33.6 0.0 copy-done.1
  33.6 1.3 %copy.26.gate_ref = bf16[16,20,1024]{2,1,0:T(8,128)(2,1)} copy(bf16[16,20,1024]{2,0,1:T(8,128)(2,1)S(1)} %copy-done.1) | data formatting | bytes 1310720 | tf_op args[5]
  34.8 0.0 copy-done.2
  34.8 0.7 negate_multiply_fusion.rest_2_
  35.5 0.0 copy-start.3
  35.5 11.6 %all-to-all-done.1 = bf16[16,20,576]{2,1,0:T(8,128)(2,1)S(1)} async-done(((bf16[16,20,576]{2,1,0:T(8,128)(2,1)}), bf16[16,20,576]{2,1,0:T(8,128)(2,1)S(1)}, u32[]{:S(2)}, u32[]{:S(2)}) %all-to-all-start.1) | async-done | bytes 368672 | tf_op jit(solution)/shard_map/all_to_all | solution.py:229
  47.1 0.2 reshape.19
  47.2 0.1 fusion.3
  47.3 0.1 copy.28
  47.4 0.1 copy.29
  47.5 0.2 reshape.20
  47.7 0.8 copy_bitcast_fusion
  48.5 0.0 copy-done
  48.5 0.0 copy-done.3
  48.5 2.1 %compare_select_fusion.rate_ref = f32[320,1024]{1,0:T(8,128)} fusion(bf16[512,1024]{1,0:T(8,128)(2,1)S(1)} %copy-done, f32[1024]{0:T(1024)S(1)} %copy-done.3, bf16[320,576]{1,0:T(8,128)(2,1)S(1)} %reshape.19), kind=kOutput, calls=%fused_computation | convolution fusion | flops 337838080 | bytes 2691072 | tf_op jit(solution)/shard_map/dot_general | solution.py:238
  50.6 11.4 %shard_map.150 = bf16[16,36,1024]{2,1,0:T(8,128)(2,1)} custom-call(s32[16]{0:T(128)} %lens_ref.1, s32[16]{0:T(128)} %fmap_ref.3, f32[320,1024]{1,0:T(8,128)} %compare_select_fusion.rate_ref, bf16[16,20,1024]{2,1,0:T(8,128)(2,1)} %get-tuple-element.5.drive_ref, bf16[16,20,1024]{2,1,0:T(8,128)(2,1)} %copy.26.gate_ref, f32[16,16,20]{2,1,0:T(8,128)} %get-tuple-element.13.b_ref, ...), custom_call_target="tpu_custom_call" | custom-call | tf_op jit(solution)/shard_map/pallas_call | solution.py:186
  62.0 36.3 %all_to_all.29 = bf16[16,36,1024]{2,1,0:T(8,128)(2,1)S(1)} all-to-all(bf16[16,36,1024]{2,1,0:T(8,128)(2,1)} %shard_map.150), channel_id=1, replica_groups=mesh['group'=2,'chan'=16] {'chan'}, dimensions={0} | all-to-all | bytes 2359296 | tf_op jit(solution)/shard_map/all_to_all | solution.py:247
  98.3 0.7 copy.27
  98.9 0.6 all_to_all.24
  99.6 0.9 slice.49
  100.5 1.0 %slice_convert_fusion = f32[1,16,16384]{2,1,0:T(8,128)} fusion(bf16[1,36,16384]{2,1,0:T(8,128)(2,1)S(1)} %all_to_all.24), kind=kLoop, calls=%fused_computation.3 | loop fusion | flops 262144 | bytes 1572864 | tf_op jit(solution)/shard_map/convert_element_type | solution.py:248
  (3 shorter events, 0.0 us)
Async XLA Ops:
  0.6 47.9 %copy-start = (bf16[512,1024]{1,0:T(8,128)(2,1)S(1)}, bf16[512,1024]{1,0:T(8,128)(2,1)}, u32[]{:S(2)}) copy-start(bf16[512,1024]{1,0:T(8,128)(2,1)} %param.24) | copy-start | bytes 3145732
  28.0 5.6 %copy-start.1 = (bf16[16,20,1024]{2,0,1:T(8,128)(2,1)S(1)}, bf16[16,20,1024]{2,0,1:T(8,128)(2,1)}, u32[]{:S(2)}) copy-start(bf16[16,20,1024]{2,0,1:T(8,128)(2,1)} %param.19) | copy-start | bytes 1966084
  29.1 5.8 %copy-start.2 = (f32[16,1024]{1,0:T(8,128)S(1)}, f32[16,1024]{1,0:T(8,128)}, u32[]{:S(2)}) copy-start(f32[16,1024]{1,0:T(8,128)} %param.26) | copy-start | bytes 196612
  29.1 18.0 %all-to-all-start.1 = ((bf16[16,20,576]{2,1,0:T(8,128)(2,1)}), bf16[16,20,576]{2,1,0:T(8,128)(2,1)S(1)}, u32[]{:S(2)}, u32[]{:S(2)}) async-start(bf16[16,20,576]{2,1,0:T(8,128)(2,1)} %broadcast_in_dim.2), calls=%async_computation.1 | async-start | bytes 983040 | tf_op jit(solution)/shard_map/all_to_all | solution.py:229
  35.5 13.0 %copy-start.3 = (f32[1024]{0:T(1024)S(1)}, f32[1024]{0:T(1024)}, u32[]{:S(2)}) copy-start(f32[1024]{0:T(1024)} %param.25) | copy-start | bytes 12292

commit v16 on v14

--- a/solution.py
+++ b/solution.py
@@ -137,7 +137,7 @@
              decay_rate, skip_gain):
     thought_count, positions, width_local = driven.shape
     state_size = parent_state.shape[1]
-    pair = 2 if thought_count % 2 == 0 else 1
+    pair = 4 if thought_count % 4 == 0 else 2
     row_block = lambda t, lens, fmap: (t, 0, 0)
     whole = lambda t, lens, fmap: (0, 0)
 

time: 102 us -> 102 us (level)
  no operation moved by 1% of the time
where the time goes in v16:
time: 102 us; the launch traced here: 101 us
  blocking collectives  57.1 us (56%)
  Pallas kernels  17.5 us (17%)
  waiting for transfers between devices  11.6 us (11%)
  local copies, waits for them, and re-layouts  5.71 us (6%)
  starting transfers between devices  4.52 us (4%)
  matrix products  2.09 us (2%)
  other arithmetic  1.95 us (2%)
    all_to_all x1, blocking collectives, body(): lax.all_to_all(packed_local, 'chan', split_axis=0, concat_axis=2, tiled=T...  36.3 us
    all_to_all x1, blocking collectives, body(): lax.all_to_all(partial.reshape(devices, -1, partial.shape[2]), 'chan', 0,...  20.8 us
    all_to_all x1, waiting for transfers between devices, body(): lax.all_to_all(jnp.broadcast_to(mine[None], (devices,) + mine.shape), 'ch...  11.6 us
    pallas_call x1, Pallas kernels, run_scan(): pl.pallas_call(scan_kernel, grid_spec=grid_spec, out_shape=jax.ShapeDtype...  11.3 us
    pallas_call x1, Pallas kernels, project(): pl.pallas_call(project_kernel, grid_spec=grid_spec, out_shape=(jax.ShapeD...  6.21 us
    all_to_all x1, starting transfers between devices, body(): lax.all_to_all(jnp.broadcast_to(mine[None], (devices,) + mine.shape), 'ch...  4.52 us
    dot_general x1, matrix products, body(): jnp.dot(rate_low, rate_up, preferred_element_type=jnp.float32)  2.09 us
  transfers between devices with their start and end apart: 1, of which 1 were waited for; matrix products, arithmetic and copies ran while one was open for 2% of the time, Pallas kernels for 0%

profile of v16, /device:TPU:1, one launch (start us, length us, event | category | flops | bytes accessed | tf_op | source)
XLA Modules:
  0.0 101.1 jit_solution(4548323165655036215)
XLA Ops:
  0.6 0.0 copy-start
  0.6 6.2 %shard_map.149 = (bf16[16,20,1024]{2,1,0:T(8,128)(2,1)}, bf16[16,20,576]{2,1,0:T(8,128)(2,1)}) custom-call(s32[16]{0:T(128)} %fmap_ref.3, bf16[3,16,1024]{2,1,0:T(8,128)(2,1)} %bitcast.19, bf16[20,16,1024]{2,1,0:T(8,128)(2,1)} %bitcast.18, bf16[4,1024]{1,0:T(4,128)(2,1)} %weight_ref.1, f32[1,1024]{1,0:T(1,128)} %bitcast.21, bf16[1024,512]{1,0:T(8,128)(2,1)} %down_ref.1, ...), custom_call_target="tpu_custom_call" | custom-call | tf_op jit(solution)/shard_map/pallas_call | solution.py:89
  6.9 20.8 %all_to_all.28 = bf16[16,20,576]{2,1,0:T(8,128)(2,1)S(1)} all-to-all(bf16[16,20,576]{2,1,0:T(8,128)(2,1)} %get-tuple-element.4), channel_id=1, replica_groups=mesh['group'=2,'chan'=16] {'chan'}, dimensions={0} | all-to-all | bytes 737280 | tf_op jit(solution)/shard_map/all_to_all | solution.py:201
  27.7 0.0 copy-start.1
  27.7 0.1 convert_reduce_fusion
  27.8 0.1 subtract_convert_fusion
  27.9 0.1 pad_maximum_fusion
  27.9 0.8 broadcast_in_dim.2
  28.8 0.0 copy-start.2
  28.8 4.5 %all-to-all-start.1 = ((bf16[16,20,576]{2,1,0:T(8,128)(2,1)}), bf16[16,20,576]{2,1,0:T(8,128)(2,1)S(1)}, u32[]{:S(2)}, u32[]{:S(2)}) async-start(bf16[16,20,576]{2,1,0:T(8,128)(2,1)} %broadcast_in_dim.2), calls=%async_computation.1 | async-start | bytes 983040 | tf_op jit(solution)/shard_map/all_to_all | solution.py:210
  33.3 0.0 copy-done.1
  33.3 1.3 %copy.26.gate_ref = bf16[16,20,1024]{2,1,0:T(8,128)(2,1)} copy(bf16[16,20,1024]{2,0,1:T(8,128)(2,1)S(1)} %copy-done.1) | data formatting | bytes 1310720 | tf_op args[5]
  34.5 0.0 copy-done.2
  34.5 0.7 negate_multiply_fusion.rest_4_
  35.2 0.0 copy-start.3
  35.2 11.6 %all-to-all-done.1 = bf16[16,20,576]{2,1,0:T(8,128)(2,1)S(1)} async-done(((bf16[16,20,576]{2,1,0:T(8,128)(2,1)}), bf16[16,20,576]{2,1,0:T(8,128)(2,1)S(1)}, u32[]{:S(2)}, u32[]{:S(2)}) %all-to-all-start.1) | async-done | bytes 368672 | tf_op jit(solution)/shard_map/all_to_all | solution.py:210
  46.8 0.2 reshape.19
  46.9 0.1 fusion.3
  47.0 0.1 copy.28
  47.1 0.1 copy.29
  47.2 0.2 reshape.20
  47.4 0.8 copy_bitcast_fusion
  48.2 0.0 copy-done
  48.2 0.0 copy-done.3
  48.2 2.1 %compare_select_fusion.rate_ref = f32[320,1024]{1,0:T(8,128)} fusion(bf16[512,1024]{1,0:T(8,128)(2,1)S(1)} %copy-done, f32[1024]{0:T(1024)S(1)} %copy-done.3, bf16[320,576]{1,0:T(8,128)(2,1)S(1)} %reshape.19), kind=kOutput, calls=%fused_computation | convolution fusion | flops 337838080 | bytes 2691072 | tf_op jit(solution)/shard_map/dot_general | solution.py:219
  50.3 11.3 %shard_map.150 = bf16[16,36,1024]{2,1,0:T(8,128)(2,1)} custom-call(s32[16]{0:T(128)} %lens_ref.1, s32[16]{0:T(128)} %fmap_ref.3, f32[320,1024]{1,0:T(8,128)} %compare_select_fusion.rate_ref, bf16[16,20,1024]{2,1,0:T(8,128)(2,1)} %get-tuple-element.5.drive_ref, bf16[16,20,1024]{2,1,0:T(8,128)(2,1)} %copy.26.gate_ref, f32[16,16,20]{2,1,0:T(8,128)} %get-tuple-element.13.b_ref, ...), custom_call_target="tpu_custom_call" | custom-call | tf_op jit(solution)/shard_map/pallas_call | solution.py:167
  61.6 36.3 %all_to_all.29 = bf16[16,36,1024]{2,1,0:T(8,128)(2,1)S(1)} all-to-all(bf16[16,36,1024]{2,1,0:T(8,128)(2,1)} %shard_map.150), channel_id=1, replica_groups=mesh['group'=2,'chan'=16] {'chan'}, dimensions={0} | all-to-all | bytes 2359296 | tf_op jit(solution)/shard_map/all_to_all | solution.py:228
  97.9 0.7 copy.27
  98.5 0.6 all_to_all.24
  99.2 0.9 slice.49
  100.1 1.0 %slice_convert_fusion = f32[1,16,16384]{2,1,0:T(8,128)} fusion(bf16[1,36,16384]{2,1,0:T(8,128)(2,1)S(1)} %all_to_all.24), kind=kLoop, calls=%fused_computation.3 | loop fusion | flops 262144 | bytes 1572864 | tf_op jit(solution)/shard_map/convert_element_type | solution.py:229
  (3 shorter events, 0.0 us)
Async XLA Ops:
  0.6 47.6 %copy-start = (bf16[512,1024]{1,0:T(8,128)(2,1)S(1)}, bf16[512,1024]{1,0:T(8,128)(2,1)}, u32[]{:S(2)}) copy-start(bf16[512,1024]{1,0:T(8,128)(2,1)} %param.24) | copy-start | bytes 3145732
  27.7 5.6 %copy-start.1 = (bf16[16,20,1024]{2,0,1:T(8,128)(2,1)S(1)}, bf16[16,20,1024]{2,0,1:T(8,128)(2,1)}, u32[]{:S(2)}) copy-start(bf16[16,20,1024]{2,0,1:T(8,128)(2,1)} %param.19) | copy-start | bytes 1966084
  28.8 5.8 %copy-start.2 = (f32[16,1024]{1,0:T(8,128)S(1)}, f32[16,1024]{1,0:T(8,128)}, u32[]{:S(2)}) copy-start(f32[16,1024]{1,0:T(8,128)} %param.26) | copy-start | bytes 196612
  28.8 18.0 %all-to-all-start.1 = ((bf16[16,20,576]{2,1,0:T(8,128)(2,1)}), bf16[16,20,576]{2,1,0:T(8,128)(2,1)S(1)}, u32[]{:S(2)}, u32[]{:S(2)}) async-start(bf16[16,20,576]{2,1,0:T(8,128)(2,1)} %broadcast_in_dim.2), calls=%async_computation.1 | async-start | bytes 983040 | tf_op jit(solution)/shard_map/all_to_all | solution.py:210
  35.2 13.0 %copy-start.3 = (f32[1024]{0:T(1024)S(1)}, f32[1024]{0:T(1024)}, u32[]{:S(2)}) copy-start(f32[1024]{0:T(1024)} %param.25) | copy-start | bytes 12292

commit v17 on v16

--- a/solution.py
+++ b/solution.py
@@ -225,7 +225,12 @@
         judge_lengths, fork_map, step_rate, driven, gate_input, b_t, c_t, parent_state,
         decay_rate, skip_gain,
     )
-    packed = lax.all_to_all(packed_local, "chan", split_axis=0, concat_axis=2, tiled=True)
+    rows = state_size + positions
+    lane_rows = packed_local.reshape(thought_count, rows * width_local // 128, 128)
+    received = lax.all_to_all(lane_rows, "chan", 0, 0, tiled=True).reshape(
+        devices, rows, width_local
+    )
+    packed = jnp.transpose(received, (1, 0, 2)).reshape(1, rows, devices * width_local)
     final_state = packed[:, :state_size].astype(jnp.float32)
     mixer_output = packed[:, state_size:]
     return (mixer_output, final_state)

time: 102 us -> 102 us (level)
  local copies, waits for them, and re-layouts: 5.71 us -> 8.73 us
  blocking collectives: 57.1 us -> 54.4 us
    reshape x0 -> x3, local copies, waits for them, and re-layouts: none -> 3.65 us  [the longest x1 2.37 us: body(): packed_local.reshape(thought_count, rows * width_local // 128, 128)]
    all_to_all x1, blocking collectives: 36.3 us -> 33.6 us  [body(): lax.all_to_all(lane_rows, 'chan', 0, 0, tiled=True)]
    all_to_all x2 -> x0, local copies, waits for them, and re-layouts: 1.29 us -> none  [body(): lax.all_to_all(packed_local, 'chan', split_axis=0, concat_axis=2, tiled=T...]
where the time goes in v17:
time: 102 us; the launch traced here: 101 us
  blocking collectives  54.4 us (53%)
  Pallas kernels  17.5 us (17%)
  waiting for transfers between devices  11.6 us (11%)
  local copies, waits for them, and re-layouts  8.73 us (9%)
  starting transfers between devices  4.52 us (4%)
  matrix products  2.09 us (2%)
  other arithmetic  1.95 us (2%)
    all_to_all x1, blocking collectives, body(): lax.all_to_all(lane_rows, 'chan', 0, 0, tiled=True)  33.6 us
    all_to_all x1, blocking collectives, body(): lax.all_to_all(partial.reshape(devices, -1, partial.shape[2]), 'chan', 0,...  20.8 us
    all_to_all x1, waiting for transfers between devices, body(): lax.all_to_all(jnp.broadcast_to(mine[None], (devices,) + mine.shape), 'ch...  11.6 us
    pallas_call x1, Pallas kernels, run_scan(): pl.pallas_call(scan_kernel, grid_spec=grid_spec, out_shape=jax.ShapeDtype...  11.3 us
    pallas_call x1, Pallas kernels, project(): pl.pallas_call(project_kernel, grid_spec=grid_spec, out_shape=(jax.ShapeD...  6.21 us
    all_to_all x1, starting transfers between devices, body(): lax.all_to_all(jnp.broadcast_to(mine[None], (devices,) + mine.shape), 'ch...  4.52 us
    reshape x1, local copies, waits for them, and re-layouts, body(): packed_local.reshape(thought_count, rows * width_local // 128, 128)  2.37 us
    dot_general x1, matrix products, body(): jnp.dot(rate_low, rate_up, preferred_element_type=jnp.float32)  2.09 us
  transfers between devices with their start and end apart: 1, of which 1 were waited for; matrix products, arithmetic and copies ran while one was open for 2% of the time, Pallas kernels for 0%

profile of v17, /device:TPU:1, one launch (start us, length us, event | category | flops | bytes accessed | tf_op | source)
XLA Modules:
  0.0 101.5 jit_solution(1522926196412232936)
XLA Ops:
  0.6 0.0 copy-start
  0.6 6.2 %shard_map.149 = (bf16[16,20,1024]{2,1,0:T(8,128)(2,1)}, bf16[16,20,576]{2,1,0:T(8,128)(2,1)}) custom-call(s32[16]{0:T(128)} %fmap_ref.3, bf16[3,16,1024]{2,1,0:T(8,128)(2,1)} %bitcast.15, bf16[20,16,1024]{2,1,0:T(8,128)(2,1)} %bitcast.14, bf16[4,1024]{1,0:T(4,128)(2,1)} %weight_ref.1, f32[1,1024]{1,0:T(1,128)} %bitcast.17, bf16[1024,512]{1,0:T(8,128)(2,1)} %down_ref.1, ...), custom_call_target="tpu_custom_call" | custom-call | tf_op jit(solution)/shard_map/pallas_call | solution.py:89
  6.9 20.8 %all_to_all.15 = bf16[16,20,576]{2,1,0:T(8,128)(2,1)S(1)} all-to-all(bf16[16,20,576]{2,1,0:T(8,128)(2,1)} %get-tuple-element.4), channel_id=1, replica_groups=mesh['group'=2,'chan'=16] {'chan'}, dimensions={0} | all-to-all | bytes 737280 | tf_op jit(solution)/shard_map/all_to_all | solution.py:201
  27.7 0.0 copy-start.1
  27.7 0.1 convert_reduce_fusion
  27.8 0.1 subtract_convert_fusion
  27.9 0.1 pad_maximum_fusion
  27.9 0.8 broadcast_in_dim.2
  28.8 0.0 copy-start.2
  28.8 4.5 %all-to-all-start.1 = ((bf16[16,20,576]{2,1,0:T(8,128)(2,1)}), bf16[16,20,576]{2,1,0:T(8,128)(2,1)S(1)}, u32[]{:S(2)}, u32[]{:S(2)}) async-start(bf16[16,20,576]{2,1,0:T(8,128)(2,1)} %broadcast_in_dim.2), calls=%async_computation.1 | async-start | bytes 983040 | tf_op jit(solution)/shard_map/all_to_all | solution.py:210
  33.3 0.0 copy-done.1
  33.3 1.3 %copy.31.gate_ref = bf16[16,20,1024]{2,1,0:T(8,128)(2,1)} copy(bf16[16,20,1024]{2,0,1:T(8,128)(2,1)S(1)} %copy-done.1) | data formatting | bytes 1310720 | tf_op args[5]
  34.5 0.0 copy-done.2
  34.5 0.7 negate_multiply_fusion.rest_4_
  35.2 0.0 copy-start.3
  35.2 11.6 %all-to-all-done.1 = bf16[16,20,576]{2,1,0:T(8,128)(2,1)S(1)} async-done(((bf16[16,20,576]{2,1,0:T(8,128)(2,1)}), bf16[16,20,576]{2,1,0:T(8,128)(2,1)S(1)}, u32[]{:S(2)}, u32[]{:S(2)}) %all-to-all-start.1) | async-done | bytes 368672 | tf_op jit(solution)/shard_map/all_to_all | solution.py:210
  46.8 0.2 reshape.28
  46.9 0.1 fusion.3
  47.0 0.1 copy.33
  47.1 0.1 copy.34
  47.2 0.2 reshape.29
  47.4 0.8 copy_bitcast_fusion
  48.2 0.0 copy-done
  48.2 0.0 copy-done.3
  48.2 2.1 %compare_select_fusion.rate_ref = f32[320,1024]{1,0:T(8,128)} fusion(bf16[512,1024]{1,0:T(8,128)(2,1)S(1)} %copy-done, f32[1024]{0:T(1024)S(1)} %copy-done.3, bf16[320,576]{1,0:T(8,128)(2,1)S(1)} %reshape.28), kind=kOutput, calls=%fused_computation | convolution fusion | flops 337838080 | bytes 2691072 | tf_op jit(solution)/shard_map/dot_general | solution.py:219
  50.3 11.3 %shard_map.150 = bf16[16,36,1024]{2,1,0:T(8,128)(2,1)} custom-call(s32[16]{0:T(128)} %lens_ref.1, s32[16]{0:T(128)} %fmap_ref.3, f32[320,1024]{1,0:T(8,128)} %compare_select_fusion.rate_ref, bf16[16,20,1024]{2,1,0:T(8,128)(2,1)} %get-tuple-element.5.drive_ref, bf16[16,20,1024]{2,1,0:T(8,128)(2,1)} %copy.31.gate_ref, f32[16,16,20]{2,1,0:T(8,128)} %get-tuple-element.13.b_ref, ...), custom_call_target="tpu_custom_call" | custom-call | tf_op jit(solution)/shard_map/pallas_call | solution.py:167
  61.6 2.4 %reshape.31 = bf16[16,288,128]{2,1,0:T(8,128)(2,1)S(1)} reshape(bf16[16,36,1024]{2,1,0:T(8,128)(2,1)} %shard_map.150) | data formatting | bytes 2359296 | tf_op jit(solution)/shard_map/reshape | solution.py:229
  64.0 33.6 %all_to_all.16 = bf16[16,288,128]{2,1,0:T(8,128)(2,1)S(1)} all-to-all(bf16[16,288,128]{2,1,0:T(8,128)(2,1)S(1)} %reshape.31), channel_id=1, replica_groups=mesh['group'=2,'chan'=16] {'chan'}, dimensions={0} | all-to-all | bytes 2359296 | tf_op jit(solution)/shard_map/all_to_all | solution.py:230
  97.5 0.6 reshape.32
  98.2 0.7 copy.32
  98.9 0.6 reshape.33
  99.5 0.9 slice.49
  100.4 1.0 %slice_convert_fusion = f32[1,16,16384]{2,1,0:T(8,128)} fusion(bf16[1,36,16384]{2,1,0:T(8,128)(2,1)S(1)} %reshape.33), kind=kLoop, calls=%fused_computation.3 | loop fusion | flops 262144 | bytes 1572864 | tf_op jit(solution)/shard_map/convert_element_type | solution.py:234
  (3 shorter events, 0.0 us)
Async XLA Ops:
  0.6 47.6 %copy-start = (bf16[512,1024]{1,0:T(8,128)(2,1)S(1)}, bf16[512,1024]{1,0:T(8,128)(2,1)}, u32[]{:S(2)}) copy-start(bf16[512,1024]{1,0:T(8,128)(2,1)} %param.24) | copy-start | bytes 3145732
  27.7 5.6 %copy-start.1 = (bf16[16,20,1024]{2,0,1:T(8,128)(2,1)S(1)}, bf16[16,20,1024]{2,0,1:T(8,128)(2,1)}, u32[]{:S(2)}) copy-start(bf16[16,20,1024]{2,0,1:T(8,128)(2,1)} %param.19) | copy-start | bytes 1966084
  28.8 5.8 %copy-start.2 = (f32[16,1024]{1,0:T(8,128)S(1)}, f32[16,1024]{1,0:T(8,128)}, u32[]{:S(2)}) copy-start(f32[16,1024]{1,0:T(8,128)} %param.26) | copy-start | bytes 196612
  28.8 18.0 %all-to-all-start.1 = ((bf16[16,20,576]{2,1,0:T(8,128)(2,1)}), bf16[16,20,576]{2,1,0:T(8,128)(2,1)S(1)}, u32[]{:S(2)}, u32[]{:S(2)}) async-start(bf16[16,20,576]{2,1,0:T(8,128)(2,1)} %broadcast_in_dim.2), calls=%async_computation.1 | async-start | bytes 983040 | tf_op jit(solution)/shard_map/all_to_all | solution.py:210
  35.2 13.0 %copy-start.3 = (f32[1024]{0:T(1024)S(1)}, f32[1024]{0:T(1024)}, u32[]{:S(2)}) copy-start(f32[1024]{0:T(1024)} %param.25) | copy-start | bytes 12292

commit v18 on v16

--- a/solution.py
+++ b/solution.py
@@ -125,12 +125,28 @@
             h = jnp.exp2(rate_rows * decay) * h + push_rows * b_col
             y_scr[k, p : p + 1, :] = jnp.sum(c_col * h, axis=0, keepdims=True)
             states[k] = h
+    lanes = packed_ref.shape[2]
+    tiles = inflow.shape[1] // lanes
+    tail = positions - state_size
     for k in range(pair):
-        packed_ref[k, :state_size, :] = states[k].astype(packed_ref.dtype)
         inflow = drive_ref[k].astype(jnp.float32)
         gate = gate_ref[k].astype(jnp.float32)
         result = (y_scr[k] + skip_ref[...] * inflow) * jax.nn.silu(gate)
-        packed_ref[k, state_size:, :] = jnp.where(lives[k], result, 0.0).astype(packed_ref.dtype)
+        result = jnp.where(lives[k], result, 0.0)
+        for j in range(tiles):
+            cols = slice(j * lanes, (j + 1) * lanes)
+            base = j * state_size
+            packed_ref[k, base : base + state_size, :] = states[k][:, cols].astype(
+                packed_ref.dtype
+            )
+            base = tiles * state_size + j * state_size
+            packed_ref[k, base : base + state_size, :] = result[:state_size, cols].astype(
+                packed_ref.dtype
+            )
+            base = 2 * tiles * state_size + j * tail
+            packed_ref[k, base : base + tail, :] = result[state_size:, cols].astype(
+                packed_ref.dtype
+            )
 
 
 def run_scan(judge_lengths, fork_map, step_rate, driven, gate_input, b_t, c_t, parent_state,
@@ -161,14 +177,16 @@
             pl.BlockSpec((state_size, width_local), whole),
             pl.BlockSpec((1, width_local), whole),
         ],
-        out_specs=pl.BlockSpec((pair, state_size + positions, width_local), row_block),
+        out_specs=pl.BlockSpec(
+            (pair, (state_size + positions) * width_local // 128, 128), row_block
+        ),
         scratch_shapes=[pltpu.VMEM((pair, positions, width_local), jnp.float32)] * 3,
     )
     return pl.pallas_call(
         scan_kernel,
         grid_spec=grid_spec,
         out_shape=jax.ShapeDtypeStruct(
-            (thought_count, state_size + positions, width_local), jnp.bfloat16
+            (thought_count, (state_size + positions) * width_local // 128, 128), jnp.bfloat16
         ),
         compiler_params=pltpu.CompilerParams(dimension_semantics=("arbitrary",)),
     )(judge_lengths, fork_map, step_rate, driven, gate_input, b_t, c_t,
@@ -225,9 +243,18 @@
         judge_lengths, fork_map, step_rate, driven, gate_input, b_t, c_t, parent_state,
         decay_rate, skip_gain,
     )
-    packed = lax.all_to_all(packed_local, "chan", split_axis=0, concat_axis=2, tiled=True)
-    final_state = packed[:, :state_size].astype(jnp.float32)
-    mixer_output = packed[:, state_size:]
+    received = lax.all_to_all(packed_local, "chan", 0, 0, tiled=True)
+    tiles = width_local // 128
+    tail = positions - state_size
+
+    def unpack(start, rows):
+        block = received[:, start : start + tiles * rows].reshape(devices, tiles, rows, 128)
+        return jnp.transpose(block, (2, 0, 1, 3)).reshape(1, rows, devices * width_local)
+
+    final_state = unpack(0, state_size).astype(jnp.float32)
+    mixer_output = jnp.concatenate(
+        [unpack(tiles * state_size, state_size), unpack(2 * tiles * state_size, tail)], axis=1
+    )
     return (mixer_output, final_state)
 
 

time: 102 us -> 101 us (level)
  blocking collectives: 57.1 us -> 54.6 us
  other arithmetic: 1.95 us -> 2.98 us
    all_to_all x1, blocking collectives: 36.3 us -> 33.8 us  [body(): received = lax.all_to_all(packed_local, 'chan', 0, 0, tiled=True)]
    concatenate x0 -> x1, other arithmetic: none -> 1.99 us  [body(): jnp.concatenate([unpack(tiles * state_size, state_size), unpack(2 * tiles...]
    convert_element_type x0 -> x2, local copies, waits for them, and re-layouts: none -> 1.5 us  [body(): final_state = unpack(0, state_size).astype(jnp.float32)]
    all_to_all x2 -> x0, local copies, waits for them, and re-layouts: 1.29 us -> none  [body(): lax.all_to_all(packed_local, 'chan', split_axis=0, concat_axis=2, tiled=T...]
    reshape x0 -> x1, local copies, waits for them, and re-layouts: none -> 1.02 us  [unpack(): jnp.transpose(block, (2, 0, 1, 3)).reshape(1, rows, devices * width_local)]
where the time goes in v18:
time: 101 us; the launch traced here: 100 us
  blocking collectives  54.6 us (54%)
  Pallas kernels  17.6 us (17%)
  waiting for transfers between devices  11.6 us (11%)
  local copies, waits for them, and re-layouts  6.29 us (6%)
  starting transfers between devices  4.52 us (4%)
  other arithmetic  2.98 us (3%)
  matrix products  2.1 us (2%)
    all_to_all x1, blocking collectives, body(): received = lax.all_to_all(packed_local, 'chan', 0, 0, tiled=True)  33.8 us
    all_to_all x1, blocking collectives, body(): lax.all_to_all(partial.reshape(devices, -1, partial.shape[2]), 'chan', 0,...  20.8 us
    all_to_all x1, waiting for transfers between devices, body(): lax.all_to_all(jnp.broadcast_to(mine[None], (devices,) + mine.shape), 'ch...  11.6 us
    pallas_call x1, Pallas kernels, run_scan(): pl.pallas_call(scan_kernel, grid_spec=grid_spec, out_shape=jax.ShapeDtype...  11.3 us
    pallas_call x1, Pallas kernels, project(): pl.pallas_call(project_kernel, grid_spec=grid_spec, out_shape=(jax.ShapeD...  6.21 us
    all_to_all x1, starting transfers between devices, body(): lax.all_to_all(jnp.broadcast_to(mine[None], (devices,) + mine.shape), 'ch...  4.52 us
    dot_general x1, matrix products, body(): jnp.dot(rate_low, rate_up, preferred_element_type=jnp.float32)  2.1 us
  transfers between devices with their start and end apart: 1, of which 1 were waited for; matrix products, arithmetic and copies ran while one was open for 2% of the time, Pallas kernels for 0%

profile of v18, /device:TPU:1, one launch (start us, length us, event | category | flops | bytes accessed | tf_op | source)
XLA Modules:
  0.0 100.4 jit_solution(5216674705550151700)
XLA Ops:
  0.6 0.0 copy-start
  0.6 6.2 %shard_map.149 = (bf16[16,20,1024]{2,1,0:T(8,128)(2,1)}, bf16[16,20,576]{2,1,0:T(8,128)(2,1)}) custom-call(s32[16]{0:T(128)} %fmap_ref.3, bf16[3,16,1024]{2,1,0:T(8,128)(2,1)} %bitcast.32, bf16[20,16,1024]{2,1,0:T(8,128)(2,1)} %bitcast.30, bf16[4,1024]{1,0:T(4,128)(2,1)} %weight_ref.1, f32[1,1024]{1,0:T(1,128)} %bitcast.34, bf16[1024,512]{1,0:T(8,128)(2,1)} %down_ref.1, ...), custom_call_target="tpu_custom_call" | custom-call | tf_op jit(solution)/shard_map/pallas_call | solution.py:89
  6.9 20.8 %all_to_all.15 = bf16[16,20,576]{2,1,0:T(8,128)(2,1)S(1)} all-to-all(bf16[16,20,576]{2,1,0:T(8,128)(2,1)} %get-tuple-element.4), channel_id=1, replica_groups=mesh['group'=2,'chan'=16] {'chan'}, dimensions={0} | all-to-all | bytes 737280 | tf_op jit(solution)/shard_map/all_to_all | solution.py:219
  27.7 0.0 copy-start.1
  27.7 0.1 convert_reduce_fusion
  27.8 0.1 subtract_convert_fusion
  27.9 0.1 pad_maximum_fusion.1
  27.9 0.8 broadcast_in_dim.2
  28.8 0.0 copy-start.2
  28.8 4.5 %all-to-all-start.1 = ((bf16[16,20,576]{2,1,0:T(8,128)(2,1)}), bf16[16,20,576]{2,1,0:T(8,128)(2,1)S(1)}, u32[]{:S(2)}, u32[]{:S(2)}) async-start(bf16[16,20,576]{2,1,0:T(8,128)(2,1)} %broadcast_in_dim.2), calls=%async_computation.1 | async-start | bytes 983040 | tf_op jit(solution)/shard_map/all_to_all | solution.py:228
  33.3 0.0 copy-done.1
  33.3 1.3 %copy.29.gate_ref = bf16[16,20,1024]{2,1,0:T(8,128)(2,1)} copy(bf16[16,20,1024]{2,0,1:T(8,128)(2,1)S(1)} %copy-done.1) | data formatting | bytes 1310720 | tf_op args[5]
  34.5 0.0 copy-done.2
  34.5 0.6 negate_multiply_fusion.rest_4_
  35.2 0.0 copy-start.3
  35.2 11.6 %all-to-all-done.1 = bf16[16,20,576]{2,1,0:T(8,128)(2,1)S(1)} async-done(((bf16[16,20,576]{2,1,0:T(8,128)(2,1)}), bf16[16,20,576]{2,1,0:T(8,128)(2,1)S(1)}, u32[]{:S(2)}, u32[]{:S(2)}) %all-to-all-start.1) | async-done | bytes 368672 | tf_op jit(solution)/shard_map/all_to_all | solution.py:228
  46.8 0.2 reshape.49
  46.9 0.1 fusion.4
  47.0 0.1 copy.32
  47.1 0.1 copy.33
  47.2 0.2 reshape.50
  47.4 0.8 copy_bitcast_fusion
  48.2 0.0 copy-done
  48.2 0.0 copy-done.3
  48.2 2.1 %compare_select_fusion.rate_ref = f32[320,1024]{1,0:T(8,128)} fusion(bf16[512,1024]{1,0:T(8,128)(2,1)S(1)} %copy-done, f32[1024]{0:T(1024)S(1)} %copy-done.3, bf16[320,576]{1,0:T(8,128)(2,1)S(1)} %reshape.49), kind=kOutput, calls=%fused_computation | convolution fusion | flops 337838080 | bytes 2691072 | tf_op jit(solution)/shard_map/dot_general | solution.py:237
  50.3 11.3 %shard_map.150 = bf16[16,288,128]{2,1,0:T(8,128)(2,1)} custom-call(s32[16]{0:T(128)} %lens_ref.1, s32[16]{0:T(128)} %fmap_ref.3, f32[320,1024]{1,0:T(8,128)} %compare_select_fusion.rate_ref, bf16[16,20,1024]{2,1,0:T(8,128)(2,1)} %get-tuple-element.5.drive_ref, bf16[16,20,1024]{2,1,0:T(8,128)(2,1)} %copy.29.gate_ref, f32[16,16,20]{2,1,0:T(8,128)} %get-tuple-element.15.b_ref, ...), custom_call_target="tpu_custom_call" | custom-call | tf_op jit(solution)/shard_map/pallas_call | solution.py:185
  61.7 33.8 %all_to_all.16 = bf16[16,288,128]{2,1,0:T(8,128)(2,1)S(1)} all-to-all(bf16[16,288,128]{2,1,0:T(8,128)(2,1)} %shard_map.150), channel_id=1, replica_groups=mesh['group'=2,'chan'=16] {'chan'}, dimensions={0} | all-to-all | bytes 2359296 | tf_op jit(solution)/shard_map/all_to_all | solution.py:246
  95.4 0.1 fusion.3
  95.6 0.1 copy.30
  95.7 1.0 %reshape.53 = bf16[1,16,16384]{2,1,0:T(8,128)(2,1)} reshape(bf16[16,16,8,128]{3,2,1,0:T(8,128)(2,1)S(1)} %copy.30) | data formatting | bytes 1048576 | tf_op jit(solution)/shard_map/reshape | solution.py:252
  96.7 0.1 convert_bitcast_fusion
  96.8 0.3 copy.31
  97.2 1.2 %reshape.56 = f32[1,16,16384]{2,1,0:T(8,128)} reshape(f32[16,16,8,128]{3,2,1,0:T(8,128)S(1)} %copy.31) | data formatting | bytes 2097152 | tf_op jit(solution)/shard_map/convert_element_type | solution.py:254
  98.4 2.0 %pad_maximum_fusion = bf16[1,20,16384]{2,1,0:T(8,128)(2,1)} fusion(bf16[1,4,16384]{2,1,0:T(4,128)(2,1)S(1)} %bitcast.31, bf16[1,16,16384]{2,1,0:T(8,128)(2,1)} %reshape.53), kind=kLoop, calls=%fused_computation.4 | loop fusion | flops 1310720 | bytes 1310720 | tf_op jit(solution)/shard_map/concatenate | solution.py:255
  (4 shorter events, 0.0 us)
Async XLA Ops:
  0.6 47.6 %copy-start = (bf16[512,1024]{1,0:T(8,128)(2,1)S(1)}, bf16[512,1024]{1,0:T(8,128)(2,1)}, u32[]{:S(2)}) copy-start(bf16[512,1024]{1,0:T(8,128)(2,1)} %param.24) | copy-start | bytes 3145732
  27.7 5.6 %copy-start.1 = (bf16[16,20,1024]{2,0,1:T(8,128)(2,1)S(1)}, bf16[16,20,1024]{2,0,1:T(8,128)(2,1)}, u32[]{:S(2)}) copy-start(bf16[16,20,1024]{2,0,1:T(8,128)(2,1)} %param.19) | copy-start | bytes 1966084
  28.8 5.8 %copy-start.2 = (f32[16,1024]{1,0:T(8,128)S(1)}, f32[16,1024]{1,0:T(8,128)}, u32[]{:S(2)}) copy-start(f32[16,1024]{1,0:T(8,128)} %param.26) | copy-start | bytes 196612
  28.8 18.0 %all-to-all-start.1 = ((bf16[16,20,576]{2,1,0:T(8,128)(2,1)}), bf16[16,20,576]{2,1,0:T(8,128)(2,1)S(1)}, u32[]{:S(2)}, u32[]{:S(2)}) async-start(bf16[16,20,576]{2,1,0:T(8,128)(2,1)} %broadcast_in_dim.2), calls=%async_computation.1 | async-start | bytes 983040 | tf_op jit(solution)/shard_map/all_to_all | solution.py:228
  35.2 13.1 %copy-start.3 = (f32[1024]{0:T(1024)S(1)}, f32[1024]{0:T(1024)}, u32[]{:S(2)}) copy-start(f32[1024]{0:T(1024)} %param.25) | copy-start | bytes 12292

commit v19 on v18

--- a/solution.py
+++ b/solution.py
@@ -127,7 +127,6 @@
             states[k] = h
     lanes = packed_ref.shape[2]
     tiles = inflow.shape[1] // lanes
-    tail = positions - state_size
     for k in range(pair):
         inflow = drive_ref[k].astype(jnp.float32)
         gate = gate_ref[k].astype(jnp.float32)
@@ -139,14 +138,8 @@
             packed_ref[k, base : base + state_size, :] = states[k][:, cols].astype(
                 packed_ref.dtype
             )
-            base = tiles * state_size + j * state_size
-            packed_ref[k, base : base + state_size, :] = result[:state_size, cols].astype(
-                packed_ref.dtype
-            )
-            base = 2 * tiles * state_size + j * tail
-            packed_ref[k, base : base + tail, :] = result[state_size:, cols].astype(
-                packed_ref.dtype
-            )
+            base = tiles * state_size + j * positions
+            packed_ref[k, base : base + positions, :] = result[:, cols].astype(packed_ref.dtype)
 
 
 def run_scan(judge_lengths, fork_map, step_rate, driven, gate_input, b_t, c_t, parent_state,
@@ -245,16 +238,13 @@
     )
     received = lax.all_to_all(packed_local, "chan", 0, 0, tiled=True)
     tiles = width_local // 128
-    tail = positions - state_size
 
     def unpack(start, rows):
         block = received[:, start : start + tiles * rows].reshape(devices, tiles, rows, 128)
         return jnp.transpose(block, (2, 0, 1, 3)).reshape(1, rows, devices * width_local)
 
     final_state = unpack(0, state_size).astype(jnp.float32)
-    mixer_output = jnp.concatenate(
-        [unpack(tiles * state_size, state_size), unpack(2 * tiles * state_size, tail)], axis=1
-    )
+    mixer_output = unpack(tiles * state_size, positions)
     return (mixer_output, final_state)
 
 

time: 101 us -> 99.9 us (0.989)
  other arithmetic: 2.98 us -> 1 us
    concatenate x1 -> x0, other arithmetic: 1.99 us -> none  [body(): jnp.concatenate([unpack(tiles * state_size, state_size), unpack(2 * tiles...]
where the time goes in v19:
time: 99.9 us; the launch traced here: 99.3 us
  blocking collectives  54.6 us (55%)
  Pallas kernels  17.7 us (18%)
  waiting for transfers between devices  11.6 us (12%)
  local copies, waits for them, and re-layouts  7.02 us (7%)
  starting transfers between devices  4.52 us (5%)
  matrix products  2.09 us (2%)
  other arithmetic  1 us (1%)
    all_to_all x1, blocking collectives, body(): received = lax.all_to_all(packed_local, 'chan', 0, 0, tiled=True)  33.8 us
    all_to_all x1, blocking collectives, body(): lax.all_to_all(partial.reshape(devices, -1, partial.shape[2]), 'chan', 0,...  20.8 us
    all_to_all x1, waiting for transfers between devices, body(): lax.all_to_all(jnp.broadcast_to(mine[None], (devices,) + mine.shape), 'ch...  11.6 us
    pallas_call x1, Pallas kernels, run_scan(): pl.pallas_call(scan_kernel, grid_spec=grid_spec, out_shape=jax.ShapeDtype...  11.5 us
    pallas_call x1, Pallas kernels, project(): pl.pallas_call(project_kernel, grid_spec=grid_spec, out_shape=(jax.ShapeD...  6.21 us
    all_to_all x1, starting transfers between devices, body(): lax.all_to_all(jnp.broadcast_to(mine[None], (devices,) + mine.shape), 'ch...  4.52 us
    dot_general x1, matrix products, body(): jnp.dot(rate_low, rate_up, preferred_element_type=jnp.float32)  2.09 us
  transfers between devices with their start and end apart: 1, of which 1 were waited for; matrix products, arithmetic and copies ran while one was open for 2% of the time, Pallas kernels for 0%

profile of v19, /device:TPU:1, one launch (start us, length us, event | category | flops | bytes accessed | tf_op | source)
XLA Modules:
  0.0 99.3 jit_solution(10960515524182319425)
XLA Ops:
  0.6 0.0 copy-start
  0.6 6.2 %shard_map.149 = (bf16[16,20,1024]{2,1,0:T(8,128)(2,1)}, bf16[16,20,576]{2,1,0:T(8,128)(2,1)}) custom-call(s32[16]{0:T(128)} %fmap_ref.3, bf16[3,16,1024]{2,1,0:T(8,128)(2,1)} %bitcast.26, bf16[20,16,1024]{2,1,0:T(8,128)(2,1)} %bitcast.25, bf16[4,1024]{1,0:T(4,128)(2,1)} %weight_ref.1, f32[1,1024]{1,0:T(1,128)} %bitcast.28, bf16[1024,512]{1,0:T(8,128)(2,1)} %down_ref.1, ...), custom_call_target="tpu_custom_call" | custom-call | tf_op jit(solution)/shard_map/pallas_call | solution.py:89
  6.9 20.8 %all_to_all.15 = bf16[16,20,576]{2,1,0:T(8,128)(2,1)S(1)} all-to-all(bf16[16,20,576]{2,1,0:T(8,128)(2,1)} %get-tuple-element.4), channel_id=1, replica_groups=mesh['group'=2,'chan'=16] {'chan'}, dimensions={0} | all-to-all | bytes 737280 | tf_op jit(solution)/shard_map/all_to_all | solution.py:212
  27.7 0.0 copy-start.1
  27.7 0.1 convert_reduce_fusion
  27.8 0.1 subtract_convert_fusion
  27.9 0.1 pad_maximum_fusion
  27.9 0.8 broadcast_in_dim.2
  28.8 0.0 copy-start.2
  28.8 4.5 %all-to-all-start.1 = ((bf16[16,20,576]{2,1,0:T(8,128)(2,1)}), bf16[16,20,576]{2,1,0:T(8,128)(2,1)S(1)}, u32[]{:S(2)}, u32[]{:S(2)}) async-start(bf16[16,20,576]{2,1,0:T(8,128)(2,1)} %broadcast_in_dim.2), calls=%async_computation.1 | async-start | bytes 983040 | tf_op jit(solution)/shard_map/all_to_all | solution.py:221
  33.3 0.0 copy-done.1
  33.3 1.3 %copy.36.gate_ref = bf16[16,20,1024]{2,1,0:T(8,128)(2,1)} copy(bf16[16,20,1024]{2,0,1:T(8,128)(2,1)S(1)} %copy-done.1) | data formatting | bytes 1310720 | tf_op args[5]
  34.5 0.0 copy-done.2
  34.5 0.6 negate_multiply_fusion.rest_4_
  35.2 0.0 copy-start.3
  35.2 11.6 %all-to-all-done.1 = bf16[16,20,576]{2,1,0:T(8,128)(2,1)S(1)} async-done(((bf16[16,20,576]{2,1,0:T(8,128)(2,1)}), bf16[16,20,576]{2,1,0:T(8,128)(2,1)S(1)}, u32[]{:S(2)}, u32[]{:S(2)}) %all-to-all-start.1) | async-done | bytes 368672 | tf_op jit(solution)/shard_map/all_to_all | solution.py:221
  46.8 0.2 reshape.43
  46.9 0.1 fusion.3
  47.0 0.1 copy.40
  47.1 0.1 copy.41
  47.2 0.2 reshape.44
  47.4 0.8 copy_bitcast_fusion
  48.2 0.0 copy-done
  48.2 0.0 copy-done.3
  48.2 2.1 %compare_select_fusion.rate_ref = f32[320,1024]{1,0:T(8,128)} fusion(bf16[512,1024]{1,0:T(8,128)(2,1)S(1)} %copy-done, f32[1024]{0:T(1024)S(1)} %copy-done.3, bf16[320,576]{1,0:T(8,128)(2,1)S(1)} %reshape.43), kind=kOutput, calls=%fused_computation | convolution fusion | flops 337838080 | bytes 2691072 | tf_op jit(solution)/shard_map/dot_general | solution.py:230
  50.3 11.5 %shard_map.150 = bf16[16,288,128]{2,1,0:T(8,128)(2,1)} custom-call(s32[16]{0:T(128)} %lens_ref.1, s32[16]{0:T(128)} %fmap_ref.3, f32[320,1024]{1,0:T(8,128)} %compare_select_fusion.rate_ref, bf16[16,20,1024]{2,1,0:T(8,128)(2,1)} %get-tuple-element.5.drive_ref, bf16[16,20,1024]{2,1,0:T(8,128)(2,1)} %copy.36.gate_ref, f32[16,16,20]{2,1,0:T(8,128)} %get-tuple-element.13.b_ref, ...), custom_call_target="tpu_custom_call" | custom-call | tf_op jit(solution)/shard_map/pallas_call | solution.py:178
  61.8 33.8 %all_to_all.16 = bf16[16,288,128]{2,1,0:T(8,128)(2,1)S(1)} all-to-all(bf16[16,288,128]{2,1,0:T(8,128)(2,1)} %shard_map.150), channel_id=1, replica_groups=mesh['group'=2,'chan'=16] {'chan'}, dimensions={0} | all-to-all | bytes 2359296 | tf_op jit(solution)/shard_map/all_to_all | solution.py:239
  95.7 0.3 copy.37
  95.9 0.4 copy.38
  96.4 1.3 %reshape.47 = bf16[1,20,16384]{2,1,0:T(8,128)(2,1)} reshape(bf16[20,16,8,128]{3,2,1,0:T(8,128)(2,1)S(1)} %copy.38) | data formatting | bytes 1310720 | tf_op jit(solution)/shard_map/reshape | solution.py:244
  97.7 0.1 convert_bitcast_fusion
  97.8 0.3 copy.39
  98.1 1.2 %reshape.48 = f32[1,16,16384]{2,1,0:T(8,128)} reshape(f32[16,16,8,128]{3,2,1,0:T(8,128)S(1)} %copy.39) | data formatting | bytes 2097152 | tf_op jit(solution)/shard_map/convert_element_type | solution.py:246
  (5 shorter events, 0.1 us)
Async XLA Ops:
  0.6 47.6 %copy-start = (bf16[512,1024]{1,0:T(8,128)(2,1)S(1)}, bf16[512,1024]{1,0:T(8,128)(2,1)}, u32[]{:S(2)}) copy-start(bf16[512,1024]{1,0:T(8,128)(2,1)} %param.24) | copy-start | bytes 3145732
  27.7 5.6 %copy-start.1 = (bf16[16,20,1024]{2,0,1:T(8,128)(2,1)S(1)}, bf16[16,20,1024]{2,0,1:T(8,128)(2,1)}, u32[]{:S(2)}) copy-start(bf16[16,20,1024]{2,0,1:T(8,128)(2,1)} %param.19) | copy-start | bytes 1966084
  28.8 5.8 %copy-start.2 = (f32[16,1024]{1,0:T(8,128)S(1)}, f32[16,1024]{1,0:T(8,128)}, u32[]{:S(2)}) copy-start(f32[16,1024]{1,0:T(8,128)} %param.26) | copy-start | bytes 196612
  28.8 18.0 %all-to-all-start.1 = ((bf16[16,20,576]{2,1,0:T(8,128)(2,1)}), bf16[16,20,576]{2,1,0:T(8,128)(2,1)S(1)}, u32[]{:S(2)}, u32[]{:S(2)}) async-start(bf16[16,20,576]{2,1,0:T(8,128)(2,1)} %broadcast_in_dim.2), calls=%async_computation.1 | async-start | bytes 983040 | tf_op jit(solution)/shard_map/all_to_all | solution.py:221
  35.2 13.1 %copy-start.3 = (f32[1024]{0:T(1024)S(1)}, f32[1024]{0:T(1024)}, u32[]{:S(2)}) copy-start(f32[1024]{0:T(1024)} %param.25) | copy-start | bytes 12292

commit v20 on v19

--- a/solution.py
+++ b/solution.py
@@ -46,14 +46,23 @@
         token_rows, select_ref[...], (((1,), (1,)), ((), ())),
         preferred_element_type=jnp.float32,
     )
+    lanes = partial_ref.shape[2]
+    quarters = rank // lanes
+    base = quarters * positions
     for t in range(thought_count):
         block = out_scr[t * positions : (t + 1) * positions, :]
         select_part = block[:, rank:]
         select_high = select_part.astype(jnp.bfloat16)
         select_low = (select_part - select_high.astype(jnp.float32)).astype(jnp.bfloat16)
-        partial_ref[t, :, :rank] = block[:, :rank].astype(jnp.bfloat16)
-        partial_ref[t, :, rank : rank + state_twice] = select_high
-        partial_ref[t, :, rank + state_twice :] = select_low
+        for j in range(quarters):
+            partial_ref[t, j * positions : (j + 1) * positions, :] = block[
+                :, j * lanes : (j + 1) * lanes
+            ].astype(jnp.bfloat16)
+        partial_ref[t, base : base + positions, 2 * state_twice :] = jnp.zeros(
+            (positions, lanes - 2 * state_twice), jnp.bfloat16
+        )
+        partial_ref[t, base : base + positions, :state_twice] = select_high
+        partial_ref[t, base : base + positions, state_twice : 2 * state_twice] = select_low
 
 
 def project(parent_conv, fork_map, mixer_input, conv_weight, conv_bias, rate_down,
@@ -78,7 +87,7 @@
         ],
         out_specs=[
             full(mixer_input.shape),
-            full((thought_count, positions, rank + 2 * state_twice)),
+            full((thought_count, (rank // 128 + 1) * positions, 128)),
         ],
         scratch_shapes=[
             pltpu.VMEM((taps - 1 + positions, width_local), jnp.float32),
@@ -91,7 +100,9 @@
         grid_spec=grid_spec,
         out_shape=(
             jax.ShapeDtypeStruct(mixer_input.shape, jnp.bfloat16),
-            jax.ShapeDtypeStruct((thought_count, positions, rank + 2 * state_twice), jnp.bfloat16),
+            jax.ShapeDtypeStruct(
+                (thought_count, (rank // 128 + 1) * positions, 128), jnp.bfloat16
+            ),
         ),
     )(fork_map, conv_view, input_view, conv_weight, conv_bias.reshape(1, width_local),
       rate_down, select_view)
@@ -209,12 +220,14 @@
         parent_conv, fork_map, mixer_input, conv_weight, conv_bias, rate_down, selection_weight
     )
     devices = lax.axis_size("chan")
-    pieces = lax.all_to_all(
-        partial.reshape(devices, -1, partial.shape[2]), "chan", 0, 0, tiled=True
-    ).astype(jnp.float32)
+    pieces = lax.all_to_all(partial, "chan", 0, 0, tiled=True).astype(jnp.float32)
     reduced = jnp.sum(pieces, axis=0)
-    low_mine = reduced[:, :rank].astype(jnp.bfloat16)
-    select_sum = reduced[:, rank : rank + 2 * state_size] + reduced[:, rank + 2 * state_size :]
+    quarters = rank // 128
+    low_mine = jnp.transpose(
+        reduced[: quarters * positions].reshape(quarters, positions, 128), (1, 0, 2)
+    ).reshape(positions, rank).astype(jnp.bfloat16)
+    select_rows = reduced[quarters * positions :]
+    select_sum = select_rows[:, : 2 * state_size] + select_rows[:, 2 * state_size : 4 * state_size]
     select_high = select_sum.astype(jnp.bfloat16)
     select_low = (select_sum - select_high.astype(jnp.float32)).astype(jnp.bfloat16)
     mine = jnp.concatenate([low_mine, select_high, select_low], axis=1)

time: 99.9 us -> 98.4 us (0.985)
  blocking collectives: 54.6 us -> 53.5 us
    all_to_all x1, blocking collectives: 20.8 us -> 19.8 us  [body(): lax.all_to_all(partial, 'chan', 0, 0, tiled=True).astype(jnp.float32)]
where the time goes in v20:
time: 98.4 us; the launch traced here: 97.8 us
  blocking collectives  53.5 us (54%)
  Pallas kernels  17.6 us (18%)
  waiting for transfers between devices  11.6 us (12%)
  local copies, waits for them, and re-layouts  7.06 us (7%)
  starting transfers between devices  4.13 us (4%)
  matrix products  2.09 us (2%)
    all_to_all x1, blocking collectives, body(): received = lax.all_to_all(packed_local, 'chan', 0, 0, tiled=True)  33.8 us
    all_to_all x1, blocking collectives, body(): lax.all_to_all(partial, 'chan', 0, 0, tiled=True).astype(jnp.float32)  19.8 us
    all_to_all x1, waiting for transfers between devices, body(): lax.all_to_all(jnp.broadcast_to(mine[None], (devices,) + mine.shape), 'ch...  11.6 us
    pallas_call x1, Pallas kernels, run_scan(): pl.pallas_call(scan_kernel, grid_spec=grid_spec, out_shape=jax.ShapeDtype...  11.5 us
    pallas_call x1, Pallas kernels, project(): pl.pallas_call(project_kernel, grid_spec=grid_spec, out_shape=(jax.ShapeD...  6.18 us
    all_to_all x1, starting transfers between devices, body(): lax.all_to_all(jnp.broadcast_to(mine[None], (devices,) + mine.shape), 'ch...  4.13 us
    dot_general x1, matrix products, body(): jnp.dot(rate_low, rate_up, preferred_element_type=jnp.float32)  2.09 us
  transfers between devices with their start and end apart: 1, of which 1 were waited for; matrix products, arithmetic and copies ran while one was open for 2% of the time, Pallas kernels for 0%

profile of v20, /device:TPU:1, one launch (start us, length us, event | category | flops | bytes accessed | tf_op | source)
XLA Modules:
  0.0 97.8 jit_solution(1933689981809276969)
XLA Ops:
  0.6 0.0 copy-start
  0.6 6.2 %shard_map.149 = (bf16[16,20,1024]{2,1,0:T(8,128)(2,1)}, bf16[16,100,128]{2,1,0:T(8,128)(2,1)}) custom-call(s32[16]{0:T(128)} %fmap_ref.3, bf16[3,16,1024]{2,1,0:T(8,128)(2,1)} %bitcast.30, bf16[20,16,1024]{2,1,0:T(8,128)(2,1)} %bitcast.29, bf16[4,1024]{1,0:T(4,128)(2,1)} %weight_ref.1, f32[1,1024]{1,0:T(1,128)} %bitcast.35, bf16[1024,512]{1,0:T(8,128)(2,1)} %down_ref.1, ...), custom_call_target="tpu_custom_call" | custom-call | tf_op jit(solution)/shard_map/pallas_call | solution.py:98
  6.8 19.8 %all_to_all.15 = bf16[16,100,128]{2,1,0:T(8,128)(2,1)S(1)} all-to-all(bf16[16,100,128]{2,1,0:T(8,128)(2,1)} %get-tuple-element.4), channel_id=1, replica_groups=mesh['group'=2,'chan'=16] {'chan'}, dimensions={0} | all-to-all | bytes 819200 | tf_op jit(solution)/shard_map/all_to_all | solution.py:223
  26.6 0.0 copy-start.1
  26.6 0.1 convert_reduce_fusion
  26.7 0.1 subtract_convert_fusion
  26.8 0.1 pad_maximum_fusion
  26.9 0.8 broadcast_in_dim.2
  27.7 0.0 copy-start.2
  27.7 4.1 %all-to-all-start.1 = ((bf16[16,20,576]{2,1,0:T(8,128)(2,1)}), bf16[16,20,576]{2,1,0:T(8,128)(2,1)S(1)}, u32[]{:S(2)}, u32[]{:S(2)}) async-start(bf16[16,20,576]{2,1,0:T(8,128)(2,1)} %broadcast_in_dim.2), calls=%async_computation.1 | async-start | bytes 983040 | tf_op jit(solution)/shard_map/all_to_all | solution.py:234
  31.8 0.0 copy-done.1
  31.8 1.3 %copy.39.gate_ref = bf16[16,20,1024]{2,1,0:T(8,128)(2,1)} copy(bf16[16,20,1024]{2,0,1:T(8,128)(2,1)S(1)} %copy-done.1) | data formatting | bytes 1310720 | tf_op args[5]
  33.1 0.0 copy-done.2
  33.1 0.6 negate_multiply_fusion.rest_4_
  33.7 0.0 copy-start.3
  33.7 11.6 %all-to-all-done.1 = bf16[16,20,576]{2,1,0:T(8,128)(2,1)S(1)} async-done(((bf16[16,20,576]{2,1,0:T(8,128)(2,1)}), bf16[16,20,576]{2,1,0:T(8,128)(2,1)S(1)}, u32[]{:S(2)}, u32[]{:S(2)}) %all-to-all-start.1) | async-done | bytes 368672 | tf_op jit(solution)/shard_map/all_to_all | solution.py:234
  45.3 0.2 reshape.47
  45.5 0.1 fusion.3
  45.6 0.1 copy.43
  45.7 0.1 copy.44
  45.8 0.2 reshape.48
  46.0 0.8 copy_bitcast_fusion
  46.8 0.0 copy-done
  46.8 0.0 copy-done.3
  46.8 2.1 %compare_select_fusion.rate_ref = f32[320,1024]{1,0:T(8,128)} fusion(bf16[512,1024]{1,0:T(8,128)(2,1)S(1)} %copy-done, f32[1024]{0:T(1024)S(1)} %copy-done.3, bf16[320,576]{1,0:T(8,128)(2,1)S(1)} %reshape.47), kind=kOutput, calls=%fused_computation | convolution fusion | flops 337838080 | bytes 2691072 | tf_op jit(solution)/shard_map/dot_general | solution.py:243
  48.9 11.5 %shard_map.150 = bf16[16,288,128]{2,1,0:T(8,128)(2,1)} custom-call(s32[16]{0:T(128)} %lens_ref.1, s32[16]{0:T(128)} %fmap_ref.3, f32[320,1024]{1,0:T(8,128)} %compare_select_fusion.rate_ref, bf16[16,20,1024]{2,1,0:T(8,128)(2,1)} %get-tuple-element.5.drive_ref, bf16[16,20,1024]{2,1,0:T(8,128)(2,1)} %copy.39.gate_ref, f32[16,16,20]{2,1,0:T(8,128)} %get-tuple-element.13.b_ref, ...), custom_call_target="tpu_custom_call" | custom-call | tf_op jit(solution)/shard_map/pallas_call | solution.py:189
  60.3 33.8 %all_to_all.16 = bf16[16,288,128]{2,1,0:T(8,128)(2,1)S(1)} all-to-all(bf16[16,288,128]{2,1,0:T(8,128)(2,1)} %shard_map.150), channel_id=1, replica_groups=mesh['group'=2,'chan'=16] {'chan'}, dimensions={0} | all-to-all | bytes 2359296 | tf_op jit(solution)/shard_map/all_to_all | solution.py:252
  94.2 0.3 copy.40
  94.4 0.4 copy.41
  94.9 1.3 %reshape.51 = bf16[1,20,16384]{2,1,0:T(8,128)(2,1)} reshape(bf16[20,16,8,128]{3,2,1,0:T(8,128)(2,1)S(1)} %copy.41) | data formatting | bytes 1310720 | tf_op jit(solution)/shard_map/reshape | solution.py:257
  96.2 0.1 convert_bitcast_fusion
  96.3 0.3 copy.42
  96.6 1.2 %reshape.52 = f32[1,16,16384]{2,1,0:T(8,128)} reshape(f32[16,16,8,128]{3,2,1,0:T(8,128)S(1)} %copy.42) | data formatting | bytes 2097152 | tf_op jit(solution)/shard_map/convert_element_type | solution.py:259
  (9 shorter events, 0.2 us)
Async XLA Ops:
  0.6 46.2 %copy-start = (bf16[512,1024]{1,0:T(8,128)(2,1)S(1)}, bf16[512,1024]{1,0:T(8,128)(2,1)}, u32[]{:S(2)}) copy-start(bf16[512,1024]{1,0:T(8,128)(2,1)} %param.24) | copy-start | bytes 3145732
  26.6 5.2 %copy-start.1 = (bf16[16,20,1024]{2,0,1:T(8,128)(2,1)S(1)}, bf16[16,20,1024]{2,0,1:T(8,128)(2,1)}, u32[]{:S(2)}) copy-start(bf16[16,20,1024]{2,0,1:T(8,128)(2,1)} %param.19) | copy-start | bytes 1966084
  27.7 5.4 %copy-start.2 = (f32[16,1024]{1,0:T(8,128)S(1)}, f32[16,1024]{1,0:T(8,128)}, u32[]{:S(2)}) copy-start(f32[16,1024]{1,0:T(8,128)} %param.26) | copy-start | bytes 196612
  27.7 17.6 %all-to-all-start.1 = ((bf16[16,20,576]{2,1,0:T(8,128)(2,1)}), bf16[16,20,576]{2,1,0:T(8,128)(2,1)S(1)}, u32[]{:S(2)}, u32[]{:S(2)}) async-start(bf16[16,20,576]{2,1,0:T(8,128)(2,1)} %broadcast_in_dim.2), calls=%async_computation.1 | async-start | bytes 983040 | tf_op jit(solution)/shard_map/all_to_all | solution.py:234
  33.7 13.1 %copy-start.3 = (f32[1024]{0:T(1024)S(1)}, f32[1024]{0:T(1024)}, u32[]{:S(2)}) copy-start(f32[1024]{0:T(1024)} %param.25) | copy-start | bytes 12292

commit v21 on v20

--- a/solution.py
+++ b/solution.py
@@ -223,22 +223,24 @@
     pieces = lax.all_to_all(partial, "chan", 0, 0, tiled=True).astype(jnp.float32)
     reduced = jnp.sum(pieces, axis=0)
     quarters = rank // 128
-    low_mine = jnp.transpose(
-        reduced[: quarters * positions].reshape(quarters, positions, 128), (1, 0, 2)
-    ).reshape(positions, rank).astype(jnp.bfloat16)
+    low_tiles = reduced[: quarters * positions].astype(jnp.bfloat16)
     select_rows = reduced[quarters * positions :]
     select_sum = select_rows[:, : 2 * state_size] + select_rows[:, 2 * state_size : 4 * state_size]
     select_high = select_sum.astype(jnp.bfloat16)
     select_low = (select_sum - select_high.astype(jnp.float32)).astype(jnp.bfloat16)
-    mine = jnp.concatenate([low_mine, select_high, select_low], axis=1)
+    spare = jnp.zeros((positions, 128 - 4 * state_size), jnp.bfloat16)
+    mine = jnp.concatenate(
+        [low_tiles, jnp.concatenate([select_high, select_low, spare], axis=1)], axis=0
+    )
     gathered = lax.all_to_all(
         jnp.broadcast_to(mine[None], (devices,) + mine.shape), "chan", 0, 0, tiled=True
-    ).reshape(-1, mine.shape[1])
-    rate_low = gathered[:, :rank]
-    selection = (
-        gathered[:, rank : rank + 2 * state_size].astype(jnp.float32)
-        + gathered[:, rank + 2 * state_size :].astype(jnp.float32)
-    ).reshape(thought_count, positions, 2 * state_size)
+    )
+    rate_low = jnp.transpose(
+        gathered[:, : quarters * positions].reshape(devices, quarters, positions, 128),
+        (0, 2, 1, 3),
+    ).reshape(devices * positions, rank)
+    select_all = gathered[:, quarters * positions :].astype(jnp.float32)
+    selection = select_all[:, :, : 2 * state_size] + select_all[:, :, 2 * state_size : 4 * state_size]
     step_rate = jax.nn.softplus(
         jnp.dot(rate_low, rate_up, preferred_element_type=jnp.float32) + rate_bias[None, :]
     )

time: 98.4 us -> 97 us (0.986)
  waiting for transfers between devices: 11.6 us -> 10.5 us
    all_to_all x1, waiting for transfers between devices: 11.6 us -> 10.5 us  [body(): lax.all_to_all(jnp.broadcast_to(mine[None], (devices,) + mine.shape), 'ch...]
where the time goes in v21:
time: 97 us; the launch traced here: 96.4 us
  blocking collectives  53.3 us (55%)
  Pallas kernels  17.6 us (18%)
  waiting for transfers between devices  10.5 us (11%)
  local copies, waits for them, and re-layouts  7.03 us (7%)
  starting transfers between devices  4 us (4%)
  matrix products  2.1 us (2%)
  other arithmetic  1.1 us (1%)
    all_to_all x1, blocking collectives, body(): received = lax.all_to_all(packed_local, 'chan', 0, 0, tiled=True)  33.4 us
    all_to_all x1, blocking collectives, body(): lax.all_to_all(partial, 'chan', 0, 0, tiled=True).astype(jnp.float32)  19.9 us
    pallas_call x1, Pallas kernels, run_scan(): pl.pallas_call(scan_kernel, grid_spec=grid_spec, out_shape=jax.ShapeDtype...  11.5 us
    all_to_all x1, waiting for transfers between devices, body(): lax.all_to_all(jnp.broadcast_to(mine[None], (devices,) + mine.shape), 'ch...  10.5 us
    pallas_call x1, Pallas kernels, project(): pl.pallas_call(project_kernel, grid_spec=grid_spec, out_shape=(jax.ShapeD...  6.18 us
    all_to_all x1, starting transfers between devices, body(): lax.all_to_all(jnp.broadcast_to(mine[None], (devices,) + mine.shape), 'ch...  4 us
    dot_general x1, matrix products, body(): jnp.dot(rate_low, rate_up, preferred_element_type=jnp.float32)  2.1 us
  transfers between devices with their start and end apart: 1, of which 1 were waited for; matrix products, arithmetic and copies ran while one was open for 2% of the time, Pallas kernels for 0%

profile of v21, /device:TPU:1, one launch (start us, length us, event | category | flops | bytes accessed | tf_op | source)
XLA Modules:
  0.0 96.4 jit_solution(3962122232114609592)
XLA Ops:
  0.6 0.0 copy-start
  0.6 6.2 %shard_map.149 = (bf16[16,20,1024]{2,1,0:T(8,128)(2,1)}, bf16[16,100,128]{2,1,0:T(8,128)(2,1)}) custom-call(s32[16]{0:T(128)} %fmap_ref.3, bf16[3,16,1024]{2,1,0:T(8,128)(2,1)} %bitcast.34, bf16[20,16,1024]{2,1,0:T(8,128)(2,1)} %bitcast.32, bf16[4,1024]{1,0:T(4,128)(2,1)} %weight_ref.1, f32[1,1024]{1,0:T(1,128)} %bitcast.36, bf16[1024,512]{1,0:T(8,128)(2,1)} %down_ref.1, ...), custom_call_target="tpu_custom_call" | custom-call | tf_op jit(solution)/shard_map/pallas_call | solution.py:98
  6.8 0.0 copy-start.1
  6.8 19.9 %all_to_all.15 = bf16[16,100,128]{2,1,0:T(8,128)(2,1)S(1)} all-to-all(bf16[16,100,128]{2,1,0:T(8,128)(2,1)} %get-tuple-element.4), channel_id=1, replica_groups=mesh['group'=2,'chan'=16] {'chan'}, dimensions={0} | all-to-all | bytes 819200 | tf_op jit(solution)/shard_map/all_to_all | solution.py:223
  26.7 0.1 convert_reduce_fusion
  26.8 0.1 subtract_convert_fusion
  26.9 0.1 maximum_maximum_fusion
  27.0 0.0 copy-start.2
  27.0 0.8 broadcast_in_dim.5
  27.8 4.0 %all-to-all-start.1 = ((bf16[16,100,128]{2,1,0:T(8,128)(2,1)}), bf16[16,100,128]{2,1,0:T(8,128)(2,1)S(1)}, u32[]{:S(2)}, u32[]{:S(2)}) async-start(bf16[16,100,128]{2,1,0:T(8,128)(2,1)} %broadcast_in_dim.5), calls=%async_computation.1 | async-start | bytes 851968 | tf_op jit(solution)/shard_map/all_to_all | solution.py:235
  31.8 0.0 copy-done.1
  31.8 1.3 %copy.33.gate_ref = bf16[16,20,1024]{2,1,0:T(8,128)(2,1)} copy(bf16[16,20,1024]{2,0,1:T(8,128)(2,1)S(1)} %copy-done.1) | data formatting | bytes 1310720 | tf_op args[5]
  33.0 0.0 copy-done.2
  33.0 0.6 negate_multiply_fusion.rest_4_
  33.7 10.5 %all-to-all-done.1 = bf16[16,100,128]{2,1,0:T(8,128)(2,1)S(1)} async-done(((bf16[16,100,128]{2,1,0:T(8,128)(2,1)}), bf16[16,100,128]{2,1,0:T(8,128)(2,1)S(1)}, u32[]{:S(2)}, u32[]{:S(2)}) %all-to-all-start.1) | async-done | bytes 409632 | tf_op jit(solution)/shard_map/all_to_all | solution.py:235
  44.2 0.1 copy.37
  44.3 0.3 copy.31
  44.6 0.3 copy.38
  44.9 0.0 copy-start.3
  44.9 0.1 convert_element_type.40
  45.1 0.7 slice_bitcast_fusion
  45.8 0.0 copy-done
  45.8 0.0 copy-done.3
  45.8 2.1 %compare_select_fusion.rate_ref = f32[320,1024]{1,0:T(8,128)} fusion(bf16[512,1024]{1,0:T(8,128)(2,1)S(1)} %copy-done, f32[1024]{0:T(1024)S(1)} %copy-done.3, bf16[40,8,4,128]{3,2,1,0:T(4,128)(2,1)S(1)} %bitcast.33), kind=kOutput, calls=%fused_computation | convolution fusion | flops 337838080 | bytes 2691072 | tf_op jit(solution)/shard_map/dot_general | solution.py:245
  47.9 11.5 %shard_map.150 = bf16[16,288,128]{2,1,0:T(8,128)(2,1)} custom-call(s32[16]{0:T(128)} %lens_ref.1, s32[16]{0:T(128)} %fmap_ref.3, f32[320,1024]{1,0:T(8,128)} %compare_select_fusion.rate_ref, bf16[16,20,1024]{2,1,0:T(8,128)(2,1)} %get-tuple-element.5.drive_ref, bf16[16,20,1024]{2,1,0:T(8,128)(2,1)} %copy.33.gate_ref, f32[16,16,20]{2,1,0:T(8,128)} %get-tuple-element.9.b_ref, ...), custom_call_target="tpu_custom_call" | custom-call | tf_op jit(solution)/shard_map/pallas_call | solution.py:189
  59.4 33.4 %all_to_all.16 = bf16[16,288,128]{2,1,0:T(8,128)(2,1)S(1)} all-to-all(bf16[16,288,128]{2,1,0:T(8,128)(2,1)} %shard_map.150), channel_id=1, replica_groups=mesh['group'=2,'chan'=16] {'chan'}, dimensions={0} | all-to-all | bytes 2359296 | tf_op jit(solution)/shard_map/all_to_all | solution.py:254
  92.8 0.3 copy.34
  93.1 0.4 copy.35
  93.5 1.3 %reshape.47 = bf16[1,20,16384]{2,1,0:T(8,128)(2,1)} reshape(bf16[20,16,8,128]{3,2,1,0:T(8,128)(2,1)S(1)} %copy.35) | data formatting | bytes 1310720 | tf_op jit(solution)/shard_map/reshape | solution.py:259
  94.8 0.1 convert_bitcast_fusion
  94.9 0.3 copy.36
  95.3 1.2 %reshape.48 = f32[1,16,16384]{2,1,0:T(8,128)} reshape(f32[16,16,8,128]{3,2,1,0:T(8,128)S(1)} %copy.36) | data formatting | bytes 2097152 | tf_op jit(solution)/shard_map/convert_element_type | solution.py:261
  (7 shorter events, 0.2 us)
Async XLA Ops:
  0.6 45.2 %copy-start = (bf16[512,1024]{1,0:T(8,128)(2,1)S(1)}, bf16[512,1024]{1,0:T(8,128)(2,1)}, u32[]{:S(2)}) copy-start(bf16[512,1024]{1,0:T(8,128)(2,1)} %param.24) | copy-start | bytes 3145732
  6.8 25.0 %copy-start.1 = (bf16[16,20,1024]{2,0,1:T(8,128)(2,1)S(1)}, bf16[16,20,1024]{2,0,1:T(8,128)(2,1)}, u32[]{:S(2)}) copy-start(bf16[16,20,1024]{2,0,1:T(8,128)(2,1)} %param.19) | copy-start | bytes 1966084
  27.0 6.1 %copy-start.2 = (f32[16,1024]{1,0:T(8,128)S(1)}, f32[16,1024]{1,0:T(8,128)}, u32[]{:S(2)}) copy-start(f32[16,1024]{1,0:T(8,128)} %param.26) | copy-start | bytes 196612
  27.8 16.4 %all-to-all-start.1 = ((bf16[16,100,128]{2,1,0:T(8,128)(2,1)}), bf16[16,100,128]{2,1,0:T(8,128)(2,1)S(1)}, u32[]{:S(2)}, u32[]{:S(2)}) async-start(bf16[16,100,128]{2,1,0:T(8,128)(2,1)} %broadcast_in_dim.5), calls=%async_computation.1 | async-start | bytes 851968 | tf_op jit(solution)/shard_map/all_to_all | solution.py:235
  44.9 0.9 copy-start.3

commit v22 on v21

--- a/solution.py
+++ b/solution.py
@@ -232,9 +232,7 @@
     mine = jnp.concatenate(
         [low_tiles, jnp.concatenate([select_high, select_low, spare], axis=1)], axis=0
     )
-    gathered = lax.all_to_all(
-        jnp.broadcast_to(mine[None], (devices,) + mine.shape), "chan", 0, 0, tiled=True
-    )
+    gathered = lax.all_gather(mine, "chan", axis=0)
     rate_low = jnp.transpose(
         gathered[:, : quarters * positions].reshape(devices, quarters, positions, 128),
         (0, 2, 1, 3),

time: 97 us -> 100 us (1.031)
  starting transfers between devices: 4 us -> 7.49 us
    all_gather x0 -> x1, blocking collectives: none -> 20.8 us  [body(): gathered = lax.all_gather(mine, 'chan', axis=0)]
    all_to_all x1 -> x0, blocking collectives: 19.9 us -> none  [body(): lax.all_to_all(partial, 'chan', 0, 0, tiled=True).astype(jnp.float32)]
    all_to_all x1, starting transfers between devices: 4 us -> 7.49 us  [body(): lax.all_to_all(partial, 'chan', 0, 0, tiled=True).astype(jnp.float32)]
where the time goes in v22:
time: 100 us; the launch traced here: 99.7 us
  blocking collectives  53.9 us (54%)
  Pallas kernels  17.6 us (18%)
  waiting for transfers between devices  10.5 us (10%)
  starting transfers between devices  7.49 us (7%)
  local copies, waits for them, and re-layouts  6.21 us (6%)
  matrix products  2.1 us (2%)
  other arithmetic  1.1 us (1%)
    all_to_all x1, blocking collectives, body(): received = lax.all_to_all(packed_local, 'chan', 0, 0, tiled=True)  33.1 us
    all_gather x1, blocking collectives, body(): gathered = lax.all_gather(mine, 'chan', axis=0)  20.8 us
    pallas_call x1, Pallas kernels, run_scan(): pl.pallas_call(scan_kernel, grid_spec=grid_spec, out_shape=jax.ShapeDtype...  11.5 us
    all_to_all x1, waiting for transfers between devices, body(): lax.all_to_all(partial, 'chan', 0, 0, tiled=True).astype(jnp.float32)  10.5 us
    all_to_all x1, starting transfers between devices, body(): lax.all_to_all(partial, 'chan', 0, 0, tiled=True).astype(jnp.float32)  7.49 us
    pallas_call x1, Pallas kernels, project(): pl.pallas_call(project_kernel, grid_spec=grid_spec, out_shape=(jax.ShapeD...  6.17 us
    dot_general x1, matrix products, body(): jnp.dot(rate_low, rate_up, preferred_element_type=jnp.float32)  2.1 us
  transfers between devices with their start and end apart: 1, of which 1 were waited for; matrix products, arithmetic and copies ran while one was open for 2% of the time, Pallas kernels for 0%

profile of v22, /device:TPU:1, one launch (start us, length us, event | category | flops | bytes accessed | tf_op | source)
XLA Modules:
  0.0 99.7 jit_solution(6512077683858811079)
XLA Ops:
  0.6 0.0 copy-start
  0.6 0.0 copy-start.1
  0.7 6.2 %shard_map.149 = (bf16[16,20,1024]{2,1,0:T(8,128)(2,1)}, bf16[16,100,128]{2,1,0:T(8,128)(2,1)}) custom-call(s32[16]{0:T(128)} %fmap_ref.3, bf16[3,16,1024]{2,1,0:T(8,128)(2,1)} %bitcast.36, bf16[20,16,1024]{2,1,0:T(8,128)(2,1)} %bitcast.34, bf16[4,1024]{1,0:T(4,128)(2,1)} %weight_ref.1, f32[1,1024]{1,0:T(1,128)} %bitcast.38, bf16[1024,512]{1,0:T(8,128)(2,1)} %down_ref.1, ...), custom_call_target="tpu_custom_call" | custom-call | tf_op jit(solution)/shard_map/pallas_call | solution.py:98
  6.8 0.0 copy-start.2
  6.8 7.5 %all-to-all-start = ((bf16[16,100,128]{2,1,0:T(8,128)(2,1)}), bf16[16,100,128]{2,1,0:T(8,128)(2,1)S(1)}, u32[]{:S(2)}, u32[]{:S(2)}) async-start(bf16[16,100,128]{2,1,0:T(8,128)(2,1)} %get-tuple-element.4), calls=%async_computation | async-start | bytes 851968 | tf_op jit(solution)/shard_map/all_to_all | solution.py:223
  14.3 0.0 copy-done.1
  14.3 1.3 %copy.33.gate_ref = bf16[16,20,1024]{2,1,0:T(8,128)(2,1)} copy(bf16[16,20,1024]{2,0,1:T(8,128)(2,1)S(1)} %copy-done.1) | data formatting | bytes 1310720 | tf_op args[5]
  15.6 0.0 copy-done.2
  15.6 0.6 negate_multiply_fusion.rest_4_
  16.2 10.5 %all-to-all-done = bf16[16,100,128]{2,1,0:T(8,128)(2,1)S(1)} async-done(((bf16[16,100,128]{2,1,0:T(8,128)(2,1)}), bf16[16,100,128]{2,1,0:T(8,128)(2,1)S(1)}, u32[]{:S(2)}, u32[]{:S(2)}) %all-to-all-start) | async-done | bytes 409632 | tf_op jit(solution)/shard_map/all_to_all | solution.py:223
  26.7 0.1 convert_reduce_fusion
  26.8 0.1 subtract_convert_fusion
  26.9 0.1 maximum_bitcast_fusion
  27.0 20.8 %all-gather.1 = bf16[16,100,128]{2,1,0:T(8,128)(2,1)S(1)} all-gather(bf16[1,100,128]{2,1,0:T(8,128)(2,1)S(1)} %maximum_bitcast_fusion), channel_id=2, replica_groups=mesh['group'=2,'chan'=16] {'chan'}, dimensions={0}, use_global_device_ids=true | all-gather | bytes 435200 | tf_op jit(solution)/shard_map/all_gather | solution.py:235
  47.8 0.1 copy.37
  47.9 0.3 copy.31
  48.2 0.3 copy.38
  48.5 0.0 copy-start.3
  48.5 0.1 convert_element_type.40
  48.7 0.7 slice_bitcast_fusion
  49.4 0.0 copy-done
  49.4 0.0 copy-done.3
  49.4 2.1 %compare_select_fusion.rate_ref = f32[320,1024]{1,0:T(8,128)} fusion(bf16[512,1024]{1,0:T(8,128)(2,1)S(1)} %copy-done, f32[1024]{0:T(1024)S(1)} %copy-done.3, bf16[40,8,4,128]{3,2,1,0:T(4,128)(2,1)S(1)} %bitcast.35), kind=kOutput, calls=%fused_computation | convolution fusion | flops 337838080 | bytes 2691072 | tf_op jit(solution)/shard_map/dot_general | solution.py:243
  51.5 11.5 %shard_map.150 = bf16[16,288,128]{2,1,0:T(8,128)(2,1)} custom-call(s32[16]{0:T(128)} %lens_ref.1, s32[16]{0:T(128)} %fmap_ref.3, f32[320,1024]{1,0:T(8,128)} %compare_select_fusion.rate_ref, bf16[16,20,1024]{2,1,0:T(8,128)(2,1)} %get-tuple-element.5.drive_ref, bf16[16,20,1024]{2,1,0:T(8,128)(2,1)} %copy.33.gate_ref, f32[16,16,20]{2,1,0:T(8,128)} %get-tuple-element.9.b_ref, ...), custom_call_target="tpu_custom_call" | custom-call | tf_op jit(solution)/shard_map/pallas_call | solution.py:189
  62.9 33.1 %all_to_all.10 = bf16[16,288,128]{2,1,0:T(8,128)(2,1)S(1)} all-to-all(bf16[16,288,128]{2,1,0:T(8,128)(2,1)} %shard_map.150), channel_id=1, replica_groups=mesh['group'=2,'chan'=16] {'chan'}, dimensions={0} | all-to-all | bytes 2359296 | tf_op jit(solution)/shard_map/all_to_all | solution.py:252
  96.1 0.3 copy.34
  96.3 0.4 copy.35
  96.7 1.3 %reshape.46 = bf16[1,20,16384]{2,1,0:T(8,128)(2,1)} reshape(bf16[20,16,8,128]{3,2,1,0:T(8,128)(2,1)S(1)} %copy.35) | data formatting | bytes 1310720 | tf_op jit(solution)/shard_map/reshape | solution.py:257
  98.1 0.1 convert_bitcast_fusion
  98.2 0.3 copy.36
  98.5 1.2 %reshape.47 = f32[1,16,16384]{2,1,0:T(8,128)} reshape(f32[16,16,8,128]{3,2,1,0:T(8,128)S(1)} %copy.36) | data formatting | bytes 2097152 | tf_op jit(solution)/shard_map/convert_element_type | solution.py:259
  (7 shorter events, 0.2 us)
Async XLA Ops:
  0.6 48.7 %copy-start = (bf16[512,1024]{1,0:T(8,128)(2,1)S(1)}, bf16[512,1024]{1,0:T(8,128)(2,1)}, u32[]{:S(2)}) copy-start(bf16[512,1024]{1,0:T(8,128)(2,1)} %param.24) | copy-start | bytes 3145732
  0.6 13.7 %copy-start.1 = (bf16[16,20,1024]{2,0,1:T(8,128)(2,1)S(1)}, bf16[16,20,1024]{2,0,1:T(8,128)(2,1)}, u32[]{:S(2)}) copy-start(bf16[16,20,1024]{2,0,1:T(8,128)(2,1)} %param.19) | copy-start | bytes 1966084
  6.8 8.7 %copy-start.2 = (f32[16,1024]{1,0:T(8,128)S(1)}, f32[16,1024]{1,0:T(8,128)}, u32[]{:S(2)}) copy-start(f32[16,1024]{1,0:T(8,128)} %param.26) | copy-start | bytes 196612
  6.8 19.9 %all-to-all-start = ((bf16[16,100,128]{2,1,0:T(8,128)(2,1)}), bf16[16,100,128]{2,1,0:T(8,128)(2,1)S(1)}, u32[]{:S(2)}, u32[]{:S(2)}) async-start(bf16[16,100,128]{2,1,0:T(8,128)(2,1)} %get-tuple-element.4), calls=%async_computation | async-start | bytes 851968 | tf_op jit(solution)/shard_map/all_to_all | solution.py:223
  48.5 0.9 copy-start.3
